TPU v7x, 512 devices: a whole 4x4x16 slice. The times are simulated.
512 devices in a mesh: section: 32 (over z, core), blk: 16 (over y, x).
Axes of the slice: x: 4, y: 4, z: 16, core: 2. Of those that a mesh axis runs over, the one named last changes fastest.
Arguments:
- held_input: bfloat16 [32, 5120, 128], P('section', 'blk'), may hold values from -6 to 6
- fresh_input: bfloat16 [5120, 128], P('blk'), may hold values from -6 to 6
- stashed: bfloat16 [32, 2, 5120, 128], P('section', None, 'blk'), may hold values from -6 to 6
- held_grad: bfloat16 [32, 5120, 128], P('section', 'blk'), may hold values from -6 to 6
- fresh_grad: bfloat16 [5120, 128], P('blk'), may hold values from -6 to 6
- first_up: bfloat16 [32, 2, 128, 6400], P('section', None, 'blk'), may hold values from -1 to 1
- second_up: bfloat16 [32, 2, 160, 16384], P('section', None, 'blk'), may hold values from -0.5 to 0.5
- first_down: bfloat16 [32, 160, 16384], P('section', 'blk'), may hold values from -0.5 to 0.5
- second_down: bfloat16 [32, 128, 6400], P('section', 'blk'), may hold values from -0.5 to 0.5
Outputs:
- passed_output: bfloat16 [32, 5120, 128], P('section', 'blk')
- passed_grad: bfloat16 [32, 5120, 128], P('section', 'blk')
- grad_first_up: bfloat16 [32, 2, 128, 6400], P('section', None, 'blk')
- grad_second_up: bfloat16 [32, 2, 160, 16384], P('section', None, 'blk')
- grad_first_down: bfloat16 [32, 160, 16384], P('section', 'blk')
- grad_second_down: bfloat16 [32, 128, 6400], P('section', 'blk')
All inputs are finite; a program needn't handle non-finite values.
Results may differ from a plain program's by a relative error of at most 0.0095.
Values may be sent and summed in bfloat16 or wider, within the bound.
No kernel may reach another device: no remote copies, remote signals or barrier semaphores. Data moves between devices by JAX's collectives and lax.ppermute only.
A program may use at most 64 MiB of HBM per device.

v0:
```python
import math

import jax
import jax.numpy as jnp
from jax import lax
from jax.sharding import PartitionSpec as P

BLOCK = 128
FIRST_BLOCKS = 128
FIRST_IN = 40
SECOND_BLOCKS = 160
TICKS = 2


def from_behind(value, axis, by):
    length = lax.axis_size(axis)
    pairs = [(i, i + by) for i in range(length) if 0 <= i + by < length]
    return lax.ppermute(value, axis, pairs)


def to_blocks(pieces):
    return lax.all_to_all(pieces, "blk", split_axis=2, concat_axis=1, tiled=True)


def to_features(pieces):
    return lax.all_to_all(pieces, "blk", split_axis=2, concat_axis=1, tiled=True)


def first_half(values, up_first):
    return jnp.einsum(
        "pqt,gpqr->gprt", values, up_first, preferred_element_type=jnp.float32
    ).astype(jnp.bfloat16)


def middle(spread, up_second, down_first):
    mixed = jnp.einsum("gprt,grpo->grot", spread, up_second, preferred_element_type=jnp.float32)
    hidden = (jax.nn.silu(mixed[0]) * mixed[1]).astype(jnp.bfloat16)
    lowered = jnp.einsum(
        "rot,rop->rpt", hidden, down_first, preferred_element_type=jnp.float32
    ).astype(jnp.bfloat16)
    return (mixed, hidden, lowered)


def last_half(values, lowered, down_second):
    added = jnp.einsum("rpt,prq->pqt", lowered, down_second, preferred_element_type=jnp.float32)
    return (values.astype(jnp.float32) + added).astype(jnp.bfloat16)


def backward_middle(mixed, grad_lowered, up_second, down_first):
    grad_hidden = jnp.einsum(
        "prt,rop->rot", grad_lowered, down_first, preferred_element_type=jnp.float32
    )
    sigmoid_gate = jax.nn.sigmoid(mixed[0])
    slope = sigmoid_gate * (1.0 + mixed[0] * (1.0 - sigmoid_gate))
    grad_mixed = jnp.stack(
        [grad_hidden * mixed[1] * slope, grad_hidden * mixed[0] * sigmoid_gate]
    ).astype(jnp.bfloat16)
    grad_spread = jnp.einsum(
        "grot,grpo->grpt", grad_mixed, up_second, preferred_element_type=jnp.float32
    ).astype(jnp.bfloat16)
    return (grad_mixed, grad_spread)


def shards(
    held_input,
    fresh_input,
    stashed,
    held_grad,
    fresh_grad,
    first_up,
    second_up,
    first_down,
    second_down,
):
    feature_blocks = first_up.shape[2]
    hidden_blocks = second_up.shape[2]
    tokens = held_input.shape[2]
    up_first = first_up[0].reshape(2, feature_blocks, FIRST_IN, SECOND_BLOCKS)
    up_second = second_up[0].reshape(2, hidden_blocks, FIRST_BLOCKS, BLOCK)
    down_first = first_down[0].reshape(hidden_blocks, BLOCK, FIRST_BLOCKS)
    down_second = second_down[0].reshape(feature_blocks, SECOND_BLOCKS, FIRST_IN)
    inputs = held_input[0].reshape(feature_blocks, FIRST_IN, tokens)
    grads = held_grad[0].reshape(feature_blocks, FIRST_IN, tokens)
    section_pos = lax.axis_index("section")
    last_section = lax.axis_size("section") - 1
    total_first_up = jnp.zeros(up_first.shape, jnp.float32)
    total_second_up = jnp.zeros(up_second.shape, jnp.float32)
    total_first_down = jnp.zeros(down_first.shape, jnp.float32)
    total_second_down = jnp.zeros(down_second.shape, jnp.float32)
    outputs = inputs
    backward = grads
    for tick_index in range(TICKS):
        stash_view = stashed[0, tick_index].reshape(feature_blocks, FIRST_IN, tokens)
        grad_lowered = jnp.einsum(
            "pqt,prq->prt", grads, down_second, preferred_element_type=jnp.float32
        ).astype(jnp.bfloat16)
        spread = to_blocks(first_half(inputs, up_first))
        mixed, hidden, lowered = middle(spread, up_second, down_first)
        outputs = last_half(inputs, to_features(lowered[None])[0], down_second)
        spread_stash = to_blocks(first_half(stash_view, up_first))
        mixed_stash, hidden_stash, lowered_stash = middle(spread_stash, up_second, down_first)
        lowered_back = to_features(lowered_stash[None])[0]
        grad_arrived = to_blocks(grad_lowered[None])[0]
        grad_mixed, grad_spread = backward_middle(mixed_stash, grad_arrived, up_second, down_first)
        grad_spread_back = to_features(grad_spread)
        added_back = jnp.einsum(
            "grpt,gpqr->pqt", grad_spread_back, up_first, preferred_element_type=jnp.float32
        )
        backward = (grads.astype(jnp.float32) + added_back).astype(jnp.bfloat16)
        total_first_up = total_first_up + jnp.einsum(
            "pqt,grpt->gpqr", stash_view, grad_spread_back, preferred_element_type=jnp.float32
        )
        total_second_up = total_second_up + jnp.einsum(
            "gprt,grot->grpo", spread_stash, grad_mixed, preferred_element_type=jnp.float32
        )
        total_first_down = total_first_down + jnp.einsum(
            "rot,prt->rop", hidden_stash, grad_arrived, preferred_element_type=jnp.float32
        )
        total_second_down = total_second_down + jnp.einsum(
            "rpt,pqt->prq", lowered_back, grads, preferred_element_type=jnp.float32
        )
        if tick_index + 1 < TICKS:
            moved_forward = from_behind(outputs, "section", 1)
            inputs = jnp.where(
                section_pos == 0,
                fresh_input.reshape(feature_blocks, FIRST_IN, tokens),
                moved_forward,
            )
            moved_backward = from_behind(backward, "section", -1)
            grads = jnp.where(
                section_pos == last_section,
                fresh_grad.reshape(feature_blocks, FIRST_IN, tokens),
                moved_backward,
            )
    factor = 1.0 / math.sqrt(TICKS * tokens)
    return (
        outputs.reshape(held_input.shape),
        backward.reshape(held_grad.shape),
        (total_first_up * factor).astype(jnp.bfloat16).reshape(first_up.shape),
        (total_second_up * factor).astype(jnp.bfloat16).reshape(second_up.shape),
        (total_first_down * factor).astype(jnp.bfloat16).reshape(first_down.shape),
        (total_second_down * factor).astype(jnp.bfloat16).reshape(second_down.shape),
    )


def solution(mesh):
    return jax.shard_map(
        shards,
        mesh=mesh,
        in_specs=(
            P("section", "blk", None),
            P("blk", None),
            P("section", None, "blk", None),
            P("section", "blk", None),
            P("blk", None),
            P("section", None, "blk", None),
            P("section", None, "blk", None),
            P("section", "blk", None),
            P("section", "blk", None),
        ),
        out_specs=(
            P("section", "blk", None),
            P("section", "blk", None),
            P("section", None, "blk", None),
            P("section", None, "blk", None),
            P("section", "blk", None),
            P("section", "blk", None),
        ),
        check_vma=False,
    )
```

profile of v0, /device:TPU:96, one launch (start us, length us, event | category | flops | bytes accessed | tf_op | source)
XLA Modules:
  0.0 197.7 jit_solution(12979514578403921260)
XLA Ops:
  4.7 7.0 %all-to-all-start = ((bf16[2,8,160,128]{3,0,1,2:T(2,128)(2,1)}), bf16[2,8,160,128]{3,0,1,2:T(2,128)(2,1)S(1)}, u32[]{:S(2)}, u32[]{:S(2)}) async-start(bf16[2,8,160,128]{3,0,1,2:T(2,128)(2,1)} %copy.186), calls=%async_computation | async-start | bytes 1310720 | tf_op jit(solution)/shard_map/all_to_all | solution.py:22
  13.5 11.1 %all-to-all-done = bf16[2,8,160,128]{3,0,1,2:T(2,128)(2,1)S(1)} async-done(((bf16[2,8,160,128]{3,0,1,2:T(2,128)(2,1)}), bf16[2,8,160,128]{3,0,1,2:T(2,128)(2,1)S(1)}, u32[]{:S(2)}, u32[]{:S(2)}) %all-to-all-start) | async-done | bytes 655392 | tf_op jit(solution)/shard_map/all_to_all | solution.py:22
  24.6 4.3 %all-to-all-start.5 = ((bf16[2,8,160,128]{3,0,1,2:T(2,128)(2,1)}), bf16[2,8,160,128]{3,0,1,2:T(2,128)(2,1)}, u32[]{:S(2)}, u32[]{:S(2)}) async-start(bf16[2,8,160,128]{3,0,1,2:T(2,128)(2,1)} %copy.212), calls=%async_computation.5 | async-start | bytes 1310720 | tf_op jit(solution)/shard_map/all_to_all | solution.py:22
  34.1 6.6 %all-to-all-done.5 = bf16[2,8,160,128]{3,0,1,2:T(2,128)(2,1)} async-done(((bf16[2,8,160,128]{3,0,1,2:T(2,128)(2,1)}), bf16[2,8,160,128]{3,0,1,2:T(2,128)(2,1)}, u32[]{:S(2)}, u32[]{:S(2)}) %all-to-all-start.5) | async-done | bytes 655392 | tf_op jit(solution)/shard_map/all_to_all | solution.py:22
  40.7 3.5 %all-to-all-start.4 = ((bf16[1,8,160,128]{3,1,0,2:T(8,128)(2,1)}), bf16[1,8,160,128]{3,1,0,2:T(8,128)(2,1)S(1)}, u32[]{:S(2)}, u32[]{:S(2)}) async-start(bf16[1,8,160,128]{3,1,0,2:T(8,128)(2,1)} %copy.208), calls=%async_computation.4 | async-start | bytes 655360 | tf_op jit(solution)/shard_map/all_to_all | solution.py:22
  48.4 4.9 %all-to-all-done.4 = bf16[1,8,160,128]{3,1,0,2:T(8,128)(2,1)S(1)} async-done(((bf16[1,8,160,128]{3,1,0,2:T(8,128)(2,1)}), bf16[1,8,160,128]{3,1,0,2:T(8,128)(2,1)S(1)}, u32[]{:S(2)}, u32[]{:S(2)}) %all-to-all-start.4) | async-done | bytes 327712 | tf_op jit(solution)/shard_map/all_to_all | solution.py:22
  54.1 3.6 %all-to-all-start.8 = ((bf16[2,8,160,128]{3,0,1,2:T(2,128)(2,1)}), bf16[2,8,160,128]{3,0,1,2:T(2,128)(2,1)S(1)}, u32[]{:S(2)}, u32[]{:S(2)}) async-start(bf16[2,8,160,128]{3,0,1,2:T(2,128)(2,1)} %copy.228), calls=%async_computation.8 | async-start | bytes 1310720 | tf_op jit(solution)/shard_map/all_to_all | solution.py:22
  62.1 2.7 %fusion.61 = (bf16[1,10,128,128]{2,3,1,0:T(8,128)(2,1)S(1)}, bf16[1,10,128,128]{2,3,1,0:T(8,128)(2,1)S(1)}, bf16[10,128,128]{1,2,0:T(8,128)(2,1)}) fusion(f32[2,10,128,128]{2,3,1,0:T(8,128)} %convolution_bitcast_fusion.1, bf16[16,128,128]{2,1,0:T(8,128)(2,1)S(1)} %bitcast.295, bf16[1,16,8,10,128]{4,2,3,1,0:T(8,128)(2,1)} %bitcast.308), kind=kOutput, calls=%fused_computation.109 | convolution fusion | flops 44564480 | bytes 2949120 | tf_op jit(solution)/shard_map/prt,rop->rot/dot_general | solution.py:50
  68.5 5.8 %all-to-all-start.1 = ((bf16[1,10,128,128]{3,1,0,2:T(8,128)(2,1)}), bf16[1,10,128,128]{3,1,0,2:T(8,128)(2,1)}, u32[]{:S(2)}, u32[]{:S(2)}) async-start(bf16[1,10,128,128]{3,1,0,2:T(8,128)(2,1)} %copy.191), calls=%async_computation.1 | async-start | bytes 1048576 | tf_op jit(solution)/shard_map/all_to_all | solution.py:26
  79.8 4.7 %all-to-all-done.1 = bf16[1,10,128,128]{3,1,0,2:T(8,128)(2,1)} async-done(((bf16[1,10,128,128]{3,1,0,2:T(8,128)(2,1)}), bf16[1,10,128,128]{3,1,0,2:T(8,128)(2,1)}, u32[]{:S(2)}, u32[]{:S(2)}) %all-to-all-start.1) | async-done | bytes 327712 | tf_op jit(solution)/shard_map/all_to_all | solution.py:26
  84.5 4.2 %all-to-all-start.10 = ((bf16[1,10,128,128]{3,1,0,2:T(8,128)(2,1)}), bf16[1,10,128,128]{3,1,0,2:T(8,128)(2,1)}, u32[]{:S(2)}, u32[]{:S(2)}) async-start(bf16[1,10,128,128]{3,1,0,2:T(8,128)(2,1)} %copy.246), calls=%async_computation.10 | async-start | bytes 1048576 | tf_op jit(solution)/shard_map/all_to_all | solution.py:26
  98.9 5.8 %all-to-all-start.6 = ((bf16[2,10,128,128]{3,0,1,2:T(2,128)(2,1)}), bf16[2,10,128,128]{3,0,1,2:T(2,128)(2,1)}, u32[]{:S(2)}, u32[]{:S(2)}) async-start(bf16[2,10,128,128]{3,0,1,2:T(2,128)(2,1)} %copy.218), calls=%async_computation.6 | async-start | bytes 1310720 | tf_op jit(solution)/shard_map/all_to_all | solution.py:26
  115.6 5.9 %all-to-all-start.2 = ((bf16[2,8,160,128]{3,0,1,2:T(2,128)(2,1)}), bf16[2,8,160,128]{3,0,1,2:T(2,128)(2,1)}, u32[]{:S(2)}, u32[]{:S(2)}) async-start(bf16[2,8,160,128]{3,0,1,2:T(2,128)(2,1)} %copy.197), calls=%async_computation.2 | async-start | bytes 1310720 | tf_op jit(solution)/shard_map/all_to_all | solution.py:22
  128.6 6.7 %all-to-all-done.2 = bf16[2,8,160,128]{3,0,1,2:T(2,128)(2,1)} async-done(((bf16[2,8,160,128]{3,0,1,2:T(2,128)(2,1)}), bf16[2,8,160,128]{3,0,1,2:T(2,128)(2,1)}, u32[]{:S(2)}, u32[]{:S(2)}) %all-to-all-start.2) | async-done | bytes 655392 | tf_op jit(solution)/shard_map/all_to_all | solution.py:22
  135.3 4.2 %all-to-all-start.7 = ((bf16[1,8,160,128]{3,1,0,2:T(8,128)(2,1)}), bf16[1,8,160,128]{3,1,0,2:T(8,128)(2,1)}, u32[]{:S(2)}, u32[]{:S(2)}) async-start(bf16[1,8,160,128]{3,1,0,2:T(8,128)(2,1)} %copy.224), calls=%async_computation.7 | async-start | bytes 655360 | tf_op jit(solution)/shard_map/all_to_all | solution.py:22
  145.0 4.8 %all-to-all-done.7 = bf16[1,8,160,128]{3,1,0,2:T(8,128)(2,1)} async-done(((bf16[1,8,160,128]{3,1,0,2:T(8,128)(2,1)}), bf16[1,8,160,128]{3,1,0,2:T(8,128)(2,1)}, u32[]{:S(2)}, u32[]{:S(2)}) %all-to-all-start.7) | async-done | bytes 327712 | tf_op jit(solution)/shard_map/all_to_all | solution.py:22
  149.8 4.2 %all-to-all-start.3 = ((bf16[1,10,128,128]{3,1,0,2:T(8,128)(2,1)}), bf16[1,10,128,128]{3,1,0,2:T(8,128)(2,1)}, u32[]{:S(2)}, u32[]{:S(2)}) async-start(bf16[1,10,128,128]{3,1,0,2:T(8,128)(2,1)} %copy.202), calls=%async_computation.3 | async-start | bytes 1048576 | tf_op jit(solution)/shard_map/all_to_all | solution.py:26
  154.0 3.0 %fusion.62 = (bf16[1,10,128,128]{2,3,1,0:T(8,128)(2,1)}, bf16[1,10,128,128]{2,3,1,0:T(8,128)(2,1)}, bf16[10,128,128]{1,2,0:T(8,128)(2,1)S(1)}) fusion(f32[2,10,128,128]{2,3,1,0:T(8,128)} %convolution_bitcast_fusion, bf16[16,128,128]{2,1,0:T(8,128)(2,1)} %bitcast.297, bf16[1,16,8,10,128]{4,2,3,1,0:T(8,128)(2,1)} %bitcast.62), kind=kOutput, calls=%fused_computation.110 | convolution fusion | flops 44564480 | bytes 2949120 | tf_op jit(solution)/shard_map/prt,rop->rot/dot_general | solution.py:50
  160.8 4.4 %all-to-all-done.3 = bf16[1,10,128,128]{3,1,0,2:T(8,128)(2,1)} async-done(((bf16[1,10,128,128]{3,1,0,2:T(8,128)(2,1)}), bf16[1,10,128,128]{3,1,0,2:T(8,128)(2,1)}, u32[]{:S(2)}, u32[]{:S(2)}) %all-to-all-start.3) | async-done | bytes 327712 | tf_op jit(solution)/shard_map/all_to_all | solution.py:26
  165.3 4.2 %all-to-all-start.11 = ((bf16[1,10,128,128]{3,1,0,2:T(8,128)(2,1)}), bf16[1,10,128,128]{3,1,0,2:T(8,128)(2,1)}, u32[]{:S(2)}, u32[]{:S(2)}) async-start(bf16[1,10,128,128]{3,1,0,2:T(8,128)(2,1)} %copy.250), calls=%async_computation.11 | async-start | bytes 1048576 | tf_op jit(solution)/shard_map/all_to_all | solution.py:26
  172.0 3.0 %copy.234 = bf16[2,10,128,128]{3,0,1,2:T(2,128)(2,1)} copy(bf16[2,10,128,128]{2,3,1,0:T(8,128)(2,1)} %fusion.3) | data formatting | bytes 1310720 | tf_op jit(solution)/shard_map/convert_element_type | solution.py:60
  176.2 3.7 %all-to-all-done.11 = bf16[1,10,128,128]{3,1,0,2:T(8,128)(2,1)} async-done(((bf16[1,10,128,128]{3,1,0,2:T(8,128)(2,1)}), bf16[1,10,128,128]{3,1,0,2:T(8,128)(2,1)}, u32[]{:S(2)}, u32[]{:S(2)}) %all-to-all-start.11) | async-done | bytes 327712 | tf_op jit(solution)/shard_map/all_to_all | solution.py:26
  180.0 3.6 %all-to-all-start.9 = ((bf16[2,10,128,128]{3,0,1,2:T(2,128)(2,1)}), bf16[2,10,128,128]{3,0,1,2:T(2,128)(2,1)S(1)}, u32[]{:S(2)}, u32[]{:S(2)}) async-start(bf16[2,10,128,128]{3,0,1,2:T(2,128)(2,1)} %copy.234), calls=%async_computation.9 | async-start | bytes 1310720 | tf_op jit(solution)/shard_map/all_to_all | solution.py:26
  192.0 2.7 %all-to-all-done.9 = bf16[2,10,128,128]{3,0,1,2:T(2,128)(2,1)S(1)} async-done(((bf16[2,10,128,128]{3,0,1,2:T(2,128)(2,1)}), bf16[2,10,128,128]{3,0,1,2:T(2,128)(2,1)S(1)}, u32[]{:S(2)}, u32[]{:S(2)}) %all-to-all-start.9) | async-done | bytes 655392 | tf_op jit(solution)/shard_map/all_to_all | solution.py:26
  (127 shorter events, 81.6 us)
Async XLA Ops:
  3.3 8.4 %copy-start.23 = (bf16[1,2,320,128]{3,2,1,0:T(8,128)(2,1)S(1)}, bf16[1,2,320,128]{3,2,1,0:T(8,128)(2,1)}, u32[]{:S(2)}) copy-start(bf16[1,2,320,128]{3,2,1,0:T(8,128)(2,1)} %param.11) | copy-start | bytes 491524
  4.7 20.0 %all-to-all-start = ((bf16[2,8,160,128]{3,0,1,2:T(2,128)(2,1)}), bf16[2,8,160,128]{3,0,1,2:T(2,128)(2,1)S(1)}, u32[]{:S(2)}, u32[]{:S(2)}) async-start(bf16[2,8,160,128]{3,0,1,2:T(2,128)(2,1)} %copy.186), calls=%async_computation | async-start | bytes 1310720 | tf_op jit(solution)/shard_map/all_to_all | solution.py:22
  12.2 16.8 %copy-start.24 = (bf16[1,8,6400]{2,1,0:T(8,128)(2,1)S(1)}, bf16[1,8,6400]{2,1,0:T(8,128)(2,1)}, u32[]{:S(2)}) copy-start(bf16[1,8,6400]{2,1,0:T(8,128)(2,1)} %param.17) | copy-start | bytes 307204
  12.2 17.3 %copy-start.10 = (bf16[1,2,10,16384]{3,1,2,0:T(2,128)(2,1)S(1)}, bf16[1,2,10,16384]{3,1,2,0:T(2,128)(2,1)}, u32[]{:S(2)}) copy-start(bf16[1,2,10,16384]{3,1,2,0:T(2,128)(2,1)} %param.15) | copy-start | bytes 1966084
  24.6 16.1 %all-to-all-start.5 = ((bf16[2,8,160,128]{3,0,1,2:T(2,128)(2,1)}), bf16[2,8,160,128]{3,0,1,2:T(2,128)(2,1)}, u32[]{:S(2)}, u32[]{:S(2)}) async-start(bf16[2,8,160,128]{3,0,1,2:T(2,128)(2,1)} %copy.212), calls=%async_computation.5 | async-start | bytes 1310720 | tf_op jit(solution)/shard_map/all_to_all | solution.py:22
  31.1 43.1 %copy-start = (bf16[2,8,128,128]{3,2,1,0:T(8,128)(2,1)}, bf16[2,8,128,128]{3,2,1,0:T(8,128)(2,1)S(1)}, u32[]{:S(2)}) copy-start(bf16[2,8,128,128]{3,2,1,0:T(8,128)(2,1)S(1)} %copy.276) | copy-start | bytes 1572868
  40.7 12.6 %all-to-all-start.4 = ((bf16[1,8,160,128]{3,1,0,2:T(8,128)(2,1)}), bf16[1,8,160,128]{3,1,0,2:T(8,128)(2,1)S(1)}, u32[]{:S(2)}, u32[]{:S(2)}) async-start(bf16[1,8,160,128]{3,1,0,2:T(8,128)(2,1)} %copy.208), calls=%async_computation.4 | async-start | bytes 655360 | tf_op jit(solution)/shard_map/all_to_all | solution.py:22
  54.1 14.4 %all-to-all-start.8 = ((bf16[2,8,160,128]{3,0,1,2:T(2,128)(2,1)}), bf16[2,8,160,128]{3,0,1,2:T(2,128)(2,1)S(1)}, u32[]{:S(2)}, u32[]{:S(2)}) async-start(bf16[2,8,160,128]{3,0,1,2:T(2,128)(2,1)} %copy.228), calls=%async_computation.8 | async-start | bytes 1310720 | tf_op jit(solution)/shard_map/all_to_all | solution.py:22
  68.5 7.8 %copy-start.5 = (bf16[2,8,160,128]{3,0,1,2:T(2,128)(2,1)}, bf16[2,8,160,128]{3,0,1,2:T(2,128)(2,1)S(1)}, u32[]{:S(2)}) copy-start(bf16[2,8,160,128]{3,0,1,2:T(2,128)(2,1)S(1)} %all-to-all-done.8) | copy-start | bytes 1966084
  68.5 16.0 %all-to-all-start.1 = ((bf16[1,10,128,128]{3,1,0,2:T(8,128)(2,1)}), bf16[1,10,128,128]{3,1,0,2:T(8,128)(2,1)}, u32[]{:S(2)}, u32[]{:S(2)}) async-start(bf16[1,10,128,128]{3,1,0,2:T(8,128)(2,1)} %copy.191), calls=%async_computation.1 | async-start | bytes 1048576 | tf_op jit(solution)/shard_map/all_to_all | solution.py:26
  79.8 11.3 %copy-start.11 = (bf16[2,10,128,128]{2,3,1,0:T(8,128)(2,1)S(1)}, bf16[2,10,128,128]{2,3,1,0:T(8,128)(2,1)}, u32[]{:S(2)}) copy-start(bf16[2,10,128,128]{2,3,1,0:T(8,128)(2,1)} %fusion.2) | copy-start | bytes 1966084
  84.5 14.4 %all-to-all-start.10 = ((bf16[1,10,128,128]{3,1,0,2:T(8,128)(2,1)}), bf16[1,10,128,128]{3,1,0,2:T(8,128)(2,1)}, u32[]{:S(2)}, u32[]{:S(2)}) async-start(bf16[1,10,128,128]{3,1,0,2:T(8,128)(2,1)} %copy.246), calls=%async_computation.10 | async-start | bytes 1048576 | tf_op jit(solution)/shard_map/all_to_all | solution.py:26
  95.6 9.1 %copy-start.12 = (bf16[1,320,128]{2,1,0:T(8,128)(2,1)S(1)}, bf16[1,320,128]{2,1,0:T(8,128)(2,1)}, u32[]{:S(2)}) copy-start(bf16[1,320,128]{2,1,0:T(8,128)(2,1)} %param.9) | copy-start | bytes 245764
  98.9 16.7 %all-to-all-start.6 = ((bf16[2,10,128,128]{3,0,1,2:T(2,128)(2,1)}), bf16[2,10,128,128]{3,0,1,2:T(2,128)(2,1)}, u32[]{:S(2)}, u32[]{:S(2)}) async-start(bf16[2,10,128,128]{3,0,1,2:T(2,128)(2,1)} %copy.218), calls=%async_computation.6 | async-start | bytes 1310720 | tf_op jit(solution)/shard_map/all_to_all | solution.py:26
  106.0 6.5 %copy-start.13 = (bf16[320,128]{1,0:T(8,128)(2,1)S(1)}, bf16[320,128]{1,0:T(8,128)(2,1)}, u32[]{:S(2)}) copy-start(bf16[320,128]{1,0:T(8,128)(2,1)} %param.10) | copy-start | bytes 245764
  106.0 5.9 %collective-permute-start = (bf16[8,40,128]{2,1,0:T(8,128)(2,1)S(1)}, bf16[8,40,128]{2,1,0:T(8,128)(2,1)S(1)}, u32[]{:S(2)}, u32[]{:S(2)}) collective-permute-start(bf16[8,40,128]{2,1,0:T(8,128)(2,1)S(1)} %fusion.24), channel_id=1, source_target_pairs={{0,16},{16,32},{32,48},{48,64},{64,80},{80,96},{96,112},{112,128},... | collective-permute-start | bytes 245768 | tf_op jit(solution)/shard_map/ppermute | solution.py:18
  115.6 19.8 %all-to-all-start.2 = ((bf16[2,8,160,128]{3,0,1,2:T(2,128)(2,1)}), bf16[2,8,160,128]{3,0,1,2:T(2,128)(2,1)}, u32[]{:S(2)}, u32[]{:S(2)}) async-start(bf16[2,8,160,128]{3,0,1,2:T(2,128)(2,1)} %copy.197), calls=%async_computation.2 | async-start | bytes 1310720 | tf_op jit(solution)/shard_map/all_to_all | solution.py:22
  123.2 4.3 %collective-permute-start.1 = (bf16[8,40,128]{2,1,0:T(8,128)(2,1)S(1)}, bf16[8,40,128]{2,1,0:T(8,128)(2,1)S(1)}, u32[]{:S(2)}, u32[]{:S(2)}) collective-permute-start(bf16[8,40,128]{2,1,0:T(8,128)(2,1)S(1)} %fusion.23), channel_id=1, source_target_pairs={{16,0},{32,16},{48,32},{64,48},{80,64},{96,80},{112,96},{128,112},... | collective-permute-start | bytes 245768 | tf_op jit(solution)/shard_map/ppermute | solution.py:18
  135.3 14.4 %all-to-all-start.7 = ((bf16[1,8,160,128]{3,1,0,2:T(8,128)(2,1)}), bf16[1,8,160,128]{3,1,0,2:T(8,128)(2,1)}, u32[]{:S(2)}, u32[]{:S(2)}) async-start(bf16[1,8,160,128]{3,1,0,2:T(8,128)(2,1)} %copy.224), calls=%async_computation.7 | async-start | bytes 655360 | tf_op jit(solution)/shard_map/all_to_all | solution.py:22
  149.8 15.5 %all-to-all-start.3 = ((bf16[1,10,128,128]{3,1,0,2:T(8,128)(2,1)}), bf16[1,10,128,128]{3,1,0,2:T(8,128)(2,1)}, u32[]{:S(2)}, u32[]{:S(2)}) async-start(bf16[1,10,128,128]{3,1,0,2:T(8,128)(2,1)} %copy.202), calls=%async_computation.3 | async-start | bytes 1048576 | tf_op jit(solution)/shard_map/all_to_all | solution.py:26
  165.3 14.7 %all-to-all-start.11 = ((bf16[1,10,128,128]{3,1,0,2:T(8,128)(2,1)}), bf16[1,10,128,128]{3,1,0,2:T(8,128)(2,1)}, u32[]{:S(2)}, u32[]{:S(2)}) async-start(bf16[1,10,128,128]{3,1,0,2:T(8,128)(2,1)} %copy.250), calls=%async_computation.11 | async-start | bytes 1048576 | tf_op jit(solution)/shard_map/all_to_all | solution.py:26
  176.2 7.3 %copy-start.3 = (f32[10,128,128]{2,1,0:T(8,128)S(1)}, f32[10,128,128]{2,1,0:T(8,128)}, u32[]{:S(2)}) copy-start(f32[10,128,128]{2,1,0:T(8,128)} %fusion.49) | copy-start | bytes 1966084
  176.2 8.8 %copy-start.6 = (bf16[2,10,128,128]{3,2,1,0:T(8,128)(2,1)S(1)}, bf16[2,10,128,128]{3,2,1,0:T(8,128)(2,1)}, u32[]{:S(2)}) copy-start(bf16[2,10,128,128]{3,2,1,0:T(8,128)(2,1)} %fusion.1) | copy-start | bytes 1966084
  180.0 14.8 %all-to-all-start.9 = ((bf16[2,10,128,128]{3,0,1,2:T(2,128)(2,1)}), bf16[2,10,128,128]{3,0,1,2:T(2,128)(2,1)S(1)}, u32[]{:S(2)}, u32[]{:S(2)}) async-start(bf16[2,10,128,128]{3,0,1,2:T(2,128)(2,1)} %copy.234), calls=%async_computation.9 | async-start | bytes 1310720 | tf_op jit(solution)/shard_map/all_to_all | solution.py:26
  (16 other events, 32.7 us)
where the time goes:
time: 200 us; the launch traced here: 198 us
  starting transfers between devices  60.7 us (30%)
  waiting for transfers between devices  56.1 us (28%)
  local copies, waits for them, and re-layouts  43.1 us (22%)
  matrix products  36.6 us (18%)
    all_to_all x6, waiting for transfers between devices, to_blocks(): lax.all_to_all(pieces, 'blk', split_axis=2, concat_axis=1, tiled=True)  35.6 us
    all_to_all x6, starting transfers between devices, to_blocks(): lax.all_to_all(pieces, 'blk', split_axis=2, concat_axis=1, tiled=True)  28.5 us
    all_to_all x6, starting transfers between devices, to_features(): lax.all_to_all(pieces, 'blk', split_axis=2, concat_axis=1, tiled=True)  27.9 us
    all_to_all x6, waiting for transfers between devices, to_features(): lax.all_to_all(pieces, 'blk', split_axis=2, concat_axis=1, tiled=True)  18.2 us
    all_to_all x12, local copies, waits for them, and re-layouts, to_features(): lax.all_to_all(pieces, 'blk', split_axis=2, concat_axis=1, tiled=True)  7.15 us
    dot_general x4, matrix products, middle(): jnp.einsum('rot,rop->rpt', hidden, down_first, preferred_element_type=jnp...  6.25 us
    dot_general x2, matrix products, backward_middle(): jnp.einsum('prt,rop->rot', grad_lowered, down_first, preferred_element_ty...  5.63 us
    unnamed x54, local copies, waits for them, and re-layouts  5.53 us
  transfers between devices with their start and end apart: 14, of which 14 were waited for; matrix products, arithmetic and copies ran while one was open for 35% of the time, Pallas kernels for 0%

commit v1 on v0

v1 whole, which is shorter than its diff:
```python
import math

import jax
import jax.numpy as jnp
from jax import lax
from jax.sharding import PartitionSpec as P

BLOCK = 128
FIRST_BLOCKS = 128
FIRST_IN = 40
SECOND_BLOCKS = 160
TICKS = 2


def from_behind(value, axis, by):
    length = lax.axis_size(axis)
    pairs = [(i, i + by) for i in range(length) if 0 <= i + by < length]
    return lax.ppermute(value, axis, pairs)


def to_blocks(pieces):
    return lax.all_to_all(pieces, "blk", split_axis=1, concat_axis=0, tiled=True)


def to_features(pieces):
    return lax.all_to_all(pieces, "blk", split_axis=1, concat_axis=0, tiled=True)


def spread_of(values, up_first):
    return jnp.einsum(
        "pqt,gpqr->prgt", values, up_first, preferred_element_type=jnp.float32
    ).astype(jnp.bfloat16)


def lowered_grad_of(grads, down_second):
    return jnp.einsum(
        "pqt,prq->prt", grads, down_second, preferred_element_type=jnp.float32
    ).astype(jnp.bfloat16)


def forward_middle(spread_r, up_second, down_first):
    mixed = jnp.einsum(
        "prgt,grpo->grot", spread_r, up_second, preferred_element_type=jnp.float32
    )
    hidden = (jax.nn.silu(mixed[0]) * mixed[1]).astype(jnp.bfloat16)
    lowered = jnp.einsum(
        "rot,rop->rpt", hidden, down_first, preferred_element_type=jnp.float32
    ).astype(jnp.bfloat16)
    return mixed, hidden, lowered


def backward_middle(mixed, grad_lowered_r, up_second, down_first):
    grad_hidden = jnp.einsum(
        "prt,rop->rot", grad_lowered_r, down_first, preferred_element_type=jnp.float32
    )
    sigmoid_gate = jax.nn.sigmoid(mixed[0])
    slope = sigmoid_gate * (1.0 + mixed[0] * (1.0 - sigmoid_gate))
    grad_mixed = jnp.stack(
        [grad_hidden * mixed[1] * slope, grad_hidden * mixed[0] * sigmoid_gate]
    ).astype(jnp.bfloat16)
    grad_spread = jnp.einsum(
        "grot,grpo->rpgt", grad_mixed, up_second, preferred_element_type=jnp.float32
    ).astype(jnp.bfloat16)
    return grad_mixed, grad_spread


def output_of(values, lowered_p, down_second):
    added = jnp.einsum("rpt,prq->pqt", lowered_p, down_second, preferred_element_type=jnp.float32)
    return (values.astype(jnp.float32) + added).astype(jnp.bfloat16)


def input_grad_of(grads, grad_spread_p, up_first):
    added = jnp.einsum(
        "rpgt,gpqr->pqt", grad_spread_p, up_first, preferred_element_type=jnp.float32
    )
    return (grads.astype(jnp.float32) + added).astype(jnp.bfloat16)


def shards(
    held_input,
    fresh_input,
    stashed,
    held_grad,
    fresh_grad,
    first_up,
    second_up,
    first_down,
    second_down,
):
    feature_blocks = first_up.shape[2]
    hidden_blocks = second_up.shape[2]
    tokens = held_input.shape[2]
    up_first = first_up[0].reshape(2, feature_blocks, FIRST_IN, SECOND_BLOCKS)
    up_second = second_up[0].reshape(2, hidden_blocks, FIRST_BLOCKS, BLOCK)
    down_first = first_down[0].reshape(hidden_blocks, BLOCK, FIRST_BLOCKS)
    down_second = second_down[0].reshape(feature_blocks, SECOND_BLOCKS, FIRST_IN)
    first_inputs = held_input[0].reshape(feature_blocks, FIRST_IN, tokens)
    first_grads = held_grad[0].reshape(feature_blocks, FIRST_IN, tokens)
    stash_views = [
        stashed[0, k].reshape(feature_blocks, FIRST_IN, tokens) for k in range(TICKS)
    ]
    section_pos = lax.axis_index("section")
    last_section = lax.axis_size("section") - 1
    t = tokens

    values_a = jnp.concatenate([first_inputs] + stash_views, axis=2)
    spread_a = spread_of(values_a, up_first)
    glow_1 = lowered_grad_of(first_grads, down_second)
    payload = jnp.concatenate(
        [spread_a.reshape(feature_blocks, SECOND_BLOCKS, 2 * 3 * t), glow_1], axis=2
    )
    arrived = to_blocks(payload)
    spread_ar = arrived[:, :, : 6 * t].reshape(FIRST_BLOCKS, hidden_blocks, 2, 3 * t)
    glow_1r = arrived[:, :, 6 * t :]
    mixed_a, hidden_a, lowered_a = forward_middle(spread_ar, up_second, down_first)
    gmix_1, gspread_1 = backward_middle(mixed_a[:, :, :, t : 2 * t], glow_1r, up_second, down_first)
    payload = jnp.concatenate(
        [lowered_a, gspread_1.reshape(hidden_blocks, FIRST_BLOCKS, 2 * t)], axis=2
    )
    back = to_features(payload)
    lowered_ap = back[:, :, : 3 * t]
    gspread_1p = back[:, :, 3 * t :].reshape(SECOND_BLOCKS, feature_blocks, 2, t)
    outputs = output_of(first_inputs, lowered_ap[:, :, :t], down_second)
    backward = input_grad_of(first_grads, gspread_1p, up_first)

    moved_forward = from_behind(outputs, "section", 1)
    inputs = jnp.where(
        section_pos == 0,
        fresh_input.reshape(feature_blocks, FIRST_IN, tokens),
        moved_forward,
    )
    moved_backward = from_behind(backward, "section", -1)
    grads = jnp.where(
        section_pos == last_section,
        fresh_grad.reshape(feature_blocks, FIRST_IN, tokens),
        moved_backward,
    )

    spread_b = spread_of(inputs, up_first)
    glow_2 = lowered_grad_of(grads, down_second)
    payload = jnp.concatenate(
        [spread_b.reshape(feature_blocks, SECOND_BLOCKS, 2 * t), glow_2], axis=2
    )
    arrived = to_blocks(payload)
    spread_br = arrived[:, :, : 2 * t].reshape(FIRST_BLOCKS, hidden_blocks, 2, t)
    glow_2r = arrived[:, :, 2 * t :]
    _, _, lowered_b = forward_middle(spread_br, up_second, down_first)
    gmix_2, gspread_2 = backward_middle(
        mixed_a[:, :, :, 2 * t :], glow_2r, up_second, down_first
    )
    payload = jnp.concatenate(
        [lowered_b, gspread_2.reshape(hidden_blocks, FIRST_BLOCKS, 2 * t)], axis=2
    )
    back = to_features(payload)
    lowered_bp = back[:, :, :t]
    gspread_2p = back[:, :, t:].reshape(SECOND_BLOCKS, feature_blocks, 2, t)
    outputs = output_of(inputs, lowered_bp, down_second)
    backward = input_grad_of(grads, gspread_2p, up_first)

    stash_both = jnp.concatenate(stash_views, axis=2)
    gspread_both = jnp.concatenate([gspread_1p, gspread_2p], axis=3)
    spread_both = spread_ar[:, :, :, t:]
    gmix_both = jnp.concatenate([gmix_1, gmix_2], axis=3)
    hidden_both = hidden_a[:, :, t:]
    glow_both = jnp.concatenate([glow_1r, glow_2r], axis=2)
    lowered_both = lowered_ap[:, :, t:]
    grads_both = jnp.concatenate([first_grads, grads], axis=2)
    total_first_up = jnp.einsum(
        "pqt,rpgt->gpqr", stash_both, gspread_both, preferred_element_type=jnp.float32
    )
    total_second_up = jnp.einsum(
        "prgt,grot->grpo", spread_both, gmix_both, preferred_element_type=jnp.float32
    )
    total_first_down = jnp.einsum(
        "rot,prt->rop", hidden_both, glow_both, preferred_element_type=jnp.float32
    )
    total_second_down = jnp.einsum(
        "rpt,pqt->prq", lowered_both, grads_both, preferred_element_type=jnp.float32
    )
    factor = 1.0 / math.sqrt(TICKS * tokens)
    return (
        outputs.reshape(held_input.shape),
        backward.reshape(held_grad.shape),
        (total_first_up * factor).astype(jnp.bfloat16).reshape(first_up.shape),
        (total_second_up * factor).astype(jnp.bfloat16).reshape(second_up.shape),
        (total_first_down * factor).astype(jnp.bfloat16).reshape(first_down.shape),
        (total_second_down * factor).astype(jnp.bfloat16).reshape(second_down.shape),
    )


def solution(mesh):
    return jax.shard_map(
        shards,
        mesh=mesh,
        in_specs=(
            P("section", "blk", None),
            P("blk", None),
            P("section", None, "blk", None),
            P("section", "blk", None),
            P("blk", None),
            P("section", None, "blk", None),
            P("section", None, "blk", None),
            P("section", "blk", None),
            P("section", "blk", None),
        ),
        out_specs=(
            P("section", "blk", None),
            P("section", "blk", None),
            P("section", None, "blk", None),
            P("section", None, "blk", None),
            P("section", "blk", None),
            P("section", "blk", None),
        ),
        check_vma=False,
    )
```

time: 200 us -> 190 us (0.950)
  the two profiles are of different devices: /device:TPU:96 before, /device:TPU:224 now
where the time goes in v1:
time: 190 us; the launch traced here: 189 us
  waiting for transfers between devices  80.6 us (42%)
  local copies, waits for them, and re-layouts  45.8 us (24%)
  blocking collectives  20.6 us (11%)
  starting transfers between devices  19.6 us (10%)
  matrix products  19.3 us (10%)
  other arithmetic  2.32 us (1%)
    all_to_all x2, waiting for transfers between devices, to_features(): lax.all_to_all(pieces, 'blk', split_axis=1, concat_axis=0, tiled=True)  46.2 us
    all_to_all x1, waiting for transfers between devices, to_blocks(): lax.all_to_all(pieces, 'blk', split_axis=1, concat_axis=0, tiled=True)  31.3 us
    all_to_all x1, blocking collectives, to_blocks(): lax.all_to_all(pieces, 'blk', split_axis=1, concat_axis=0, tiled=True)  20.6 us
    unnamed x66, local copies, waits for them, and re-layouts  9.14 us
    all_to_all x2, starting transfers between devices, to_features(): lax.all_to_all(pieces, 'blk', split_axis=1, concat_axis=0, tiled=True)  8.12 us
    all_to_all x1, starting transfers between devices, to_blocks(): lax.all_to_all(pieces, 'blk', split_axis=1, concat_axis=0, tiled=True)  7.18 us
    slice x2, local copies, waits for them, and re-layouts, shards(): arrived[:, :, :6 * t].reshape(FIRST_BLOCKS, hidden_blocks, 2, 3 * t)  5.57 us
    concatenate x1, local copies, waits for them, and re-layouts, shards(): jnp.concatenate([lowered_a, gspread_1.reshape(hidden_blocks, FIRST_BLOCKS...  5.41 us
  transfers between devices with their start and end apart: 5, of which 4 were waited for; matrix products, arithmetic and copies ran while one was open for 10% of the time, Pallas kernels for 0%

profile of v1, /device:TPU:224, one launch (start us, length us, event | category | flops | bytes accessed | tf_op | source)
XLA Modules:
  0.0 189.4 jit_solution(17170293980062510391)
XLA Ops:
  7.4 2.1 %copy.123 = bf16[8,160,896]{2,0,1:T(8,128)(2,1)} copy(bf16[8,160,896]{2,1,0:T(8,128)(2,1)S(1)} %pad_maximum_fusion) | data formatting | bytes 4587520 | tf_op jit(solution)/shard_map/concatenate | solution.py:109
  9.6 7.2 %all-to-all-start = ((bf16[8,160,896]{2,0,1:T(8,128)(2,1)}), bf16[8,160,896]{2,0,1:T(8,128)(2,1)S(1)}, u32[]{:S(2)}, u32[]{:S(2)}) async-start(bf16[8,160,896]{2,0,1:T(8,128)(2,1)} %copy.123), calls=%async_computation | async-start | bytes 4587520 | tf_op jit(solution)/shard_map/all_to_all | solution.py:22
  17.7 2.3 %reshape_squeeze.30 = bf16[2,10,128,128]{3,2,0,1:T(8,128)(2,1)S(1)} reshape(bf16[1,2,10,16384]{3,1,2,0:T(2,128)(2,1)} %param.15) | data formatting | bytes 1310720 | tf_op jit(solution)/shard_map/reshape;squeeze | solution.py:94
  20.0 31.3 %all-to-all-done = bf16[8,160,896]{2,0,1:T(8,128)(2,1)S(1)} async-done(((bf16[8,160,896]{2,0,1:T(8,128)(2,1)}), bf16[8,160,896]{2,0,1:T(8,128)(2,1)S(1)}, u32[]{:S(2)}, u32[]{:S(2)}) %all-to-all-start) | async-done | bytes 2293792 | tf_op jit(solution)/shard_map/all_to_all | solution.py:22
  52.7 2.0 %copy.229 = bf16[16,8,10,896]{3,1,0,2:T(8,128)(2,1)S(1)} copy(bf16[16,8,10,896]{3,1,2,0:T(8,128)(2,1)} %bitcast.208) | data formatting | bytes 4587520 | tf_op jit(solution)/shard_map/all_to_all | solution.py:22
  56.2 4.0 %copy.125 = bf16[128,10,768]{0,2,1:T(8,128)(2,1)} copy(bf16[128,10,768]{2,0,1:T(8,128)(2,1)} %slice.97) | data formatting | bytes 3932160 | tf_op jit(solution)/shard_map/slice | solution.py:113
  60.2 2.2 %convolution_bitcast_fusion = f32[2,10,128,384]{2,3,1,0:T(8,128)S(1)} fusion(bf16[128,10,2,384]{0,3,2,1:T(8,128)(2,1)} %bitcast.209, bf16[2,10,128,128]{3,2,0,1:T(8,128)(2,1)S(1)} %reshape_squeeze.30), kind=kOutput, calls=%fused_computation.2 | convolution fusion | flops 251658240 | bytes 6553600 | tf_op jit(solution)/shard_map/prgt,grpo->grot/dot_general | solution.py:42
  66.0 5.4 %copy.130 = bf16[10,128,640]{2,0,1:T(8,128)(2,1)} copy(bf16[10,128,640]{1,2,0:T(8,128)(2,1)S(1)} %pad_maximum_fusion.1) | data formatting | bytes 3276800 | tf_op jit(solution)/shard_map/concatenate | solution.py:117
  71.4 3.7 %all-to-all-start.1 = ((bf16[10,128,640]{2,0,1:T(8,128)(2,1)}), bf16[10,128,640]{2,0,1:T(8,128)(2,1)S(1)}, u32[]{:S(2)}, u32[]{:S(2)}) async-start(bf16[10,128,640]{2,0,1:T(8,128)(2,1)} %copy.130), calls=%async_computation.1 | async-start | bytes 5242880 | tf_op jit(solution)/shard_map/all_to_all | solution.py:26
  75.2 37.0 %all-to-all-done.1 = bf16[10,128,640]{2,0,1:T(8,128)(2,1)S(1)} async-done(((bf16[10,128,640]{2,0,1:T(8,128)(2,1)}), bf16[10,128,640]{2,0,1:T(8,128)(2,1)S(1)}, u32[]{:S(2)}, u32[]{:S(2)}) %all-to-all-start.1) | async-done | bytes 1638432 | tf_op jit(solution)/shard_map/all_to_all | solution.py:26
  113.9 1.9 %collective-permute-start.1 = (bf16[8,40,128]{2,1,0:T(8,128)(2,1)S(1)}, bf16[8,40,128]{2,1,0:T(8,128)(2,1)S(1)}, u32[]{:S(2)}, u32[]{:S(2)}) collective-permute-start(bf16[8,40,128]{2,1,0:T(8,128)(2,1)S(1)} %fusion.33), channel_id=1, source_target_pairs={{16,0},{32,16},{48,32},{64,48},{80,64},{96,80},{112,96},{128,112},... | collective-permute-start | bytes 245768 | tf_op jit(solution)/shard_map/ppermute | solution.py:18
  116.1 2.4 %collective-permute-start = (bf16[8,40,128]{2,1,0:T(8,128)(2,1)S(1)}, bf16[8,40,128]{2,1,0:T(8,128)(2,1)S(1)}, u32[]{:S(2)}, u32[]{:S(2)}) collective-permute-start(bf16[8,40,128]{2,1,0:T(8,128)(2,1)S(1)} %fusion.34), channel_id=1, source_target_pairs={{0,16},{16,32},{32,48},{48,64},{64,80},{80,96},{96,112},{112,128},... | collective-permute-start | bytes 245768 | tf_op jit(solution)/shard_map/ppermute | solution.py:18
  118.8 3.1 %collective-permute-done = bf16[8,40,128]{2,1,0:T(8,128)(2,1)S(1)} collective-permute-done((bf16[8,40,128]{2,1,0:T(8,128)(2,1)S(1)}, bf16[8,40,128]{2,1,0:T(8,128)(2,1)S(1)}, u32[]{:S(2)}, u32[]{:S(2)}) %collective-permute-start) | collective-permute-done | bytes 81952 | tf_op jit(solution)/shard_map/ppermute | solution.py:18
  123.0 20.6 %all_to_all.72 = bf16[8,160,384]{2,0,1:T(8,128)(2,1)S(1)} all-to-all(bf16[8,160,384]{2,0,1:T(8,128)(2,1)S(1)} %copy.140), channel_id=1, replica_groups=mesh['section'=32,'blk'=16] {'blk'}, dimensions={1} | all-to-all | bytes 1966080 | tf_op jit(solution)/shard_map/all_to_all | solution.py:22
  143.7 2.7 %fusion.59 = (bf16[1,10,128,128]{2,3,1,0:T(8,128)(2,1)}, bf16[1,10,128,128]{2,3,1,0:T(8,128)(2,1)}) fusion(f32[2,10,128,384]{2,3,1,0:T(8,128)} %copy-done, bf16[16,128,128]{2,1,0:T(8,128)(2,1)S(1)} %bitcast.224, bf16[128,10,384]{2,0,1:T(8,128)(2,1)S(1)} %bitcast.216), kind=kOutput, calls=%fused_computation.94 | convolution fusion | flops 44072960 | bytes 2621440 | tf_op jit(solution)/shard_map/prt,rop->rot/dot_general | solution.py:53
  148.6 2.5 %convolution_convert_fusion.2 = bf16[10,2,128,128]{3,2,1,0:T(8,128)(2,1)} fusion(bf16[2,10,128,128]{3,2,0,1:T(8,128)(2,1)S(1)} %copy-done.5, bf16[1,10,128,128]{2,3,1,0:T(8,128)(2,1)} %get-tuple-element.31, bf16[1,10,128,128]{2,3,1,0:T(8,128)(2,1)} %get-tuple-element.30), kind=kOutput, calls=%fused_computation.17 | convolution fusion | flops 84541440 | bytes 1966080 | tf_op jit(solution)/shard_map/grot,grpo->rpgt/dot_general | solution.py:61
  151.0 2.0 %copy.148 = bf16[10,128,256]{2,0,1:T(8,128)(2,1)S(1)} copy(bf16[10,128,256]{1,2,0:T(8,128)(2,1)} %bitcast.226) | data formatting | bytes 1310720 | tf_op jit(solution)/shard_map/reshape | solution.py:152
  154.4 4.4 %all-to-all-start.3 = ((bf16[10,128,384]{2,0,1:T(8,128)(2,1)}), bf16[10,128,384]{2,0,1:T(8,128)(2,1)}, u32[]{:S(2)}, u32[]{:S(2)}) async-start(bf16[10,128,384]{2,0,1:T(8,128)(2,1)} %pad_maximum_fusion.2), calls=%async_computation.3 | async-start | bytes 3145728 | tf_op jit(solution)/shard_map/all_to_all | solution.py:26
  160.7 2.2 %copy.137 = bf16[160,8,2,128]{3,0,2,1:T(8,128)(2,1)} copy(bf16[160,8,2,128]{3,1,2,0:T(8,128)(2,1)} %copy-done.11) | data formatting | bytes 1310720 | tf_op jit(solution)/shard_map/reshape | solution.py:122
  163.0 2.1 %fusion.30 = bf16[8,160,40]{1,2,0:T(8,128)(2,1)} fusion(bf16[160,8,256]{2,1,0:T(8,128)(2,1)} %get-tuple-element.34, bf16[8,40,128]{2,1,0:T(8,128)(2,1)} %copy-done.23, bf16[8,40,128]{2,1,0:T(8,128)(2,1)} %bitcast.239), kind=kOutput, calls=%fused_computation.45 | convolution fusion | flops 26644480 | bytes 921600 | tf_op jit(solution)/shard_map/rpt,pqt->prq/dot_general | solution.py:177
  165.1 1.8 copy.163
  166.9 2.0 %reshape.75 = bf16[1,8,6400]{2,1,0:T(8,128)(2,1)} reshape(bf16[8,160,40]{2,1,0:T(8,128)(2,1)} %copy.163) | data formatting | bytes 204800 | tf_op jit(solution)/shard_map/reshape | solution.py:187
  169.7 1.8 fusion.3
  174.6 9.2 %all-to-all-done.3 = bf16[10,128,384]{2,0,1:T(8,128)(2,1)} async-done(((bf16[10,128,384]{2,0,1:T(8,128)(2,1)}), bf16[10,128,384]{2,0,1:T(8,128)(2,1)}, u32[]{:S(2)}, u32[]{:S(2)}) %all-to-all-start.3) | async-done | bytes 983072 | tf_op jit(solution)/shard_map/all_to_all | solution.py:26
  (110 shorter events, 32.3 us)
Async XLA Ops:
  2.9 3.4 %copy-start.8 = (bf16[2,8,40,160]{3,2,1,0:T(8,128)(2,1)}, bf16[2,8,40,160]{3,2,1,0:T(8,128)(2,1)S(1)}, u32[]{:S(2)}) copy-start(bf16[2,8,40,160]{3,2,1,0:T(8,128)(2,1)S(1)} %reshape_squeeze.27) | copy-start | bytes 614404
  9.6 7.2 %copy-start.17 = (bf16[1,10,16384]{2,1,0:T(8,128)(2,1)S(1)}, bf16[1,10,16384]{2,1,0:T(8,128)(2,1)}, u32[]{:S(2)}) copy-start(bf16[1,10,16384]{2,1,0:T(8,128)(2,1)} %param.16) | copy-start | bytes 983044
  9.6 41.7 %all-to-all-start = ((bf16[8,160,896]{2,0,1:T(8,128)(2,1)}), bf16[8,160,896]{2,0,1:T(8,128)(2,1)S(1)}, u32[]{:S(2)}, u32[]{:S(2)}) async-start(bf16[8,160,896]{2,0,1:T(8,128)(2,1)} %copy.123), calls=%async_computation | async-start | bytes 4587520 | tf_op jit(solution)/shard_map/all_to_all | solution.py:22
  20.0 45.3 %copy-start.4 = (bf16[2,10,128,128]{3,2,0,1:T(8,128)(2,1)}, bf16[2,10,128,128]{3,2,0,1:T(8,128)(2,1)S(1)}, u32[]{:S(2)}) copy-start(bf16[2,10,128,128]{3,2,0,1:T(8,128)(2,1)S(1)} %reshape_squeeze.30) | copy-start | bytes 1966084
  54.6 8.4 %copy-start.1 = (bf16[16,8,10,896]{3,1,0,2:T(8,128)(2,1)}, bf16[16,8,10,896]{3,1,0,2:T(8,128)(2,1)S(1)}, u32[]{:S(2)}) copy-start(bf16[16,8,10,896]{3,1,0,2:T(8,128)(2,1)S(1)} %copy.229) | copy-start | bytes 6881284
  62.4 1.9 copy-start
  62.4 1.9 copy-start.12
  63.0 1.9 copy-start.6
  71.4 40.7 %all-to-all-start.1 = ((bf16[10,128,640]{2,0,1:T(8,128)(2,1)}), bf16[10,128,640]{2,0,1:T(8,128)(2,1)S(1)}, u32[]{:S(2)}, u32[]{:S(2)}) async-start(bf16[10,128,640]{2,0,1:T(8,128)(2,1)} %copy.130), calls=%async_computation.1 | async-start | bytes 5242880 | tf_op jit(solution)/shard_map/all_to_all | solution.py:26
  112.5 3.3 %copy-start.18 = (bf16[1,320,128]{2,1,0:T(8,128)(2,1)S(1)}, bf16[1,320,128]{2,1,0:T(8,128)(2,1)}, u32[]{:S(2)}) copy-start(bf16[1,320,128]{2,1,0:T(8,128)(2,1)} %param.9) | copy-start | bytes 245764
  112.6 6.0 %copy-start.25 = (bf16[320,128]{1,0:T(8,128)(2,1)S(1)}, bf16[320,128]{1,0:T(8,128)(2,1)}, u32[]{:S(2)}) copy-start(bf16[320,128]{1,0:T(8,128)(2,1)} %param.13) | copy-start | bytes 245764
  113.6 8.8 %copy-start.11 = (bf16[160,8,2,128]{3,1,2,0:T(8,128)(2,1)}, bf16[160,8,2,128]{3,1,2,0:T(8,128)(2,1)S(1)}, u32[]{:S(2)}) copy-start(bf16[160,8,2,128]{3,1,2,0:T(8,128)(2,1)S(1)} %get-tuple-element.35) | copy-start | bytes 1966084
  113.6 8.3 %copy-start.19 = (bf16[320,128]{1,0:T(8,128)(2,1)S(1)}, bf16[320,128]{1,0:T(8,128)(2,1)}, u32[]{:S(2)}) copy-start(bf16[320,128]{1,0:T(8,128)(2,1)} %param.10) | copy-start | bytes 245764
  113.9 4.6 %collective-permute-start.1 = (bf16[8,40,128]{2,1,0:T(8,128)(2,1)S(1)}, bf16[8,40,128]{2,1,0:T(8,128)(2,1)S(1)}, u32[]{:S(2)}, u32[]{:S(2)}) collective-permute-start(bf16[8,40,128]{2,1,0:T(8,128)(2,1)S(1)} %fusion.33), channel_id=1, source_target_pairs={{16,0},{32,16},{48,32},{64,48},{80,64},{96,80},{112,96},{128,112},... | collective-permute-start | bytes 245768 | tf_op jit(solution)/shard_map/ppermute | solution.py:18
  116.1 5.8 %collective-permute-start = (bf16[8,40,128]{2,1,0:T(8,128)(2,1)S(1)}, bf16[8,40,128]{2,1,0:T(8,128)(2,1)S(1)}, u32[]{:S(2)}, u32[]{:S(2)}) collective-permute-start(bf16[8,40,128]{2,1,0:T(8,128)(2,1)S(1)} %fusion.34), channel_id=1, source_target_pairs={{0,16},{16,32},{32,48},{48,64},{64,80},{80,96},{96,112},{112,128},... | collective-permute-start | bytes 245768 | tf_op jit(solution)/shard_map/ppermute | solution.py:18
  118.6 3.3 %copy-start.23 = (bf16[8,40,128]{2,1,0:T(8,128)(2,1)}, bf16[8,40,128]{2,1,0:T(8,128)(2,1)S(1)}, u32[]{:S(2)}) copy-start(bf16[8,40,128]{2,1,0:T(8,128)(2,1)S(1)} %broadcast_select_fusion) | copy-start | bytes 245764
  123.0 20.7 %copy-start.13 = (bf16[2,8,128,128]{3,2,1,0:T(8,128)(2,1)S(1)}, bf16[2,8,128,128]{3,2,1,0:T(8,128)(2,1)}, u32[]{:S(2)}) copy-start(bf16[2,8,128,128]{3,2,1,0:T(8,128)(2,1)} %copy.187) | copy-start | bytes 1572868
  154.4 29.4 %all-to-all-start.3 = ((bf16[10,128,384]{2,0,1:T(8,128)(2,1)}), bf16[10,128,384]{2,0,1:T(8,128)(2,1)}, u32[]{:S(2)}, u32[]{:S(2)}) async-start(bf16[10,128,384]{2,0,1:T(8,128)(2,1)} %pad_maximum_fusion.2), calls=%async_computation.3 | async-start | bytes 3145728 | tf_op jit(solution)/shard_map/all_to_all | solution.py:26
  160.7 9.0 %copy-start.3 = (bf16[128,10,768]{0,2,1:T(8,128)(2,1)S(1)}, bf16[128,10,768]{0,2,1:T(8,128)(2,1)}, u32[]{:S(2)}) copy-start(bf16[128,10,768]{0,2,1:T(8,128)(2,1)} %copy.125) | copy-start | bytes 5898244
  171.6 1.5 copy-start.7
  171.6 1.6 copy-start.22
  183.8 1.9 copy-start.10
  183.8 1.9 copy-start.24
  186.8 1.7 copy-start.21
  (11 other events, 11.7 us)

commit v2 on v1

v2 whole, which is shorter than its diff:
```python
import math

import jax
import jax.numpy as jnp
from jax import lax
from jax.sharding import PartitionSpec as P

BLOCK = 128
FIRST_BLOCKS = 128
FIRST_IN = 40
SECOND_BLOCKS = 160
TICKS = 2


def from_behind(value, axis, by):
    length = lax.axis_size(axis)
    pairs = [(i, i + by) for i in range(length) if 0 <= i + by < length]
    return lax.ppermute(value, axis, pairs)


def exchange(pieces):
    return lax.all_to_all(pieces, "blk", split_axis=0, concat_axis=1, tiled=True)


def spread_of(values, up_first):
    spread = jnp.einsum(
        "pqt,gpqr->rpgt", values, up_first, preferred_element_type=jnp.float32
    ).astype(jnp.bfloat16)
    return spread.reshape(spread.shape[0], spread.shape[1], -1)


def lowered_grad_of(grads, down_second):
    return jnp.einsum(
        "pqt,prq->rpt", grads, down_second, preferred_element_type=jnp.float32
    ).astype(jnp.bfloat16)


def forward_middle(spread_r, up_second, down_first):
    mixed = jnp.einsum(
        "rpgt,grpo->grot", spread_r, up_second, preferred_element_type=jnp.float32
    )
    hidden = (jax.nn.silu(mixed[0]) * mixed[1]).astype(jnp.bfloat16)
    lowered = jnp.einsum(
        "rot,rop->prt", hidden, down_first, preferred_element_type=jnp.float32
    ).astype(jnp.bfloat16)
    return mixed, hidden, lowered


def backward_middle(mixed, grad_lowered_r, up_second, down_first):
    grad_hidden = jnp.einsum(
        "rpt,rop->rot", grad_lowered_r, down_first, preferred_element_type=jnp.float32
    )
    sigmoid_gate = jax.nn.sigmoid(mixed[0])
    slope = sigmoid_gate * (1.0 + mixed[0] * (1.0 - sigmoid_gate))
    grad_mixed = jnp.stack(
        [grad_hidden * mixed[1] * slope, grad_hidden * mixed[0] * sigmoid_gate]
    ).astype(jnp.bfloat16)
    grad_spread = jnp.einsum(
        "grot,grpo->prgt", grad_mixed, up_second, preferred_element_type=jnp.float32
    ).astype(jnp.bfloat16)
    return grad_mixed, grad_spread.reshape(grad_spread.shape[0], grad_spread.shape[1], -1)


def output_of(values, lowered_p, down_second):
    added = jnp.einsum("prt,prq->pqt", lowered_p, down_second, preferred_element_type=jnp.float32)
    return (values.astype(jnp.float32) + added).astype(jnp.bfloat16)


def input_grad_of(grads, grad_spread_p, up_first):
    added = jnp.einsum(
        "prgt,gpqr->pqt", grad_spread_p, up_first, preferred_element_type=jnp.float32
    )
    return (grads.astype(jnp.float32) + added).astype(jnp.bfloat16)


def shards(
    held_input,
    fresh_input,
    stashed,
    held_grad,
    fresh_grad,
    first_up,
    second_up,
    first_down,
    second_down,
):
    pb = first_up.shape[2]
    rb = second_up.shape[2]
    t = held_input.shape[2]
    up_first = first_up[0].reshape(2, pb, FIRST_IN, SECOND_BLOCKS)
    up_second = second_up[0].reshape(2, rb, FIRST_BLOCKS, BLOCK)
    down_first = first_down[0].reshape(rb, BLOCK, FIRST_BLOCKS)
    down_second = second_down[0].reshape(pb, SECOND_BLOCKS, FIRST_IN)
    first_inputs = held_input[0].reshape(pb, FIRST_IN, t)
    first_grads = held_grad[0].reshape(pb, FIRST_IN, t)
    stash_0 = stashed[0, 0].reshape(pb, FIRST_IN, t)
    stash_1 = stashed[0, 1].reshape(pb, FIRST_IN, t)
    section_pos = lax.axis_index("section")
    last_section = lax.axis_size("section") - 1

    spread_a = spread_of(jnp.concatenate([first_inputs, stash_0], axis=2), up_first)
    glow_1 = lowered_grad_of(first_grads, down_second)
    arrived = exchange(jnp.concatenate([spread_a, glow_1], axis=2))
    spread_ar = arrived[:, :, : 4 * t].reshape(rb, FIRST_BLOCKS, 2, 2 * t)
    glow_1r = arrived[:, :, 4 * t :]
    spread_s1r = exchange(spread_of(stash_1, up_first)).reshape(rb, FIRST_BLOCKS, 2, t)

    mixed_a, hidden_a, lowered_a = forward_middle(spread_ar, up_second, down_first)
    gmix_1, gspread_1 = backward_middle(mixed_a[..., t:], glow_1r, up_second, down_first)
    back = exchange(jnp.concatenate([lowered_a[..., :t], gspread_1], axis=2))
    outputs = output_of(first_inputs, back[..., :t], down_second)
    gspread_1p = back[..., t:].reshape(pb, SECOND_BLOCKS, 2, t)
    backward = input_grad_of(first_grads, gspread_1p, up_first)

    mixed_s1, hidden_s1, lowered_s1 = forward_middle(spread_s1r, up_second, down_first)
    lowered_sp = exchange(jnp.concatenate([lowered_a[..., t:], lowered_s1], axis=2))

    moved_forward = from_behind(outputs, "section", 1)
    inputs = jnp.where(section_pos == 0, fresh_input.reshape(pb, FIRST_IN, t), moved_forward)
    moved_backward = from_behind(backward, "section", -1)
    grads = jnp.where(
        section_pos == last_section, fresh_grad.reshape(pb, FIRST_IN, t), moved_backward
    )

    spread_b = spread_of(inputs, up_first)
    glow_2 = lowered_grad_of(grads, down_second)
    arrived = exchange(jnp.concatenate([spread_b, glow_2], axis=2))
    spread_br = arrived[:, :, : 2 * t].reshape(rb, FIRST_BLOCKS, 2, t)
    glow_2r = arrived[:, :, 2 * t :]
    _, _, lowered_b = forward_middle(spread_br, up_second, down_first)
    gmix_2, gspread_2 = backward_middle(mixed_s1, glow_2r, up_second, down_first)
    back = exchange(jnp.concatenate([lowered_b, gspread_2], axis=2))
    outputs = output_of(inputs, back[..., :t], down_second)
    gspread_2p = back[..., t:].reshape(pb, SECOND_BLOCKS, 2, t)
    backward = input_grad_of(grads, gspread_2p, up_first)

    stash_both = jnp.concatenate([stash_0, stash_1], axis=2)
    gspread_both = jnp.concatenate([gspread_1p, gspread_2p], axis=3)
    spread_both = jnp.concatenate([spread_ar[..., t:], spread_s1r], axis=3)
    gmix_both = jnp.concatenate([gmix_1, gmix_2], axis=3)
    hidden_both = jnp.concatenate([hidden_a[..., t:], hidden_s1], axis=2)
    glow_both = jnp.concatenate([glow_1r, glow_2r], axis=2)
    grads_both = jnp.concatenate([first_grads, grads], axis=2)
    total_first_up = jnp.einsum(
        "pqt,prgt->gpqr", stash_both, gspread_both, preferred_element_type=jnp.float32
    )
    total_second_up = jnp.einsum(
        "rpgt,grot->grpo", spread_both, gmix_both, preferred_element_type=jnp.float32
    )
    total_first_down = jnp.einsum(
        "rot,rpt->rop", hidden_both, glow_both, preferred_element_type=jnp.float32
    )
    total_second_down = jnp.einsum(
        "prt,pqt->prq", lowered_sp, grads_both, preferred_element_type=jnp.float32
    )
    factor = 1.0 / math.sqrt(TICKS * t)
    return (
        outputs.reshape(held_input.shape),
        backward.reshape(held_grad.shape),
        (total_first_up * factor).astype(jnp.bfloat16).reshape(first_up.shape),
        (total_second_up * factor).astype(jnp.bfloat16).reshape(second_up.shape),
        (total_first_down * factor).astype(jnp.bfloat16).reshape(first_down.shape),
        (total_second_down * factor).astype(jnp.bfloat16).reshape(second_down.shape),
    )


def solution(mesh):
    return jax.shard_map(
        shards,
        mesh=mesh,
        in_specs=(
            P("section", "blk", None),
            P("blk", None),
            P("section", None, "blk", None),
            P("section", "blk", None),
            P("blk", None),
            P("section", None, "blk", None),
            P("section", None, "blk", None),
            P("section", "blk", None),
            P("section", "blk", None),
        ),
        out_specs=(
            P("section", "blk", None),
            P("section", "blk", None),
            P("section", None, "blk", None),
            P("section", None, "blk", None),
            P("section", "blk", None),
            P("section", "blk", None),
        ),
        check_vma=False,
    )
```

time: 190 us -> 209 us (1.10)
  blocking collectives: 20.6 us -> 0 us
  starting transfers between devices: 19.6 us -> 36.4 us
  local copies, waits for them, and re-layouts: 45.8 us -> 61.7 us
  other arithmetic: 2.32 us -> 9.02 us
  waiting for transfers between devices: 80.6 us -> 75.3 us
  matrix products: 19.3 us -> 23.3 us
    all_to_all x1 -> x0, blocking collectives: 20.6 us -> none  [to_blocks(): lax.all_to_all(pieces, 'blk', split_axis=1, concat_axis=0, tiled=True)]
    all_to_all x3 -> x6, starting transfers between devices: 15.3 us -> 32 us  [exchange(): lax.all_to_all(pieces, 'blk', split_axis=0, concat_axis=1, tiled=True)]
    reshape x6 -> x9, local copies, waits for them, and re-layouts: 4.8 us -> 14.7 us  [the longest x2 5.28 us: backward_middle(): grad_spread.reshape(grad_spread.shape[0], grad_spread.shape[1], -1)]
    concatenate x4 -> x5, other arithmetic: 1.79 us -> 8.65 us  [the longest x1 2.69 us: shards(): back = exchange(jnp.concatenate([lowered_b, gspread_2], axis=2))]
    convert_element_type x1 -> x6, local copies, waits for them, and re-layouts: 0.43 us -> 6.57 us  [the longest x3 4.16 us: spread_of(): spread = jnp.einsum('pqt,gpqr->rpgt', values, up_first, preferred_element...]
    all_to_all x4 -> x6, local copies, waits for them, and re-layouts: 4.11 us -> 9.76 us  [exchange(): lax.all_to_all(pieces, 'blk', split_axis=0, concat_axis=1, tiled=True)]
    concatenate x3 -> x1, local copies, waits for them, and re-layouts: 7.86 us -> 2.61 us  [shards(): jnp.concatenate([lowered_a[..., t:], lowered_s1], axis=2)]
    all_to_all x3 -> x6, waiting for transfers between devices: 77.5 us -> 72.4 us  [exchange(): lax.all_to_all(pieces, 'blk', split_axis=0, concat_axis=1, tiled=True)]
  transfers between devices with their start and end apart: 5 -> 8, of which waited for: 4 -> 6; matrix products, arithmetic and copies ran while one was open for 10% -> 20% of each run, Pallas kernels for 0% -> 0%
where the time goes in v2:
time: 209 us; the launch traced here: 207 us
  waiting for transfers between devices  75.3 us (36%)
  local copies, waits for them, and re-layouts  61.7 us (30%)
  starting transfers between devices  36.4 us (17%)
  matrix products  23.3 us (11%)
  other arithmetic  9.02 us (4%)
    all_to_all x6, waiting for transfers between devices, exchange(): lax.all_to_all(pieces, 'blk', split_axis=0, concat_axis=1, tiled=True)  72.4 us
    all_to_all x6, starting transfers between devices, exchange(): lax.all_to_all(pieces, 'blk', split_axis=0, concat_axis=1, tiled=True)  32 us
    all_to_all x6, local copies, waits for them, and re-layouts, exchange(): lax.all_to_all(pieces, 'blk', split_axis=0, concat_axis=1, tiled=True)  9.76 us
    unnamed x77, local copies, waits for them, and re-layouts  9.76 us
    reshape x2, local copies, waits for them, and re-layouts, backward_middle(): grad_spread.reshape(grad_spread.shape[0], grad_spread.shape[1], -1)  5.28 us
    dot_general x2, matrix products, backward_middle(): jnp.einsum('grot,grpo->prgt', grad_mixed, up_second, preferred_element_ty...  4.95 us
    dot_general x3, matrix products, forward_middle(): jnp.einsum('rpgt,grpo->grot', spread_r, up_second, preferred_element_type...  4.57 us
    ppermute x2, starting transfers between devices, from_behind(): return lax.ppermute(value, axis, pairs)  4.46 us
  transfers between devices with their start and end apart: 8, of which 6 were waited for; matrix products, arithmetic and copies ran while one was open for 20% of the time, Pallas kernels for 0%

profile of v2, /device:TPU:224, one launch (start us, length us, event | category | flops | bytes accessed | tf_op | source)
XLA Modules:
  0.0 207.1 jit_solution(7776138339748848309)
XLA Ops:
  5.4 2.5 %copy.146 = bf16[160,8,2,256]{3,2,1,0:T(2,128)(2,1)} copy(bf16[160,8,2,256]{3,0,2,1:T(8,128)(2,1)S(1)} %fusion) | data formatting | bytes 2621440 | tf_op jit(solution)/shard_map/convert_element_type | solution.py:28
  7.9 3.4 %reshape.68 = bf16[160,8,512]{2,1,0:T(8,128)(2,1)S(1)} reshape(bf16[160,8,2,256]{3,2,1,0:T(2,128)(2,1)} %copy.146) | data formatting | bytes 2621440 | tf_op jit(solution)/shard_map/reshape | solution.py:29
  12.6 7.2 %all-to-all-start = ((bf16[160,8,640]{2,1,0:T(8,128)(2,1)}), bf16[160,8,640]{2,1,0:T(8,128)(2,1)}, u32[]{:S(2)}, u32[]{:S(2)}) async-start(bf16[160,8,640]{2,1,0:T(8,128)(2,1)} %pad_maximum_fusion), calls=%async_computation | async-start | bytes 3276800 | tf_op jit(solution)/shard_map/all_to_all | solution.py:22
  21.4 23.8 %all-to-all-done = bf16[160,8,640]{2,1,0:T(8,128)(2,1)} async-done(((bf16[160,8,640]{2,1,0:T(8,128)(2,1)}), bf16[160,8,640]{2,1,0:T(8,128)(2,1)}, u32[]{:S(2)}, u32[]{:S(2)}) %all-to-all-start) | async-done | bytes 1638432 | tf_op jit(solution)/shard_map/all_to_all | solution.py:22
  51.8 2.6 %fusion.65 = (bf16[1,10,128,128]{2,3,1,0:T(8,128)(2,1)}, bf16[1,10,128,128]{2,3,1,0:T(8,128)(2,1)}) fusion(f32[2,10,128,256]{2,3,1,0:T(8,128)S(1)} %convolution_bitcast_fusion, bf16[16,128,128]{2,1,0:T(8,128)(2,1)S(1)} %bitcast.240, bf16[10,128,640]{2,1,0:T(8,128)(2,1)} %bitcast.231), kind=kOutput, calls=%fused_computation.106 | convolution fusion | flops 44072960 | bytes 2621440 | tf_op jit(solution)/shard_map/rpt,rop->rot/dot_general | solution.py:50
  57.1 2.5 %convolution_convert_fusion.5 = bf16[10,2,128,128]{3,2,1,0:T(8,128)(2,1)} fusion(bf16[2,10,128,128]{3,2,0,1:T(8,128)(2,1)S(1)} %reshape_squeeze.29, bf16[1,10,128,128]{2,3,1,0:T(8,128)(2,1)} %get-tuple-element.31, bf16[1,10,128,128]{2,3,1,0:T(8,128)(2,1)} %get-tuple-element.30), kind=kOutput, calls=%fused_computation.15 | convolution fusion | flops 84541440 | bytes 1966080 | tf_op jit(solution)/shard_map/grot,grpo->prgt/dot_general | solution.py:58
  59.5 2.6 %copy.156 = bf16[128,10,256]{2,1,0:T(8,128)(2,1)} copy(bf16[128,10,256]{0,2,1:T(8,128)(2,1)} %bitcast.250) | data formatting | bytes 1310720 | tf_op jit(solution)/shard_map/reshape | solution.py:61
  62.2 2.6 %pad_maximum_fusion.1 = bf16[128,10,384]{2,1,0:T(8,128)(2,1)} fusion(bf16[128,10,256]{2,1,0:T(8,128)(2,1)} %copy.156, bf16[128,10,128]{2,1,0:T(8,128)(2,1)S(1)} %copy.155), kind=kLoop, calls=%fused_computation.4 | loop fusion | flops 1966080 | bytes 1966080 | tf_op jit(solution)/shard_map/concatenate | solution.py:110
  64.8 4.4 %all-to-all-start.1 = ((bf16[128,10,384]{2,1,0:T(8,128)(2,1)}), bf16[128,10,384]{2,1,0:T(8,128)(2,1)}, u32[]{:S(2)}, u32[]{:S(2)}) async-start(bf16[128,10,384]{2,1,0:T(8,128)(2,1)} %pad_maximum_fusion.1), calls=%async_computation.1 | async-start | bytes 3145728 | tf_op jit(solution)/shard_map/all_to_all | solution.py:22
  70.9 20.5 %all-to-all-done.1 = bf16[128,10,384]{2,1,0:T(8,128)(2,1)} async-done(((bf16[128,10,384]{2,1,0:T(8,128)(2,1)}), bf16[128,10,384]{2,1,0:T(8,128)(2,1)}, u32[]{:S(2)}, u32[]{:S(2)}) %all-to-all-start.1) | async-done | bytes 983072 | tf_op jit(solution)/shard_map/all_to_all | solution.py:22
  91.5 4.4 %all-to-all-start.3 = ((bf16[160,8,256]{2,1,0:T(8,128)(2,1)}), bf16[160,8,256]{2,1,0:T(8,128)(2,1)}, u32[]{:S(2)}, u32[]{:S(2)}) async-start(bf16[160,8,256]{2,1,0:T(8,128)(2,1)} %bitcast.226), calls=%async_computation.3 | async-start | bytes 1310720 | tf_op jit(solution)/shard_map/all_to_all | solution.py:22
  103.8 2.4 %collective-permute-start = (bf16[8,40,128]{2,1,0:T(8,128)(2,1)S(1)}, bf16[8,40,128]{2,1,0:T(8,128)(2,1)S(1)}, u32[]{:S(2)}, u32[]{:S(2)}) collective-permute-start(bf16[8,40,128]{2,1,0:T(8,128)(2,1)S(1)} %fusion.40), channel_id=1, source_target_pairs={{0,16},{16,32},{32,48},{48,64},{64,80},{80,96},{96,112},{112,128},... | collective-permute-start | bytes 245768 | tf_op jit(solution)/shard_map/ppermute | solution.py:18
  106.6 2.9 %collective-permute-done = bf16[8,40,128]{2,1,0:T(8,128)(2,1)S(1)} collective-permute-done((bf16[8,40,128]{2,1,0:T(8,128)(2,1)S(1)}, bf16[8,40,128]{2,1,0:T(8,128)(2,1)S(1)}, u32[]{:S(2)}, u32[]{:S(2)}) %collective-permute-start) | collective-permute-done | bytes 81952 | tf_op jit(solution)/shard_map/ppermute | solution.py:18
  111.6 7.0 %all-to-all-start.2 = ((bf16[160,8,384]{2,1,0:T(8,128)(2,1)}), bf16[160,8,384]{2,1,0:T(8,128)(2,1)}, u32[]{:S(2)}, u32[]{:S(2)}) async-start(bf16[160,8,384]{2,1,0:T(8,128)(2,1)} %pad_maximum_fusion.3), calls=%async_computation.2 | async-start | bytes 1966080 | tf_op jit(solution)/shard_map/all_to_all | solution.py:22
  123.8 14.0 %all-to-all-done.2 = bf16[160,8,384]{2,1,0:T(8,128)(2,1)} async-done(((bf16[160,8,384]{2,1,0:T(8,128)(2,1)}), bf16[160,8,384]{2,1,0:T(8,128)(2,1)}, u32[]{:S(2)}, u32[]{:S(2)}) %all-to-all-start.2) | async-done | bytes 983072 | tf_op jit(solution)/shard_map/all_to_all | solution.py:22
  145.6 2.6 %convolution_bitcast_fusion.2 = f32[2,10,128,128]{2,3,1,0:T(8,128)} fusion(bf16[10,128,2,128]{1,3,2,0:T(8,128)(2,1)} %bitcast.245, bf16[2,10,128,128]{3,2,0,1:T(8,128)(2,1)S(1)} %reshape_squeeze.29), kind=kOutput, calls=%fused_computation.8 | convolution fusion | flops 83886080 | bytes 2621440 | tf_op jit(solution)/shard_map/rpgt,grpo->grot/dot_general | solution.py:39
  149.1 2.6 %copy.196 = bf16[128,10,256]{2,1,0:T(8,128)(2,1)} copy(bf16[128,10,256]{0,2,1:T(8,128)(2,1)} %pad_maximum_fusion.6) | data formatting | bytes 1310720 | tf_op jit(solution)/shard_map/concatenate | solution.py:116
  151.7 4.3 %all-to-all-start.5 = ((bf16[128,10,256]{2,1,0:T(8,128)(2,1)}), bf16[128,10,256]{2,1,0:T(8,128)(2,1)}, u32[]{:S(2)}, u32[]{:S(2)}) async-start(bf16[128,10,256]{2,1,0:T(8,128)(2,1)} %copy.196), calls=%async_computation.5 | async-start | bytes 2097152 | tf_op jit(solution)/shard_map/all_to_all | solution.py:22
  160.6 2.5 %convolution_convert_fusion.4 = bf16[10,2,128,128]{3,2,1,0:T(8,128)(2,1)} fusion(bf16[2,10,128,128]{3,2,0,1:T(8,128)(2,1)S(1)} %reshape_squeeze.29, bf16[1,10,128,128]{2,3,1,0:T(8,128)(2,1)} %get-tuple-element.33, bf16[1,10,128,128]{2,3,1,0:T(8,128)(2,1)} %get-tuple-element.32), kind=kOutput, calls=%fused_computation.14 | convolution fusion | flops 84541440 | bytes 1966080 | tf_op jit(solution)/shard_map/grot,grpo->prgt/dot_general | solution.py:58
  163.1 2.7 %copy.180 = bf16[128,10,256]{2,1,0:T(8,128)(2,1)} copy(bf16[128,10,256]{0,2,1:T(8,128)(2,1)} %bitcast.248) | data formatting | bytes 1310720 | tf_op jit(solution)/shard_map/reshape | solution.py:61
  165.8 2.7 %pad_maximum_fusion.2 = bf16[128,10,384]{2,1,0:T(8,128)(2,1)} fusion(bf16[128,10,256]{2,1,0:T(8,128)(2,1)} %copy.180, bf16[128,10,128]{2,1,0:T(8,128)(2,1)S(1)} %copy-done.7), kind=kLoop, calls=%fused_computation.5 | loop fusion | flops 1966080 | bytes 1966080 | tf_op jit(solution)/shard_map/concatenate | solution.py:132
  168.5 5.4 %all-to-all-done.5 = bf16[128,10,256]{2,1,0:T(8,128)(2,1)} async-done(((bf16[128,10,256]{2,1,0:T(8,128)(2,1)}), bf16[128,10,256]{2,1,0:T(8,128)(2,1)}, u32[]{:S(2)}, u32[]{:S(2)}) %all-to-all-start.5) | async-done | bytes 655392 | tf_op jit(solution)/shard_map/all_to_all | solution.py:22
  173.9 4.6 %all-to-all-start.4 = ((bf16[128,10,384]{2,1,0:T(8,128)(2,1)}), bf16[128,10,384]{2,1,0:T(8,128)(2,1)}, u32[]{:S(2)}, u32[]{:S(2)}) async-start(bf16[128,10,384]{2,1,0:T(8,128)(2,1)} %pad_maximum_fusion.2), calls=%async_computation.4 | async-start | bytes 3145728 | tf_op jit(solution)/shard_map/all_to_all | solution.py:22
  192.0 8.6 %all-to-all-done.4 = bf16[128,10,384]{2,1,0:T(8,128)(2,1)} async-done(((bf16[128,10,384]{2,1,0:T(8,128)(2,1)}), bf16[128,10,384]{2,1,0:T(8,128)(2,1)}, u32[]{:S(2)}, u32[]{:S(2)}) %all-to-all-start.4) | async-done | bytes 983072 | tf_op jit(solution)/shard_map/all_to_all | solution.py:22
  (144 shorter events, 66.8 us)
Async XLA Ops:
  0.6 3.9 %copy-start.29 = (bf16[1,320,128]{2,1,0:T(8,128)(2,1)S(1)}, bf16[1,320,128]{2,1,0:T(8,128)(2,1)}, u32[]{:S(2)}) copy-start(bf16[1,320,128]{2,1,0:T(8,128)(2,1)} %param.12) | copy-start | bytes 245764
  0.6 4.2 %copy-start.16 = (bf16[1,320,128]{2,1,0:T(8,128)(2,1)S(1)}, bf16[1,320,128]{2,1,0:T(8,128)(2,1)}, u32[]{:S(2)}) copy-start(bf16[1,320,128]{2,1,0:T(8,128)(2,1)} %param.9) | copy-start | bytes 245764
  1.6 67.6 %copy-start.18 = (bf16[1,1,320,128]{3,2,1,0:T(8,128)(2,1)}, bf16[1,1,320,128]{3,2,1,0:T(8,128)(2,1)S(1)}, u32[]{:S(2)}) copy-start(bf16[1,1,320,128]{3,2,1,0:T(8,128)(2,1)S(1)} %get-tuple-element.37) | copy-start | bytes 245764
  12.6 7.2 %copy-start.15 = (bf16[1,10,16384]{2,1,0:T(8,128)(2,1)S(1)}, bf16[1,10,16384]{2,1,0:T(8,128)(2,1)}, u32[]{:S(2)}) copy-start(bf16[1,10,16384]{2,1,0:T(8,128)(2,1)} %param.16) | copy-start | bytes 983044
  12.6 32.6 %all-to-all-start = ((bf16[160,8,640]{2,1,0:T(8,128)(2,1)}), bf16[160,8,640]{2,1,0:T(8,128)(2,1)}, u32[]{:S(2)}, u32[]{:S(2)}) async-start(bf16[160,8,640]{2,1,0:T(8,128)(2,1)} %pad_maximum_fusion), calls=%async_computation | async-start | bytes 3276800 | tf_op jit(solution)/shard_map/all_to_all | solution.py:22
  20.9 33.5 %copy-start.3 = (bf16[2,8,128,128]{3,2,1,0:T(8,128)(2,1)}, bf16[2,8,128,128]{3,2,1,0:T(8,128)(2,1)S(1)}, u32[]{:S(2)}) copy-start(bf16[2,8,128,128]{3,2,1,0:T(8,128)(2,1)S(1)} %copy.229) | copy-start | bytes 1572868
  51.8 2.6 %copy-start.1 = (bf16[10,128,256]{1,2,0:T(8,128)(2,1)}, bf16[10,128,256]{1,2,0:T(8,128)(2,1)S(1)}, u32[]{:S(2)}) copy-start(bf16[10,128,256]{1,2,0:T(8,128)(2,1)S(1)} %fusion.3) | copy-start | bytes 1966084
  64.8 26.7 %all-to-all-start.1 = ((bf16[128,10,384]{2,1,0:T(8,128)(2,1)}), bf16[128,10,384]{2,1,0:T(8,128)(2,1)}, u32[]{:S(2)}, u32[]{:S(2)}) async-start(bf16[128,10,384]{2,1,0:T(8,128)(2,1)} %pad_maximum_fusion.1), calls=%async_computation.1 | async-start | bytes 3145728 | tf_op jit(solution)/shard_map/all_to_all | solution.py:22
  91.5 20.1 %all-to-all-start.3 = ((bf16[160,8,256]{2,1,0:T(8,128)(2,1)}), bf16[160,8,256]{2,1,0:T(8,128)(2,1)}, u32[]{:S(2)}, u32[]{:S(2)}) async-start(bf16[160,8,256]{2,1,0:T(8,128)(2,1)} %bitcast.226), calls=%async_computation.3 | async-start | bytes 1310720 | tf_op jit(solution)/shard_map/all_to_all | solution.py:22
  101.1 5.4 %copy-start.5 = (bf16[8,160,2,128]{3,2,0,1:T(2,128)(2,1)}, bf16[8,160,2,128]{3,2,0,1:T(2,128)(2,1)S(1)}, u32[]{:S(2)}) copy-start(bf16[8,160,2,128]{3,2,0,1:T(2,128)(2,1)S(1)} %reshape.91) | copy-start | bytes 1966084
  101.1 5.1 %copy-start.28 = (bf16[320,128]{1,0:T(8,128)(2,1)S(1)}, bf16[320,128]{1,0:T(8,128)(2,1)}, u32[]{:S(2)}) copy-start(bf16[320,128]{1,0:T(8,128)(2,1)} %param.13) | copy-start | bytes 245764
  101.4 8.1 %copy-start.17 = (bf16[320,128]{1,0:T(8,128)(2,1)S(1)}, bf16[320,128]{1,0:T(8,128)(2,1)}, u32[]{:S(2)}) copy-start(bf16[320,128]{1,0:T(8,128)(2,1)} %param.10) | copy-start | bytes 245764
  101.4 4.8 %collective-permute-start.1 = (bf16[8,40,128]{2,1,0:T(8,128)(2,1)S(1)}, bf16[8,40,128]{2,1,0:T(8,128)(2,1)S(1)}, u32[]{:S(2)}, u32[]{:S(2)}) collective-permute-start(bf16[8,40,128]{2,1,0:T(8,128)(2,1)S(1)} %fusion.39), channel_id=1, source_target_pairs={{16,0},{32,16},{48,32},{64,48},{80,64},{96,80},{112,96},{128,112},... | collective-permute-start | bytes 245768 | tf_op jit(solution)/shard_map/ppermute | solution.py:18
  103.8 5.8 %collective-permute-start = (bf16[8,40,128]{2,1,0:T(8,128)(2,1)S(1)}, bf16[8,40,128]{2,1,0:T(8,128)(2,1)S(1)}, u32[]{:S(2)}, u32[]{:S(2)}) collective-permute-start(bf16[8,40,128]{2,1,0:T(8,128)(2,1)S(1)} %fusion.40), channel_id=1, source_target_pairs={{0,16},{16,32},{32,48},{48,64},{64,80},{80,96},{96,112},{112,128},... | collective-permute-start | bytes 245768 | tf_op jit(solution)/shard_map/ppermute | solution.py:18
  106.3 3.3 %copy-start.25 = (bf16[8,40,128]{2,1,0:T(8,128)(2,1)}, bf16[8,40,128]{2,1,0:T(8,128)(2,1)S(1)}, u32[]{:S(2)}) copy-start(bf16[8,40,128]{2,1,0:T(8,128)(2,1)S(1)} %broadcast_select_fusion) | copy-start | bytes 245764
  111.6 26.3 %all-to-all-start.2 = ((bf16[160,8,384]{2,1,0:T(8,128)(2,1)}), bf16[160,8,384]{2,1,0:T(8,128)(2,1)}, u32[]{:S(2)}, u32[]{:S(2)}) async-start(bf16[160,8,384]{2,1,0:T(8,128)(2,1)} %pad_maximum_fusion.3), calls=%async_computation.2 | async-start | bytes 1966080 | tf_op jit(solution)/shard_map/all_to_all | solution.py:22
  137.8 2.4 %copy-start.10 = (f32[2,10,128,128]{2,3,1,0:T(8,128)S(1)}, f32[2,10,128,128]{2,3,1,0:T(8,128)}, u32[]{:S(2)}) copy-start(f32[2,10,128,128]{2,3,1,0:T(8,128)} %convolution_bitcast_fusion.1) | copy-start | bytes 3932164
  145.6 2.6 %copy-start.8 = (bf16[128,10,128]{0,2,1:T(8,128)(2,1)S(1)}, bf16[128,10,128]{0,2,1:T(8,128)(2,1)}, u32[]{:S(2)}) copy-start(bf16[128,10,128]{0,2,1:T(8,128)(2,1)} %get-tuple-element.35) | copy-start | bytes 983044
  145.6 2.6 %copy-start.11 = (bf16[128,10,128]{0,2,1:T(8,128)(2,1)S(1)}, bf16[128,10,128]{0,2,1:T(8,128)(2,1)}, u32[]{:S(2)}) copy-start(bf16[128,10,128]{0,2,1:T(8,128)(2,1)} %fusion.30) | copy-start | bytes 983044
  151.7 22.1 %all-to-all-start.5 = ((bf16[128,10,256]{2,1,0:T(8,128)(2,1)}), bf16[128,10,256]{2,1,0:T(8,128)(2,1)}, u32[]{:S(2)}, u32[]{:S(2)}) async-start(bf16[128,10,256]{2,1,0:T(8,128)(2,1)} %copy.196), calls=%async_computation.5 | async-start | bytes 2097152 | tf_op jit(solution)/shard_map/all_to_all | solution.py:22
  163.1 2.7 %copy-start.7 = (bf16[128,10,128]{2,1,0:T(8,128)(2,1)S(1)}, bf16[128,10,128]{2,1,0:T(8,128)(2,1)}, u32[]{:S(2)}) copy-start(bf16[128,10,128]{2,1,0:T(8,128)(2,1)} %copy.179) | copy-start | bytes 983044
  173.9 26.8 %all-to-all-start.4 = ((bf16[128,10,384]{2,1,0:T(8,128)(2,1)}), bf16[128,10,384]{2,1,0:T(8,128)(2,1)}, u32[]{:S(2)}, u32[]{:S(2)}) async-start(bf16[128,10,384]{2,1,0:T(8,128)(2,1)} %pad_maximum_fusion.2), calls=%async_computation.4 | async-start | bytes 3145728 | tf_op jit(solution)/shard_map/all_to_all | solution.py:22
  187.9 2.5 %copy-start.26 = (bf16[8,40,128]{2,1,0:T(8,128)(2,1)S(1)}, bf16[8,40,128]{2,1,0:T(8,128)(2,1)}, u32[]{:S(2)}) copy-start(bf16[8,40,128]{2,1,0:T(8,128)(2,1)} %copy-done.25) | copy-start | bytes 245764
  187.9 2.5 %copy-start.30 = (bf16[1,320,128]{2,1,0:T(8,128)(2,1)S(1)}, bf16[1,320,128]{2,1,0:T(8,128)(2,1)}, u32[]{:S(2)}) copy-start(bf16[1,320,128]{2,1,0:T(8,128)(2,1)} %param.12) | copy-start | bytes 245764
  (20 other events, 34.1 us)

commit v3 on v1

--- a/solution.py
+++ b/solution.py
@@ -23,7 +23,12 @@
 
 
 def to_features(pieces):
-    return lax.all_to_all(pieces, "blk", split_axis=1, concat_axis=0, tiled=True)
+    groups = lax.axis_size("blk")
+    r_local, p_all, n = pieces.shape
+    p_local = p_all // groups
+    grouped = pieces.reshape(r_local, groups, p_local, n).transpose(1, 0, 2, 3)
+    arrived = lax.all_to_all(grouped, "blk", split_axis=0, concat_axis=0, tiled=True)
+    return arrived.reshape(groups * r_local, p_local, n)
 
 
 def spread_of(values, up_first):

time: 190 us -> 184 us (0.968)
  waiting for transfers between devices: 80.6 us -> 62.8 us
  local copies, waits for them, and re-layouts: 45.8 us -> 53.3 us
  matrix products: 19.3 us -> 21.6 us
    all_to_all x2, waiting for transfers between devices: 46.2 us -> 28.4 us  [to_features(): lax.all_to_all(grouped, 'blk', split_axis=0, concat_axis=0, tiled=True)]
    convert_element_type x1 -> x2, local copies, waits for them, and re-layouts: 0.43 us -> 5.9 us  [backward_middle(): grad_spread = jnp.einsum('grot,grpo->rpgt', grad_mixed, up_second, prefer...]
    concatenate x0 -> x1, local copies, waits for them, and re-layouts: none -> 2.86 us  [shards(): jnp.concatenate([lowered_b, gspread_2.reshape(hidden_blocks, FIRST_BLOCKS...]
    slice x2, local copies, waits for them, and re-layouts: 0.37 us -> 3.21 us  [shards(): spread_br = arrived[:, :, :2 * t].reshape(FIRST_BLOCKS, hidden_blocks, 2, t)]
    concatenate x1, local copies, waits for them, and re-layouts: 5.41 us -> 2.86 us  [shards(): jnp.concatenate([lowered_a, gspread_1.reshape(hidden_blocks, FIRST_BLOCKS...]
    all_to_all x2 -> x0, local copies, waits for them, and re-layouts: 2.03 us -> none  [to_features(): lax.all_to_all(pieces, 'blk', split_axis=1, concat_axis=0, tiled=True)]
    reshape x1 -> x0, local copies, waits for them, and re-layouts: 1.96 us -> none  [shards(): gspread_2.reshape(hidden_blocks, FIRST_BLOCKS, 2 * t)]
    unnamed x66 -> x72, local copies, waits for them, and re-layouts: 9.14 us -> 10.3 us
  transfers between devices with their start and end apart: 5 -> 5, of which waited for: 4 -> 4; matrix products, arithmetic and copies ran while one was open for 10% -> 8% of each run, Pallas kernels for 0% -> 0%
where the time goes in v3:
time: 184 us; the launch traced here: 183 us
  waiting for transfers between devices  62.8 us (34%)
  local copies, waits for them, and re-layouts  53.3 us (29%)
  matrix products  21.6 us (12%)
  blocking collectives  20.5 us (11%)
  starting transfers between devices  20.4 us (11%)
  other arithmetic  3.36 us (2%)
    all_to_all x1, waiting for transfers between devices, to_blocks(): lax.all_to_all(pieces, 'blk', split_axis=1, concat_axis=0, tiled=True)  31.3 us
    all_to_all x2, waiting for transfers between devices, to_features(): lax.all_to_all(grouped, 'blk', split_axis=0, concat_axis=0, tiled=True)  28.4 us
    all_to_all x1, blocking collectives, to_blocks(): lax.all_to_all(pieces, 'blk', split_axis=1, concat_axis=0, tiled=True)  20.5 us
    unnamed x72, local copies, waits for them, and re-layouts  10.3 us
    all_to_all x2, starting transfers between devices, to_features(): lax.all_to_all(grouped, 'blk', split_axis=0, concat_axis=0, tiled=True)  8.86 us
    all_to_all x1, starting transfers between devices, to_blocks(): lax.all_to_all(pieces, 'blk', split_axis=1, concat_axis=0, tiled=True)  7.16 us
    convert_element_type x2, local copies, waits for them, and re-layouts, backward_middle(): grad_spread = jnp.einsum('grot,grpo->rpgt', grad_mixed, up_second, prefer...  5.9 us
    slice x2, local copies, waits for them, and re-layouts, shards(): arrived[:, :, :6 * t].reshape(FIRST_BLOCKS, hidden_blocks, 2, 3 * t)  5.45 us
  transfers between devices with their start and end apart: 5, of which 4 were waited for; matrix products, arithmetic and copies ran while one was open for 8% of the time, Pallas kernels for 0%

profile of v3, /device:TPU:224, one launch (start us, length us, event | category | flops | bytes accessed | tf_op | source)
XLA Modules:
  0.0 183.0 jit_solution(17558690886890364551)
XLA Ops:
  7.5 2.1 %copy.137 = bf16[8,160,896]{2,0,1:T(8,128)(2,1)} copy(bf16[8,160,896]{2,1,0:T(8,128)(2,1)S(1)} %pad_maximum_fusion) | data formatting | bytes 4587520 | tf_op jit(solution)/shard_map/concatenate | solution.py:114
  9.6 7.2 %all-to-all-start = ((bf16[8,160,896]{2,0,1:T(8,128)(2,1)}), bf16[8,160,896]{2,0,1:T(8,128)(2,1)S(1)}, u32[]{:S(2)}, u32[]{:S(2)}) async-start(bf16[8,160,896]{2,0,1:T(8,128)(2,1)} %copy.137), calls=%async_computation | async-start | bytes 4587520 | tf_op jit(solution)/shard_map/all_to_all | solution.py:22
  17.7 2.3 %reshape_squeeze.30 = bf16[2,10,128,128]{3,2,0,1:T(8,128)(2,1)S(1)} reshape(bf16[1,2,10,16384]{3,1,2,0:T(2,128)(2,1)} %param.15) | data formatting | bytes 1310720 | tf_op jit(solution)/shard_map/reshape;squeeze | solution.py:99
  20.0 31.3 %all-to-all-done = bf16[8,160,896]{2,0,1:T(8,128)(2,1)S(1)} async-done(((bf16[8,160,896]{2,0,1:T(8,128)(2,1)}), bf16[8,160,896]{2,0,1:T(8,128)(2,1)S(1)}, u32[]{:S(2)}, u32[]{:S(2)}) %all-to-all-start) | async-done | bytes 2293792 | tf_op jit(solution)/shard_map/all_to_all | solution.py:22
  52.7 2.0 %copy.249 = bf16[16,8,10,896]{3,1,0,2:T(8,128)(2,1)S(1)} copy(bf16[16,8,10,896]{3,1,2,0:T(8,128)(2,1)} %bitcast.207) | data formatting | bytes 4587520 | tf_op jit(solution)/shard_map/all_to_all | solution.py:22
  56.2 4.0 %copy.139 = bf16[128,10,768]{0,2,1:T(8,128)(2,1)} copy(bf16[128,10,768]{2,0,1:T(8,128)(2,1)} %slice.97) | data formatting | bytes 3932160 | tf_op jit(solution)/shard_map/slice | solution.py:118
  60.2 2.2 %convolution_bitcast_fusion = f32[2,10,128,384]{2,3,1,0:T(8,128)S(1)} fusion(bf16[128,10,2,384]{0,3,2,1:T(8,128)(2,1)} %bitcast.208, bf16[2,10,128,128]{3,2,0,1:T(8,128)(2,1)S(1)} %reshape_squeeze.30), kind=kOutput, calls=%fused_computation.2 | convolution fusion | flops 251658240 | bytes 6553600 | tf_op jit(solution)/shard_map/prgt,grpo->grot/dot_general | solution.py:47
  67.4 3.0 %copy.146 = bf16[10,128,2,128]{3,2,1,0:T(2,128)(2,1)} copy(bf16[10,128,2,128]{1,3,2,0:T(8,128)(2,1)} %fusion.17) | data formatting | bytes 1310720 | tf_op jit(solution)/shard_map/convert_element_type | solution.py:68
  70.3 2.9 %concatenate.43 = bf16[10,16,8,256]{3,2,1,0:T(8,128)(2,1)} reshape(bf16[10,128,2,128]{3,2,1,0:T(2,128)(2,1)} %copy.146) | data formatting | bytes 1310720 | tf_op jit(solution)/shard_map/concatenate | solution.py:122
  73.2 1.9 %fusion.4 = bf16[10,16,8,384]{3,2,1,0:T(8,128)(2,1)S(1)} fusion(bf16[10,128,384]{1,2,0:T(8,128)(2,1)} %fusion.1, bf16[16,128,128]{2,1,0:T(8,128)(2,1)} %bitcast.217), kind=kOutput, calls=%fused_computation.15 | convolution fusion | flops 126320640 | bytes 2293760 | tf_op jit(solution)/shard_map/rot,rop->rpt/dot_general | solution.py:51
  76.5 4.4 %all-to-all-start.1 = ((bf16[16,10,8,640]{3,2,1,0:T(8,128)(2,1)}), bf16[16,10,8,640]{3,2,1,0:T(8,128)(2,1)}, u32[]{:S(2)}, u32[]{:S(2)}) async-start(bf16[16,10,8,640]{3,2,1,0:T(8,128)(2,1)} %copy_bitcast_fusion.1), calls=%async_computation.1 | async-start | bytes 3276800 | tf_op jit(solution)/shard_map/all_to_all | solution.py:30
  81.0 23.7 %all-to-all-done.1 = bf16[16,10,8,640]{3,2,1,0:T(8,128)(2,1)} async-done(((bf16[16,10,8,640]{3,2,1,0:T(8,128)(2,1)}), bf16[16,10,8,640]{3,2,1,0:T(8,128)(2,1)}, u32[]{:S(2)}, u32[]{:S(2)}) %all-to-all-start.1) | async-done | bytes 1638432 | tf_op jit(solution)/shard_map/all_to_all | solution.py:30
  105.7 2.3 %fusion.94 = (bf16[160,8,256]{2,1,0:T(8,128)(2,1)}, bf16[160,8,2,128]{3,1,2,0:T(8,128)(2,1)S(1)}) fusion(bf16[160,8,640]{2,1,0:T(8,128)(2,1)} %bitcast.24), kind=kLoop, calls=%fused_computation.132 | loop fusion | bytes 2621440 | tf_op jit(solution)/shard_map/slice | solution.py:171
  109.4 1.9 %collective-permute-start.1 = (bf16[8,40,128]{2,1,0:T(8,128)(2,1)S(1)}, bf16[8,40,128]{2,1,0:T(8,128)(2,1)S(1)}, u32[]{:S(2)}, u32[]{:S(2)}) collective-permute-start(bf16[8,40,128]{2,1,0:T(8,128)(2,1)S(1)} %fusion.35), channel_id=1, source_target_pairs={{16,0},{32,16},{48,32},{64,48},{80,64},{96,80},{112,96},{128,112},... | collective-permute-start | bytes 245768 | tf_op jit(solution)/shard_map/ppermute | solution.py:18
  111.6 2.4 %collective-permute-start = (bf16[8,40,128]{2,1,0:T(8,128)(2,1)S(1)}, bf16[8,40,128]{2,1,0:T(8,128)(2,1)S(1)}, u32[]{:S(2)}, u32[]{:S(2)}) collective-permute-start(bf16[8,40,128]{2,1,0:T(8,128)(2,1)S(1)} %fusion.36), channel_id=1, source_target_pairs={{0,16},{16,32},{32,48},{48,64},{64,80},{80,96},{96,112},{112,128},... | collective-permute-start | bytes 245768 | tf_op jit(solution)/shard_map/ppermute | solution.py:18
  114.3 3.1 %collective-permute-done = bf16[8,40,128]{2,1,0:T(8,128)(2,1)S(1)} collective-permute-done((bf16[8,40,128]{2,1,0:T(8,128)(2,1)S(1)}, bf16[8,40,128]{2,1,0:T(8,128)(2,1)S(1)}, u32[]{:S(2)}, u32[]{:S(2)}) %collective-permute-start) | collective-permute-done | bytes 81952 | tf_op jit(solution)/shard_map/ppermute | solution.py:18
  118.5 20.5 %all_to_all.46 = bf16[8,160,384]{2,0,1:T(8,128)(2,1)S(1)} all-to-all(bf16[8,160,384]{2,0,1:T(8,128)(2,1)S(1)} %copy.156), channel_id=1, replica_groups=mesh['section'=32,'blk'=16] {'blk'}, dimensions={1} | all-to-all | bytes 1966080 | tf_op jit(solution)/shard_map/all_to_all | solution.py:22
  139.1 2.2 %fusion.61 = (bf16[1,10,128,128]{2,3,1,0:T(8,128)(2,1)S(1)}, bf16[1,10,128,128]{2,3,1,0:T(8,128)(2,1)S(1)}) fusion(f32[2,10,128,384]{2,3,1,0:T(8,128)} %copy-done, bf16[16,128,128]{2,1,0:T(8,128)(2,1)S(1)} %bitcast.219, bf16[128,10,384]{2,0,1:T(8,128)(2,1)S(1)} %bitcast.211), kind=kOutput, calls=%fused_computation.97 | convolution fusion | flops 44072960 | bytes 2621440 | tf_op jit(solution)/shard_map/prt,rop->rot/dot_general | solution.py:58
  143.8 2.9 %copy.165 = bf16[10,128,2,128]{3,2,1,0:T(2,128)(2,1)} copy(bf16[10,128,2,128]{1,3,2,0:T(8,128)(2,1)} %fusion.18) | data formatting | bytes 1310720 | tf_op jit(solution)/shard_map/convert_element_type | solution.py:68
  146.7 2.9 %concatenate.47 = bf16[10,16,8,256]{3,2,1,0:T(8,128)(2,1)} reshape(bf16[10,128,2,128]{3,2,1,0:T(2,128)(2,1)} %copy.165) | data formatting | bytes 1310720 | tf_op jit(solution)/shard_map/concatenate | solution.py:156
  149.6 2.2 %copy.158 = bf16[128,10,256]{0,2,1:T(8,128)(2,1)} copy(bf16[128,10,256]{2,0,1:T(8,128)(2,1)} %slice.105) | data formatting | bytes 1310720 | tf_op jit(solution)/shard_map/slice | solution.py:150
  155.7 4.4 %all-to-all-start.3 = ((bf16[16,10,8,384]{3,2,1,0:T(8,128)(2,1)}), bf16[16,10,8,384]{3,2,1,0:T(8,128)(2,1)}, u32[]{:S(2)}, u32[]{:S(2)}) async-start(bf16[16,10,8,384]{3,2,1,0:T(8,128)(2,1)} %copy.166), calls=%async_computation.3 | async-start | bytes 1966080 | tf_op jit(solution)/shard_map/all_to_all | solution.py:30
  160.9 1.9 %copy.198 = bf16[128,10,128]{0,2,1:T(8,128)(2,1)} copy(bf16[128,10,128]{2,0,1:T(8,128)(2,1)} %slice.100) | data formatting | bytes 655360
  172.2 4.7 %all-to-all-done.3 = bf16[16,10,8,384]{3,2,1,0:T(8,128)(2,1)} async-done(((bf16[16,10,8,384]{3,2,1,0:T(8,128)(2,1)}), bf16[16,10,8,384]{3,2,1,0:T(8,128)(2,1)}, u32[]{:S(2)}, u32[]{:S(2)}) %all-to-all-start.3) | async-done | bytes 983072 | tf_op jit(solution)/shard_map/all_to_all | solution.py:30
  (116 shorter events, 43.5 us)
Async XLA Ops:
  9.6 7.2 %copy-start.16 = (bf16[1,10,16384]{2,1,0:T(8,128)(2,1)S(1)}, bf16[1,10,16384]{2,1,0:T(8,128)(2,1)}, u32[]{:S(2)}) copy-start(bf16[1,10,16384]{2,1,0:T(8,128)(2,1)} %param.16) | copy-start | bytes 983044
  9.6 41.7 %all-to-all-start = ((bf16[8,160,896]{2,0,1:T(8,128)(2,1)}), bf16[8,160,896]{2,0,1:T(8,128)(2,1)S(1)}, u32[]{:S(2)}, u32[]{:S(2)}) async-start(bf16[8,160,896]{2,0,1:T(8,128)(2,1)} %copy.137), calls=%async_computation | async-start | bytes 4587520 | tf_op jit(solution)/shard_map/all_to_all | solution.py:22
  62.4 2.2 %copy-start = (f32[2,10,128,384]{2,3,1,0:T(8,128)}, f32[2,10,128,384]{2,3,1,0:T(8,128)S(1)}, u32[]{:S(2)}) copy-start(f32[2,10,128,384]{2,3,1,0:T(8,128)S(1)} %convolution_bitcast_fusion) | copy-start | bytes 11796484
  62.4 2.2 %copy-start.12 = (bf16[2,8,128,128]{3,2,1,0:T(8,128)(2,1)S(1)}, bf16[2,8,128,128]{3,2,1,0:T(8,128)(2,1)}, u32[]{:S(2)}) copy-start(bf16[2,8,128,128]{3,2,1,0:T(8,128)(2,1)} %copy.206) | copy-start | bytes 1572868
  76.5 28.1 %all-to-all-start.1 = ((bf16[16,10,8,640]{3,2,1,0:T(8,128)(2,1)}), bf16[16,10,8,640]{3,2,1,0:T(8,128)(2,1)}, u32[]{:S(2)}, u32[]{:S(2)}) async-start(bf16[16,10,8,640]{3,2,1,0:T(8,128)(2,1)} %copy_bitcast_fusion.1), calls=%async_computation.1 | async-start | bytes 3276800 | tf_op jit(solution)/shard_map/all_to_all | solution.py:30
  104.7 3.4 %copy-start.6 = (bf16[2,8,40,160]{3,2,1,0:T(8,128)(2,1)S(1)}, bf16[2,8,40,160]{3,2,1,0:T(8,128)(2,1)}, u32[]{:S(2)}) copy-start(bf16[2,8,40,160]{3,2,1,0:T(8,128)(2,1)} %copy-done.5) | copy-start | bytes 614404
  105.7 5.6 %copy-start.17 = (bf16[1,320,128]{2,1,0:T(8,128)(2,1)S(1)}, bf16[1,320,128]{2,1,0:T(8,128)(2,1)}, u32[]{:S(2)}) copy-start(bf16[1,320,128]{2,1,0:T(8,128)(2,1)} %param.9) | copy-start | bytes 245764
  105.7 8.3 %copy-start.25 = (bf16[320,128]{1,0:T(8,128)(2,1)S(1)}, bf16[320,128]{1,0:T(8,128)(2,1)}, u32[]{:S(2)}) copy-start(bf16[320,128]{1,0:T(8,128)(2,1)} %param.13) | copy-start | bytes 245764
  108.0 9.8 %copy-start.8 = (bf16[160,8,2,128]{3,1,2,0:T(8,128)(2,1)}, bf16[160,8,2,128]{3,1,2,0:T(8,128)(2,1)S(1)}, u32[]{:S(2)}) copy-start(bf16[160,8,2,128]{3,1,2,0:T(8,128)(2,1)S(1)} %get-tuple-element.35) | copy-start | bytes 1966084
  108.0 9.4 %copy-start.18 = (bf16[320,128]{1,0:T(8,128)(2,1)S(1)}, bf16[320,128]{1,0:T(8,128)(2,1)}, u32[]{:S(2)}) copy-start(bf16[320,128]{1,0:T(8,128)(2,1)} %param.10) | copy-start | bytes 245764
  109.4 4.6 %collective-permute-start.1 = (bf16[8,40,128]{2,1,0:T(8,128)(2,1)S(1)}, bf16[8,40,128]{2,1,0:T(8,128)(2,1)S(1)}, u32[]{:S(2)}, u32[]{:S(2)}) collective-permute-start(bf16[8,40,128]{2,1,0:T(8,128)(2,1)S(1)} %fusion.35), channel_id=1, source_target_pairs={{16,0},{32,16},{48,32},{64,48},{80,64},{96,80},{112,96},{128,112},... | collective-permute-start | bytes 245768 | tf_op jit(solution)/shard_map/ppermute | solution.py:18
  111.6 5.8 %collective-permute-start = (bf16[8,40,128]{2,1,0:T(8,128)(2,1)S(1)}, bf16[8,40,128]{2,1,0:T(8,128)(2,1)S(1)}, u32[]{:S(2)}, u32[]{:S(2)}) collective-permute-start(bf16[8,40,128]{2,1,0:T(8,128)(2,1)S(1)} %fusion.36), channel_id=1, source_target_pairs={{0,16},{16,32},{32,48},{48,64},{64,80},{80,96},{96,112},{112,128},... | collective-permute-start | bytes 245768 | tf_op jit(solution)/shard_map/ppermute | solution.py:18
  114.1 3.3 %copy-start.22 = (bf16[8,40,128]{2,1,0:T(8,128)(2,1)}, bf16[8,40,128]{2,1,0:T(8,128)(2,1)S(1)}, u32[]{:S(2)}) copy-start(bf16[8,40,128]{2,1,0:T(8,128)(2,1)S(1)} %broadcast_select_fusion) | copy-start | bytes 245764
  118.5 20.6 %copy-start.13 = (bf16[2,8,128,128]{3,2,1,0:T(8,128)(2,1)S(1)}, bf16[2,8,128,128]{3,2,1,0:T(8,128)(2,1)}, u32[]{:S(2)}) copy-start(bf16[2,8,128,128]{3,2,1,0:T(8,128)(2,1)} %copy.206) | copy-start | bytes 1572868
  139.1 2.2 %copy-start.4 = (bf16[16,8,10,384]{3,1,0,2:T(8,128)(2,1)}, bf16[16,8,10,384]{3,1,0,2:T(8,128)(2,1)S(1)}, u32[]{:S(2)}) copy-start(bf16[16,8,10,384]{3,1,0,2:T(8,128)(2,1)S(1)} %copy.250) | copy-start | bytes 2949124
  155.7 7.2 %copy-start.9 = (bf16[160,8,2,128]{3,1,2,0:T(8,128)(2,1)S(1)}, bf16[160,8,2,128]{3,1,2,0:T(8,128)(2,1)}, u32[]{:S(2)}) copy-start(bf16[160,8,2,128]{3,1,2,0:T(8,128)(2,1)} %copy-done.8) | copy-start | bytes 1966084
  155.7 21.2 %all-to-all-start.3 = ((bf16[16,10,8,384]{3,2,1,0:T(8,128)(2,1)}), bf16[16,10,8,384]{3,2,1,0:T(8,128)(2,1)}, u32[]{:S(2)}, u32[]{:S(2)}) async-start(bf16[16,10,8,384]{3,2,1,0:T(8,128)(2,1)} %copy.166), calls=%async_computation.3 | async-start | bytes 1966080 | tf_op jit(solution)/shard_map/all_to_all | solution.py:30
  160.9 2.9 %copy-start.23 = (bf16[8,40,128]{2,1,0:T(8,128)(2,1)S(1)}, bf16[8,40,128]{2,1,0:T(8,128)(2,1)}, u32[]{:S(2)}) copy-start(bf16[8,40,128]{2,1,0:T(8,128)(2,1)} %copy-done.22) | copy-start | bytes 245764
  160.9 2.9 %copy-start.27 = (bf16[1,320,128]{2,1,0:T(8,128)(2,1)S(1)}, bf16[1,320,128]{2,1,0:T(8,128)(2,1)}, u32[]{:S(2)}) copy-start(bf16[1,320,128]{2,1,0:T(8,128)(2,1)} %param.12) | copy-start | bytes 245764
  162.8 4.7 %copy-start.2 = (bf16[128,10,768]{0,2,1:T(8,128)(2,1)S(1)}, bf16[128,10,768]{0,2,1:T(8,128)(2,1)}, u32[]{:S(2)}) copy-start(bf16[128,10,768]{0,2,1:T(8,128)(2,1)} %copy.139) | copy-start | bytes 5898244
  163.8 3.8 %copy-start.29 = (bf16[1,10,128,128]{2,3,1,0:T(8,128)(2,1)S(1)}, bf16[1,10,128,128]{2,3,1,0:T(8,128)(2,1)}, u32[]{:S(2)}) copy-start(bf16[1,10,128,128]{2,3,1,0:T(8,128)(2,1)} %copy-done.28) | copy-start | bytes 983044
  170.9 8.3 %copy-start.7 = (bf16[2,8,40,160]{3,2,1,0:T(8,128)(2,1)S(1)}, bf16[2,8,40,160]{3,2,1,0:T(8,128)(2,1)}, u32[]{:S(2)}) copy-start(bf16[2,8,40,160]{3,2,1,0:T(8,128)(2,1)} %copy-done.5) | copy-start | bytes 614404
  170.9 8.3 %copy-start.24 = (bf16[8,40,128]{2,1,0:T(8,128)(2,1)S(1)}, bf16[8,40,128]{2,1,0:T(8,128)(2,1)}, u32[]{:S(2)}) copy-start(bf16[8,40,128]{2,1,0:T(8,128)(2,1)} %copy-done.22) | copy-start | bytes 245764
  177.9 2.4 %copy-start.15 = (bf16[160,8,2,128]{3,0,2,1:T(8,128)(2,1)S(1)}, bf16[160,8,2,128]{3,0,2,1:T(8,128)(2,1)}, u32[]{:S(2)}) copy-start(bf16[160,8,2,128]{3,0,2,1:T(8,128)(2,1)} %copy.153) | copy-start | bytes 1966084
  (14 other events, 17.2 us)

commit v4 on v3

--- a/solution.py
+++ b/solution.py
@@ -64,7 +64,7 @@
         [grad_hidden * mixed[1] * slope, grad_hidden * mixed[0] * sigmoid_gate]
     ).astype(jnp.bfloat16)
     grad_spread = jnp.einsum(
-        "grot,grpo->rpgt", grad_mixed, up_second, preferred_element_type=jnp.float32
+        "grot,grpo->grpt", grad_mixed, up_second, preferred_element_type=jnp.float32
     ).astype(jnp.bfloat16)
     return grad_mixed, grad_spread
 
@@ -119,9 +119,7 @@
     glow_1r = arrived[:, :, 6 * t :]
     mixed_a, hidden_a, lowered_a = forward_middle(spread_ar, up_second, down_first)
     gmix_1, gspread_1 = backward_middle(mixed_a[:, :, :, t : 2 * t], glow_1r, up_second, down_first)
-    payload = jnp.concatenate(
-        [lowered_a, gspread_1.reshape(hidden_blocks, FIRST_BLOCKS, 2 * t)], axis=2
-    )
+    payload = jnp.concatenate([lowered_a, gspread_1[0], gspread_1[1]], axis=2)
     back = to_features(payload)
     lowered_ap = back[:, :, : 3 * t]
     gspread_1p = back[:, :, 3 * t :].reshape(SECOND_BLOCKS, feature_blocks, 2, t)
@@ -153,9 +151,7 @@
     gmix_2, gspread_2 = backward_middle(
         mixed_a[:, :, :, 2 * t :], glow_2r, up_second, down_first
     )
-    payload = jnp.concatenate(
-        [lowered_b, gspread_2.reshape(hidden_blocks, FIRST_BLOCKS, 2 * t)], axis=2
-    )
+    payload = jnp.concatenate([lowered_b, gspread_2[0], gspread_2[1]], axis=2)
     back = to_features(payload)
     lowered_bp = back[:, :, :t]
     gspread_2p = back[:, :, t:].reshape(SECOND_BLOCKS, feature_blocks, 2, t)

time: 184 us -> 169 us (0.918)
  local copies, waits for them, and re-layouts: 53.3 us -> 41.2 us
  matrix products: 21.6 us -> 18.5 us
    convert_element_type x2 -> x0, local copies, waits for them, and re-layouts: 5.9 us -> none  [backward_middle(): grad_spread = jnp.einsum('grot,grpo->rpgt', grad_mixed, up_second, prefer...]
    concatenate x2, local copies, waits for them, and re-layouts: 5.73 us -> 0.97 us  [the longest x1 0.91 us: shards(): payload = jnp.concatenate([lowered_b, gspread_2[0], gspread_2[1]], axis=2)]
    unnamed x72 -> x74, local copies, waits for them, and re-layouts: 10.3 us -> 10 us
  transfers between devices with their start and end apart: 5 -> 5, of which waited for: 4 -> 4; matrix products, arithmetic and copies ran while one was open for 8% -> 9% of each run, Pallas kernels for 0% -> 0%
where the time goes in v4:
time: 169 us; the launch traced here: 168 us
  waiting for transfers between devices  63 us (37%)
  local copies, waits for them, and re-layouts  41.2 us (24%)
  blocking collectives  20.6 us (12%)
  starting transfers between devices  20.3 us (12%)
  matrix products  18.5 us (11%)
  other arithmetic  3.42 us (2%)
    all_to_all x1, waiting for transfers between devices, to_blocks(): lax.all_to_all(pieces, 'blk', split_axis=1, concat_axis=0, tiled=True)  31.3 us
    all_to_all x2, waiting for transfers between devices, to_features(): lax.all_to_all(grouped, 'blk', split_axis=0, concat_axis=0, tiled=True)  28.6 us
    all_to_all x1, blocking collectives, to_blocks(): lax.all_to_all(pieces, 'blk', split_axis=1, concat_axis=0, tiled=True)  20.6 us
    unnamed x74, local copies, waits for them, and re-layouts  10 us
    all_to_all x2, starting transfers between devices, to_features(): lax.all_to_all(grouped, 'blk', split_axis=0, concat_axis=0, tiled=True)  8.86 us
    all_to_all x1, starting transfers between devices, to_blocks(): lax.all_to_all(pieces, 'blk', split_axis=1, concat_axis=0, tiled=True)  7.16 us
    slice x2, local copies, waits for them, and re-layouts, shards(): arrived[:, :, :6 * t].reshape(FIRST_BLOCKS, hidden_blocks, 2, 3 * t)  5.45 us
    ppermute x2, starting transfers between devices, from_behind(): return lax.ppermute(value, axis, pairs)  4.33 us
  transfers between devices with their start and end apart: 5, of which 4 were waited for; matrix products, arithmetic and copies ran while one was open for 9% of the time, Pallas kernels for 0%

profile of v4, /device:TPU:224, one launch (start us, length us, event | category | flops | bytes accessed | tf_op | source)
XLA Modules:
  0.0 168.3 jit_solution(5044812806253064722)
XLA Ops:
  3.0 1.6 reshape_squeeze.28
  4.5 1.6 convert_bitcast_fusion
  7.5 2.1 %copy.143 = bf16[8,160,896]{2,0,1:T(8,128)(2,1)} copy(bf16[8,160,896]{2,1,0:T(8,128)(2,1)S(1)} %pad_maximum_fusion) | data formatting | bytes 4587520 | tf_op jit(solution)/shard_map/concatenate | solution.py:114
  9.6 7.2 %all-to-all-start = ((bf16[8,160,896]{2,0,1:T(8,128)(2,1)}), bf16[8,160,896]{2,0,1:T(8,128)(2,1)S(1)}, u32[]{:S(2)}, u32[]{:S(2)}) async-start(bf16[8,160,896]{2,0,1:T(8,128)(2,1)} %copy.143), calls=%async_computation | async-start | bytes 4587520 | tf_op jit(solution)/shard_map/all_to_all | solution.py:22
  17.7 2.3 %reshape_squeeze.30 = bf16[2,10,128,128]{3,2,0,1:T(8,128)(2,1)S(1)} reshape(bf16[1,2,10,16384]{3,1,2,0:T(2,128)(2,1)} %param.15) | data formatting | bytes 1310720 | tf_op jit(solution)/shard_map/reshape;squeeze | solution.py:99
  20.0 31.3 %all-to-all-done = bf16[8,160,896]{2,0,1:T(8,128)(2,1)S(1)} async-done(((bf16[8,160,896]{2,0,1:T(8,128)(2,1)}), bf16[8,160,896]{2,0,1:T(8,128)(2,1)S(1)}, u32[]{:S(2)}, u32[]{:S(2)}) %all-to-all-start) | async-done | bytes 2293792 | tf_op jit(solution)/shard_map/all_to_all | solution.py:22
  52.8 2.0 %copy.262 = bf16[16,8,10,896]{3,1,0,2:T(8,128)(2,1)S(1)} copy(bf16[16,8,10,896]{3,1,2,0:T(8,128)(2,1)} %bitcast.213) | data formatting | bytes 4587520 | tf_op jit(solution)/shard_map/all_to_all | solution.py:22
  54.7 1.5 slice.113
  56.2 4.0 %copy.145 = bf16[128,10,768]{0,2,1:T(8,128)(2,1)} copy(bf16[128,10,768]{2,0,1:T(8,128)(2,1)} %slice.113) | data formatting | bytes 3932160 | tf_op jit(solution)/shard_map/slice | solution.py:118
  60.2 2.2 %convolution_bitcast_fusion = f32[2,10,128,384]{2,3,1,0:T(8,128)S(1)} fusion(bf16[128,10,2,384]{0,3,2,1:T(8,128)(2,1)} %bitcast.214, bf16[2,10,128,128]{3,2,0,1:T(8,128)(2,1)S(1)} %reshape_squeeze.30), kind=kOutput, calls=%fused_computation.2 | convolution fusion | flops 251658240 | bytes 6553600 | tf_op jit(solution)/shard_map/prgt,grpo->grot/dot_general | solution.py:47
  67.5 4.4 %all-to-all-start.1 = ((bf16[16,10,8,640]{3,2,1,0:T(8,128)(2,1)}), bf16[16,10,8,640]{3,2,1,0:T(8,128)(2,1)}, u32[]{:S(2)}, u32[]{:S(2)}) async-start(bf16[16,10,8,640]{3,2,1,0:T(8,128)(2,1)} %copy_bitcast_fusion.1), calls=%async_computation.1 | async-start | bytes 3276800 | tf_op jit(solution)/shard_map/all_to_all | solution.py:30
  71.9 23.7 %all-to-all-done.1 = bf16[16,10,8,640]{3,2,1,0:T(8,128)(2,1)} async-done(((bf16[16,10,8,640]{3,2,1,0:T(8,128)(2,1)}), bf16[16,10,8,640]{3,2,1,0:T(8,128)(2,1)}, u32[]{:S(2)}, u32[]{:S(2)}) %all-to-all-start.1) | async-done | bytes 1638432 | tf_op jit(solution)/shard_map/all_to_all | solution.py:30
  96.7 2.3 %fusion.102 = (bf16[160,8,256]{2,1,0:T(8,128)(2,1)}, bf16[160,8,2,128]{3,1,2,0:T(8,128)(2,1)S(1)}) fusion(bf16[160,8,640]{2,1,0:T(8,128)(2,1)} %bitcast.26), kind=kLoop, calls=%fused_computation.143 | loop fusion | bytes 2621440 | tf_op jit(solution)/shard_map/slice | solution.py:167
  100.3 1.9 %collective-permute-start.1 = (bf16[8,40,128]{2,1,0:T(8,128)(2,1)S(1)}, bf16[8,40,128]{2,1,0:T(8,128)(2,1)S(1)}, u32[]{:S(2)}, u32[]{:S(2)}) collective-permute-start(bf16[8,40,128]{2,1,0:T(8,128)(2,1)S(1)} %fusion.35), channel_id=1, source_target_pairs={{16,0},{32,16},{48,32},{64,48},{80,64},{96,80},{112,96},{128,112},... | collective-permute-start | bytes 245768 | tf_op jit(solution)/shard_map/ppermute | solution.py:18
  102.6 2.4 %collective-permute-start = (bf16[8,40,128]{2,1,0:T(8,128)(2,1)S(1)}, bf16[8,40,128]{2,1,0:T(8,128)(2,1)S(1)}, u32[]{:S(2)}, u32[]{:S(2)}) collective-permute-start(bf16[8,40,128]{2,1,0:T(8,128)(2,1)S(1)} %fusion.36), channel_id=1, source_target_pairs={{0,16},{16,32},{32,48},{48,64},{64,80},{80,96},{96,112},{112,128},... | collective-permute-start | bytes 245768 | tf_op jit(solution)/shard_map/ppermute | solution.py:18
  105.3 3.1 %collective-permute-done = bf16[8,40,128]{2,1,0:T(8,128)(2,1)S(1)} collective-permute-done((bf16[8,40,128]{2,1,0:T(8,128)(2,1)S(1)}, bf16[8,40,128]{2,1,0:T(8,128)(2,1)S(1)}, u32[]{:S(2)}, u32[]{:S(2)}) %collective-permute-start) | collective-permute-done | bytes 81952 | tf_op jit(solution)/shard_map/ppermute | solution.py:18
  109.4 20.6 %all_to_all.46 = bf16[8,160,384]{2,0,1:T(8,128)(2,1)S(1)} all-to-all(bf16[8,160,384]{2,0,1:T(8,128)(2,1)S(1)} %copy.163), channel_id=1, replica_groups=mesh['section'=32,'blk'=16] {'blk'}, dimensions={1} | all-to-all | bytes 1966080 | tf_op jit(solution)/shard_map/all_to_all | solution.py:22
  130.1 2.2 %fusion.67 = (bf16[1,10,128,128]{2,3,1,0:T(8,128)(2,1)S(1)}, bf16[1,10,128,128]{2,3,1,0:T(8,128)(2,1)S(1)}) fusion(f32[2,10,128,384]{2,3,1,0:T(8,128)} %copy-done, bf16[16,128,128]{2,1,0:T(8,128)(2,1)S(1)} %bitcast.225, bf16[128,10,384]{2,0,1:T(8,128)(2,1)S(1)} %bitcast.217), kind=kOutput, calls=%fused_computation.106 | convolution fusion | flops 44072960 | bytes 2621440 | tf_op jit(solution)/shard_map/prt,rop->rot/dot_general | solution.py:58
  134.8 2.2 %copy.165 = bf16[128,10,256]{0,2,1:T(8,128)(2,1)} copy(bf16[128,10,256]{2,0,1:T(8,128)(2,1)} %slice.123) | data formatting | bytes 1310720 | tf_op jit(solution)/shard_map/slice | solution.py:148
  137.0 1.5 convolution_bitcast_fusion.1
  140.7 4.4 %all-to-all-start.3 = ((bf16[16,10,8,384]{3,2,1,0:T(8,128)(2,1)}), bf16[16,10,8,384]{3,2,1,0:T(8,128)(2,1)}, u32[]{:S(2)}, u32[]{:S(2)}) async-start(bf16[16,10,8,384]{3,2,1,0:T(8,128)(2,1)} %copy_bitcast_fusion.2), calls=%async_computation.3 | async-start | bytes 1966080 | tf_op jit(solution)/shard_map/all_to_all | solution.py:30
  146.0 1.9 %copy.210 = bf16[128,10,128]{0,2,1:T(8,128)(2,1)} copy(bf16[128,10,128]{2,0,1:T(8,128)(2,1)} %slice.116) | data formatting | bytes 655360
  152.7 1.7 %fusion.3 = bf16[2,10,128,128]{3,2,1,0:T(8,128)(2,1)S(1)} fusion(bf16[1,10,128,128]{2,3,1,0:T(8,128)(2,1)} %copy-done.33, bf16[1,10,128,128]{2,3,1,0:T(8,128)(2,1)} %copy-done.32, bf16[1,10,128,128]{2,3,1,0:T(8,128)(2,1)} %copy-done.31, bf16[1,10,128,128]{2,3,1,0:T(8,128)(2,1)S(1)} %copy-done.30, bf16[128,10,2,384]{0,3,2,1:T(8,128)(2,1)S(1)} %bitcast.215), kind=kOutput, calls=%fused_computation.14 | convolution fusion | flops 173670400 | bytes 3276800 | tf_op jit(solution)/shard_map/prgt,grot->grpo/dot_general | solution.py:172
  157.3 4.9 %all-to-all-done.3 = bf16[16,10,8,384]{3,2,1,0:T(8,128)(2,1)} async-done(((bf16[16,10,8,384]{3,2,1,0:T(8,128)(2,1)}), bf16[16,10,8,384]{3,2,1,0:T(8,128)(2,1)}, u32[]{:S(2)}, u32[]{:S(2)}) %all-to-all-start.3) | async-done | bytes 983072 | tf_op jit(solution)/shard_map/all_to_all | solution.py:30
  (115 shorter events, 34.2 us)
Async XLA Ops:
  9.6 7.2 %copy-start.17 = (bf16[1,10,16384]{2,1,0:T(8,128)(2,1)S(1)}, bf16[1,10,16384]{2,1,0:T(8,128)(2,1)}, u32[]{:S(2)}) copy-start(bf16[1,10,16384]{2,1,0:T(8,128)(2,1)} %param.16) | copy-start | bytes 983044
  9.6 41.7 %all-to-all-start = ((bf16[8,160,896]{2,0,1:T(8,128)(2,1)}), bf16[8,160,896]{2,0,1:T(8,128)(2,1)S(1)}, u32[]{:S(2)}, u32[]{:S(2)}) async-start(bf16[8,160,896]{2,0,1:T(8,128)(2,1)} %copy.143), calls=%async_computation | async-start | bytes 4587520 | tf_op jit(solution)/shard_map/all_to_all | solution.py:22
  62.4 1.9 %copy-start = (f32[2,10,128,384]{2,3,1,0:T(8,128)}, f32[2,10,128,384]{2,3,1,0:T(8,128)S(1)}, u32[]{:S(2)}) copy-start(f32[2,10,128,384]{2,3,1,0:T(8,128)S(1)} %convolution_bitcast_fusion) | copy-start | bytes 11796484
  62.9 2.6 %copy-start.3 = (bf16[10,128,384]{1,2,0:T(8,128)(2,1)}, bf16[10,128,384]{1,2,0:T(8,128)(2,1)S(1)}, u32[]{:S(2)}) copy-start(bf16[10,128,384]{1,2,0:T(8,128)(2,1)S(1)} %fusion.1) | copy-start | bytes 2949124
  67.5 28.1 %all-to-all-start.1 = ((bf16[16,10,8,640]{3,2,1,0:T(8,128)(2,1)}), bf16[16,10,8,640]{3,2,1,0:T(8,128)(2,1)}, u32[]{:S(2)}, u32[]{:S(2)}) async-start(bf16[16,10,8,640]{3,2,1,0:T(8,128)(2,1)} %copy_bitcast_fusion.1), calls=%async_computation.1 | async-start | bytes 3276800 | tf_op jit(solution)/shard_map/all_to_all | solution.py:30
  95.6 3.4 %copy-start.7 = (bf16[2,8,40,160]{3,2,1,0:T(8,128)(2,1)S(1)}, bf16[2,8,40,160]{3,2,1,0:T(8,128)(2,1)}, u32[]{:S(2)}) copy-start(bf16[2,8,40,160]{3,2,1,0:T(8,128)(2,1)} %copy-done.6) | copy-start | bytes 614404
  96.6 5.6 %copy-start.18 = (bf16[1,320,128]{2,1,0:T(8,128)(2,1)S(1)}, bf16[1,320,128]{2,1,0:T(8,128)(2,1)}, u32[]{:S(2)}) copy-start(bf16[1,320,128]{2,1,0:T(8,128)(2,1)} %param.9) | copy-start | bytes 245764
  96.6 8.3 %copy-start.26 = (bf16[320,128]{1,0:T(8,128)(2,1)S(1)}, bf16[320,128]{1,0:T(8,128)(2,1)}, u32[]{:S(2)}) copy-start(bf16[320,128]{1,0:T(8,128)(2,1)} %param.13) | copy-start | bytes 245764
  99.0 9.8 %copy-start.9 = (bf16[160,8,2,128]{3,1,2,0:T(8,128)(2,1)}, bf16[160,8,2,128]{3,1,2,0:T(8,128)(2,1)S(1)}, u32[]{:S(2)}) copy-start(bf16[160,8,2,128]{3,1,2,0:T(8,128)(2,1)S(1)} %get-tuple-element.35) | copy-start | bytes 1966084
  99.0 9.4 %copy-start.19 = (bf16[320,128]{1,0:T(8,128)(2,1)S(1)}, bf16[320,128]{1,0:T(8,128)(2,1)}, u32[]{:S(2)}) copy-start(bf16[320,128]{1,0:T(8,128)(2,1)} %param.10) | copy-start | bytes 245764
  100.3 4.6 %collective-permute-start.1 = (bf16[8,40,128]{2,1,0:T(8,128)(2,1)S(1)}, bf16[8,40,128]{2,1,0:T(8,128)(2,1)S(1)}, u32[]{:S(2)}, u32[]{:S(2)}) collective-permute-start(bf16[8,40,128]{2,1,0:T(8,128)(2,1)S(1)} %fusion.35), channel_id=1, source_target_pairs={{16,0},{32,16},{48,32},{64,48},{80,64},{96,80},{112,96},{128,112},... | collective-permute-start | bytes 245768 | tf_op jit(solution)/shard_map/ppermute | solution.py:18
  102.6 5.8 %collective-permute-start = (bf16[8,40,128]{2,1,0:T(8,128)(2,1)S(1)}, bf16[8,40,128]{2,1,0:T(8,128)(2,1)S(1)}, u32[]{:S(2)}, u32[]{:S(2)}) collective-permute-start(bf16[8,40,128]{2,1,0:T(8,128)(2,1)S(1)} %fusion.36), channel_id=1, source_target_pairs={{0,16},{16,32},{32,48},{48,64},{64,80},{80,96},{96,112},{112,128},... | collective-permute-start | bytes 245768 | tf_op jit(solution)/shard_map/ppermute | solution.py:18
  105.0 3.3 %copy-start.23 = (bf16[8,40,128]{2,1,0:T(8,128)(2,1)}, bf16[8,40,128]{2,1,0:T(8,128)(2,1)S(1)}, u32[]{:S(2)}) copy-start(bf16[8,40,128]{2,1,0:T(8,128)(2,1)S(1)} %broadcast_select_fusion) | copy-start | bytes 245764
  109.4 20.7 %copy-start.12 = (bf16[2,8,128,128]{3,2,1,0:T(8,128)(2,1)S(1)}, bf16[2,8,128,128]{3,2,1,0:T(8,128)(2,1)}, u32[]{:S(2)}) copy-start(bf16[2,8,128,128]{3,2,1,0:T(8,128)(2,1)} %copy.218) | copy-start | bytes 1572868
  130.1 2.2 %copy-start.5 = (bf16[16,8,10,384]{3,1,0,2:T(8,128)(2,1)}, bf16[16,8,10,384]{3,1,0,2:T(8,128)(2,1)S(1)}, u32[]{:S(2)}) copy-start(bf16[16,8,10,384]{3,1,0,2:T(8,128)(2,1)S(1)} %copy.263) | copy-start | bytes 2949124
  140.7 7.2 %copy-start.10 = (bf16[160,8,2,128]{3,1,2,0:T(8,128)(2,1)S(1)}, bf16[160,8,2,128]{3,1,2,0:T(8,128)(2,1)}, u32[]{:S(2)}) copy-start(bf16[160,8,2,128]{3,1,2,0:T(8,128)(2,1)} %copy-done.9) | copy-start | bytes 1966084
  140.7 21.5 %all-to-all-start.3 = ((bf16[16,10,8,384]{3,2,1,0:T(8,128)(2,1)}), bf16[16,10,8,384]{3,2,1,0:T(8,128)(2,1)}, u32[]{:S(2)}, u32[]{:S(2)}) async-start(bf16[16,10,8,384]{3,2,1,0:T(8,128)(2,1)} %copy_bitcast_fusion.2), calls=%async_computation.3 | async-start | bytes 1966080 | tf_op jit(solution)/shard_map/all_to_all | solution.py:30
  146.0 2.9 %copy-start.24 = (bf16[8,40,128]{2,1,0:T(8,128)(2,1)S(1)}, bf16[8,40,128]{2,1,0:T(8,128)(2,1)}, u32[]{:S(2)}) copy-start(bf16[8,40,128]{2,1,0:T(8,128)(2,1)} %copy-done.23) | copy-start | bytes 245764
  146.0 2.9 %copy-start.28 = (bf16[1,320,128]{2,1,0:T(8,128)(2,1)S(1)}, bf16[1,320,128]{2,1,0:T(8,128)(2,1)}, u32[]{:S(2)}) copy-start(bf16[1,320,128]{2,1,0:T(8,128)(2,1)} %param.12) | copy-start | bytes 245764
  147.9 4.8 %copy-start.2 = (bf16[128,10,768]{0,2,1:T(8,128)(2,1)S(1)}, bf16[128,10,768]{0,2,1:T(8,128)(2,1)}, u32[]{:S(2)}) copy-start(bf16[128,10,768]{0,2,1:T(8,128)(2,1)} %copy.145) | copy-start | bytes 5898244
  148.9 3.8 %copy-start.30 = (bf16[1,10,128,128]{2,3,1,0:T(8,128)(2,1)S(1)}, bf16[1,10,128,128]{2,3,1,0:T(8,128)(2,1)}, u32[]{:S(2)}) copy-start(bf16[1,10,128,128]{2,3,1,0:T(8,128)(2,1)} %copy-done.29) | copy-start | bytes 983044
  155.9 8.6 %copy-start.8 = (bf16[2,8,40,160]{3,2,1,0:T(8,128)(2,1)S(1)}, bf16[2,8,40,160]{3,2,1,0:T(8,128)(2,1)}, u32[]{:S(2)}) copy-start(bf16[2,8,40,160]{3,2,1,0:T(8,128)(2,1)} %copy-done.6) | copy-start | bytes 614404
  155.9 8.6 %copy-start.25 = (bf16[8,40,128]{2,1,0:T(8,128)(2,1)S(1)}, bf16[8,40,128]{2,1,0:T(8,128)(2,1)}, u32[]{:S(2)}) copy-start(bf16[8,40,128]{2,1,0:T(8,128)(2,1)} %copy-done.23) | copy-start | bytes 245764
  163.2 2.4 %copy-start.16 = (bf16[160,8,2,128]{3,0,2,1:T(8,128)(2,1)S(1)}, bf16[160,8,2,128]{3,0,2,1:T(8,128)(2,1)}, u32[]{:S(2)}) copy-start(bf16[160,8,2,128]{3,0,2,1:T(8,128)(2,1)} %copy.160) | copy-start | bytes 1966084
  (15 other events, 19.6 us)

commit v5 on v2

v5 whole, which is shorter than its diff:
```python
import functools
import math

import jax
import jax.numpy as jnp
from jax import lax
from jax.experimental import pallas as pl
from jax.experimental.pallas import tpu as pltpu
from jax.sharding import PartitionSpec as P

BLOCK = 128
FIRST_BLOCKS = 128
FIRST_IN = 40
SECOND_BLOCKS = 160
TICKS = 2


def from_behind(value, axis, by):
    length = lax.axis_size(axis)
    pairs = [(i, i + by) for i in range(length) if 0 <= i + by < length]
    return lax.ppermute(value, axis, pairs)


def to_blocks(pieces):
    return lax.all_to_all(pieces, "blk", split_axis=1, concat_axis=0, tiled=True)


def to_features(pieces):
    groups = lax.axis_size("blk")
    r_local, p_all, n = pieces.shape
    p_local = p_all // groups
    grouped = pieces.reshape(r_local, groups, p_local, n).transpose(1, 0, 2, 3)
    arrived = lax.all_to_all(grouped, "blk", split_axis=0, concat_axis=0, tiled=True)
    return arrived.reshape(groups * r_local, p_local, n)


def spread_of(values, up_first):
    return jnp.einsum(
        "pqt,gpqr->prgt", values, up_first, preferred_element_type=jnp.float32
    ).astype(jnp.bfloat16)


def lowered_grad_of(grads, down_second):
    return jnp.einsum(
        "pqt,prq->prt", grads, down_second, preferred_element_type=jnp.float32
    ).astype(jnp.bfloat16)


def _middle_kernel(fwd, bwd, bwd_at, keep_at, has_mixed_in, *refs):
    refs = list(refs)
    arrived, up, up_t, down, down_t = refs[:5]
    refs = refs[5:]
    mixed_in = refs.pop(0) if has_mixed_in else None
    payload, grad_mixed = refs[0], refs[1]
    rest = refs[2:]
    hidden_out = rest.pop(0) if not has_mixed_in else None
    keep_out = rest.pop(0) if keep_at is not None else None
    for r in range(arrived.shape[0]):
        gate = jnp.dot(up_t[0, r], arrived[r, :, :fwd], preferred_element_type=jnp.float32)
        upper = jnp.dot(
            up_t[1, r], arrived[r, :, fwd : 2 * fwd], preferred_element_type=jnp.float32
        )
        hidden = (gate / (1.0 + jnp.exp(-gate)) * upper).astype(jnp.bfloat16)
        payload[r, :, :fwd] = jnp.dot(
            down_t[r], hidden, preferred_element_type=jnp.float32
        ).astype(jnp.bfloat16)
        if hidden_out is not None:
            hidden_out[r] = hidden
        if keep_out is not None:
            keep_out[0, r] = gate[:, keep_at : keep_at + bwd]
            keep_out[1, r] = upper[:, keep_at : keep_at + bwd]
        if has_mixed_in:
            m0, m1 = mixed_in[0, r], mixed_in[1, r]
        else:
            m0, m1 = gate[:, bwd_at : bwd_at + bwd], upper[:, bwd_at : bwd_at + bwd]
        grad_hidden = jnp.dot(
            down[r], arrived[r, :, 2 * fwd :], preferred_element_type=jnp.float32
        )
        sg = 1.0 / (1.0 + jnp.exp(-m0))
        gm0 = (grad_hidden * m1 * (sg * (1.0 + m0 * (1.0 - sg)))).astype(jnp.bfloat16)
        gm1 = (grad_hidden * m0 * sg).astype(jnp.bfloat16)
        grad_mixed[0, r] = gm0
        grad_mixed[1, r] = gm1
        payload[r, :, fwd : fwd + bwd] = jnp.dot(
            up[0, r], gm0, preferred_element_type=jnp.float32
        ).astype(jnp.bfloat16)
        payload[r, :, fwd + bwd :] = jnp.dot(
            up[1, r], gm1, preferred_element_type=jnp.float32
        ).astype(jnp.bfloat16)


def middle(arrived, up, up_t, down, down_t, fwd, bwd, bwd_at=0, keep_at=None, mixed_in=None):
    rb, pa, _ = arrived.shape
    o = up.shape[3]
    outs = [
        jax.ShapeDtypeStruct((rb, pa, fwd + 2 * bwd), jnp.bfloat16),
        jax.ShapeDtypeStruct((2, rb, o, bwd), jnp.bfloat16),
    ]
    if mixed_in is None:
        outs.append(jax.ShapeDtypeStruct((rb, o, fwd), jnp.bfloat16))
    if keep_at is not None:
        outs.append(jax.ShapeDtypeStruct((2, rb, o, bwd), jnp.float32))
    ins = [arrived, up, up_t, down, down_t] + ([mixed_in] if mixed_in is not None else [])
    flops = 2 * rb * o * pa * (3 * fwd + 3 * bwd)
    bytes_accessed = sum(x.size * x.dtype.itemsize for x in ins) + sum(
        math.prod(s.shape) * s.dtype.itemsize for s in outs
    )
    vmem = pltpu.MemorySpace.VMEM
    return pl.pallas_call(
        functools.partial(_middle_kernel, fwd, bwd, bwd_at, keep_at, mixed_in is not None),
        out_shape=tuple(outs),
        in_specs=[pl.BlockSpec(memory_space=vmem)] * len(ins),
        out_specs=tuple(pl.BlockSpec(memory_space=vmem) for _ in outs),
        cost_estimate=pl.CostEstimate(
            flops=flops, transcendentals=rb * o * (fwd + bwd), bytes_accessed=bytes_accessed
        ),
    )(*ins)


def output_of(values, lowered_p, down_second):
    added = jnp.einsum("rpt,prq->pqt", lowered_p, down_second, preferred_element_type=jnp.float32)
    return (values.astype(jnp.float32) + added).astype(jnp.bfloat16)


def input_grad_of(grads, grad_spread_p, up_first):
    added = jnp.einsum(
        "rpgt,gpqr->pqt", grad_spread_p, up_first, preferred_element_type=jnp.float32
    )
    return (grads.astype(jnp.float32) + added).astype(jnp.bfloat16)


def shards(
    held_input,
    fresh_input,
    stashed,
    held_grad,
    fresh_grad,
    first_up,
    second_up,
    first_down,
    second_down,
):
    pb = first_up.shape[2]
    rb = second_up.shape[2]
    t = held_input.shape[2]
    up_first = first_up[0].reshape(2, pb, FIRST_IN, SECOND_BLOCKS)
    up_second = second_up[0].reshape(2, rb, FIRST_BLOCKS, BLOCK)
    down_first = first_down[0].reshape(rb, BLOCK, FIRST_BLOCKS)
    down_second = second_down[0].reshape(pb, SECOND_BLOCKS, FIRST_IN)
    up_second_t = jnp.swapaxes(up_second, 2, 3)
    down_first_t = jnp.swapaxes(down_first, 1, 2)
    first_inputs = held_input[0].reshape(pb, FIRST_IN, t)
    first_grads = held_grad[0].reshape(pb, FIRST_IN, t)
    stash_0 = stashed[0, 0].reshape(pb, FIRST_IN, t)
    stash_1 = stashed[0, 1].reshape(pb, FIRST_IN, t)
    section_pos = lax.axis_index("section")
    last_section = lax.axis_size("section") - 1
    weights = (up_second, up_second_t, down_first, down_first_t)

    spread_a = spread_of(jnp.concatenate([first_inputs, stash_0, stash_1], axis=2), up_first)
    glow_1 = lowered_grad_of(first_grads, down_second)
    payload = jnp.concatenate([spread_a.reshape(pb, SECOND_BLOCKS, 6 * t), glow_1], axis=2)
    arrived_a = jnp.swapaxes(to_blocks(payload), 0, 1)
    payload_a, gmix_1, hidden_a, mixed_s1 = middle(
        arrived_a, *weights, fwd=3 * t, bwd=t, bwd_at=t, keep_at=2 * t
    )
    back = to_features(payload_a)
    lowered_ap = back[:, :, : 3 * t]
    gspread_1p = back[:, :, 3 * t :].reshape(SECOND_BLOCKS, pb, 2, t)
    outputs = output_of(first_inputs, lowered_ap[:, :, :t], down_second)
    backward = input_grad_of(first_grads, gspread_1p, up_first)

    moved_forward = from_behind(outputs, "section", 1)
    inputs = jnp.where(section_pos == 0, fresh_input.reshape(pb, FIRST_IN, t), moved_forward)
    moved_backward = from_behind(backward, "section", -1)
    grads = jnp.where(
        section_pos == last_section, fresh_grad.reshape(pb, FIRST_IN, t), moved_backward
    )

    spread_b = spread_of(inputs, up_first)
    glow_2 = lowered_grad_of(grads, down_second)
    payload = jnp.concatenate([spread_b.reshape(pb, SECOND_BLOCKS, 2 * t), glow_2], axis=2)
    arrived_b = jnp.swapaxes(to_blocks(payload), 0, 1)
    payload_b, gmix_2 = middle(arrived_b, *weights, fwd=t, bwd=t, mixed_in=mixed_s1)
    back = to_features(payload_b)
    outputs = output_of(inputs, back[:, :, :t], down_second)
    gspread_2p = back[:, :, t:].reshape(SECOND_BLOCKS, pb, 2, t)
    backward = input_grad_of(grads, gspread_2p, up_first)

    stash_both = jnp.concatenate([stash_0, stash_1], axis=2)
    gspread_both = jnp.concatenate([gspread_1p, gspread_2p], axis=3)
    spread_both = jnp.stack(
        [arrived_a[:, :, t : 3 * t], arrived_a[:, :, 4 * t : 6 * t]]
    )
    gmix_both = jnp.concatenate([gmix_1, gmix_2], axis=3)
    hidden_both = hidden_a[:, :, t:]
    glow_both = jnp.concatenate([arrived_a[:, :, 6 * t :], arrived_b[:, :, 2 * t :]], axis=2)
    lowered_both = lowered_ap[:, :, t:]
    grads_both = jnp.concatenate([first_grads, grads], axis=2)
    total_first_up = jnp.einsum(
        "pqt,rpgt->gpqr", stash_both, gspread_both, preferred_element_type=jnp.float32
    )
    total_second_up = jnp.einsum(
        "grpt,grot->grpo", spread_both, gmix_both, preferred_element_type=jnp.float32
    )
    total_first_down = jnp.einsum(
        "rot,rpt->rop", hidden_both, glow_both, preferred_element_type=jnp.float32
    )
    total_second_down = jnp.einsum(
        "rpt,pqt->prq", lowered_both, grads_both, preferred_element_type=jnp.float32
    )
    factor = 1.0 / math.sqrt(TICKS * t)
    return (
        outputs.reshape(held_input.shape),
        backward.reshape(held_grad.shape),
        (total_first_up * factor).astype(jnp.bfloat16).reshape(first_up.shape),
        (total_second_up * factor).astype(jnp.bfloat16).reshape(second_up.shape),
        (total_first_down * factor).astype(jnp.bfloat16).reshape(first_down.shape),
        (total_second_down * factor).astype(jnp.bfloat16).reshape(second_down.shape),
    )


def solution(mesh):
    return jax.shard_map(
        shards,
        mesh=mesh,
        in_specs=(
            P("section", "blk", None),
            P("blk", None),
            P("section", None, "blk", None),
            P("section", "blk", None),
            P("blk", None),
            P("section", None, "blk", None),
            P("section", None, "blk", None),
            P("section", "blk", None),
            P("section", "blk", None),
        ),
        out_specs=(
            P("section", "blk", None),
            P("section", "blk", None),
            P("section", None, "blk", None),
            P("section", None, "blk", None),
            P("section", "blk", None),
            P("section", "blk", None),
        ),
        check_vma=False,
    )
```

time: 209 us -> 158 us (0.76)
  local copies, waits for them, and re-layouts: 61.7 us -> 34.4 us
  blocking collectives: 0 us -> 20.4 us
  starting transfers between devices: 36.4 us -> 19.6 us
  waiting for transfers between devices: 75.3 us -> 59 us
  matrix products: 23.3 us -> 9.65 us
  Pallas kernels: 0 us -> 13.1 us
  other arithmetic: 9.02 us -> 0.3 us
    all_to_all x0 -> x1, blocking collectives: none -> 20.4 us  [to_blocks(): lax.all_to_all(pieces, 'blk', split_axis=1, concat_axis=0, tiled=True)]
    all_to_all x6 -> x3, starting transfers between devices: 32 us -> 15.3 us  [the longest x2 8.22 us: to_features(): lax.all_to_all(grouped, 'blk', split_axis=0, concat_axis=0, tiled=True)]
    all_to_all x6 -> x3, waiting for transfers between devices: 72.4 us -> 55.9 us  [the longest x1 28.2 us: to_blocks(): lax.all_to_all(pieces, 'blk', split_axis=1, concat_axis=0, tiled=True)]
    dot_general x22 -> x11, matrix products: 22.9 us -> 8.23 us  [the longest x2 2.02 us: spread_of(): jnp.einsum('pqt,gpqr->prgt', values, up_first, preferred_element_type=jnp...]
    pallas_call x0 -> x2, Pallas kernels: none -> 13.1 us  [middle(): pl.pallas_call(functools.partial(_middle_kernel, fwd, bwd, bwd_at, keep_a...]
    reshape x9 -> x5, local copies, waits for them, and re-layouts: 14.7 us -> 1.86 us  [the longest x2 1.37 us: shards(): gspread_2p = back[:, :, t:].reshape(SECOND_BLOCKS, pb, 2, t)]
    concatenate x5 -> x2, other arithmetic: 8.65 us -> 0.29 us  [the longest x1 0.18 us: shards(): jnp.concatenate([spread_a.reshape(pb, SECOND_BLOCKS, 6 * t), glow_1], axi...]
    unnamed x77 -> x32, local copies, waits for them, and re-layouts: 9.76 us -> 2.57 us
  transfers between devices with their start and end apart: 8 -> 5, of which waited for: 6 -> 4; matrix products, arithmetic and copies ran while one was open for 20% -> 12% of each run, Pallas kernels for 0% -> 0%
where the time goes in v5:
time: 158 us; the launch traced here: 157 us
  waiting for transfers between devices  59 us (37%)
  local copies, waits for them, and re-layouts  34.4 us (22%)
  blocking collectives  20.4 us (13%)
  starting transfers between devices  19.6 us (12%)
  Pallas kernels  13.1 us (8%)
  matrix products  9.65 us (6%)
    all_to_all x1, waiting for transfers between devices, to_blocks(): lax.all_to_all(pieces, 'blk', split_axis=1, concat_axis=0, tiled=True)  28.2 us
    all_to_all x2, waiting for transfers between devices, to_features(): lax.all_to_all(grouped, 'blk', split_axis=0, concat_axis=0, tiled=True)  27.8 us
    all_to_all x1, blocking collectives, to_blocks(): lax.all_to_all(pieces, 'blk', split_axis=1, concat_axis=0, tiled=True)  20.4 us
    pallas_call x2, Pallas kernels, middle(): pl.pallas_call(functools.partial(_middle_kernel, fwd, bwd, bwd_at, keep_a...  13.1 us
    all_to_all x2, starting transfers between devices, to_features(): lax.all_to_all(grouped, 'blk', split_axis=0, concat_axis=0, tiled=True)  8.22 us
    all_to_all x1, starting transfers between devices, to_blocks(): lax.all_to_all(pieces, 'blk', split_axis=1, concat_axis=0, tiled=True)  7.03 us
    transpose x2, local copies, waits for them, and re-layouts, to_features(): grouped = pieces.reshape(r_local, groups, p_local, n).transpose(1, 0, 2, 3)  5.13 us
    ppermute x2, starting transfers between devices, from_behind(): return lax.ppermute(value, axis, pairs)  4.33 us
  transfers between devices with their start and end apart: 5, of which 4 were waited for; matrix products, arithmetic and copies ran while one was open for 12% of the time, Pallas kernels for 0%

profile of v5, /device:TPU:224, one launch (start us, length us, event | category | flops | bytes accessed | tf_op | source)
XLA Modules:
  0.0 157.4 jit_solution(11972637261423346610)
XLA Ops:
  1.6 1.4 reshape_squeeze.27
  3.0 1.6 reshape_squeeze.28
  4.5 1.6 %convert_bitcast_fusion = bf16[8,2,20,8,384]{4,3,2,1,0:T(8,128)(2,1)S(1)} fusion(bf16[8,40,128]{2,1,0:T(8,128)(2,1)S(1)} %bitcast.144, bf16[8,40,128]{2,1,0:T(8,128)(2,1)S(1)} %bitcast.142, bf16[8,40,128]{2,1,0:T(8,128)(2,1)} %bitcast.138, bf16[2,8,40,160]{3,2,1,0:T(8,128)(2,1)S(1)} %reshape_squeeze.27), kind=kOutput, calls=%fused_computation.2 | convolution fusion | flops 80363520 | bytes 2416640 | tf_op jit(solution)/shard_map/pqt,gpqr->prgt/dot_general | solution.py:38
  7.4 2.2 %copy.94 = bf16[8,160,896]{2,0,1:T(8,128)(2,1)} copy(bf16[8,160,896]{2,1,0:T(8,128)(2,1)S(1)} %pad_maximum_fusion) | data formatting | bytes 4587520 | tf_op jit(solution)/shard_map/concatenate | solution.py:162
  9.6 7.0 %all-to-all-start = ((bf16[8,160,896]{2,0,1:T(8,128)(2,1)}), bf16[8,160,896]{2,0,1:T(8,128)(2,1)S(1)}, u32[]{:S(2)}, u32[]{:S(2)}) async-start(bf16[8,160,896]{2,0,1:T(8,128)(2,1)} %copy.94), calls=%async_computation | async-start | bytes 4587520 | tf_op jit(solution)/shard_map/all_to_all | solution.py:25
  16.6 2.3 %reshape_squeeze.30 = bf16[2,10,128,128]{3,2,0,1:T(8,128)(2,1)S(1)} reshape(bf16[1,2,10,16384]{3,1,2,0:T(2,128)(2,1)} %param.15) | data formatting | bytes 1310720 | tf_op jit(solution)/shard_map/reshape;squeeze | solution.py:147
  23.0 28.2 %all-to-all-done = bf16[8,160,896]{2,0,1:T(8,128)(2,1)S(1)} async-done(((bf16[8,160,896]{2,0,1:T(8,128)(2,1)}), bf16[8,160,896]{2,0,1:T(8,128)(2,1)S(1)}, u32[]{:S(2)}, u32[]{:S(2)}) %all-to-all-start) | async-done | bytes 2293792 | tf_op jit(solution)/shard_map/all_to_all | solution.py:25
  51.2 1.7 %copy.165 = bf16[16,8,10,896]{3,1,0,2:T(8,128)(2,1)} copy(bf16[16,8,10,896]{3,1,2,0:T(8,128)(2,1)S(1)} %bitcast.124) | data formatting | bytes 4587520 | tf_op jit(solution)/shard_map/all_to_all | solution.py:25
  52.9 7.8 %shard_map.136 = (bf16[10,128,640]{2,1,0:T(8,128)(2,1)}, bf16[2,10,128,128]{3,2,1,0:T(8,128)(2,1)}, bf16[10,128,384]{2,1,0:T(8,128)(2,1)}, f32[2,10,128,128]{3,2,1,0:T(8,128)}) custom-call(bf16[10,128,896]{2,1,0:T(8,128)(2,1)} %bitcast.121, bf16[2,10,128,128]{3,2,1,0:T(8,128)(2,1)} %copy.98.refs_1_, bf16[2,10,128,128]{3,2,1,0:T(8,128)(2,1)} %bitcast.128, ...), custom_call_target="tpu_custom_call" | custom-call | flops 503316480 | bytes 8847360 | tf_op jit(solution)/shard_map/pallas_call | solution.py:109
  60.7 2.7 %copy_bitcast_fusion.1 = bf16[16,10,8,640]{3,2,1,0:T(8,128)(2,1)} fusion(bf16[10,128,640]{2,1,0:T(8,128)(2,1)} %get-tuple-element.12), kind=kLoop, calls=%fused_computation.3 | loop fusion | bytes 3276800 | tf_op jit(solution)/shard_map/transpose | solution.py:32
  63.5 3.7 %all-to-all-start.1 = ((bf16[16,10,8,640]{3,2,1,0:T(8,128)(2,1)}), bf16[16,10,8,640]{3,2,1,0:T(8,128)(2,1)S(1)}, u32[]{:S(2)}, u32[]{:S(2)}) async-start(bf16[16,10,8,640]{3,2,1,0:T(8,128)(2,1)} %copy_bitcast_fusion.1), calls=%async_computation.1 | async-start | bytes 3276800 | tf_op jit(solution)/shard_map/all_to_all | solution.py:33
  67.2 23.6 %all-to-all-done.1 = bf16[16,10,8,640]{3,2,1,0:T(8,128)(2,1)S(1)} async-done(((bf16[16,10,8,640]{3,2,1,0:T(8,128)(2,1)}), bf16[16,10,8,640]{3,2,1,0:T(8,128)(2,1)S(1)}, u32[]{:S(2)}, u32[]{:S(2)}) %all-to-all-start.1) | async-done | bytes 1638432 | tf_op jit(solution)/shard_map/all_to_all | solution.py:33
  92.2 1.9 %collective-permute-start.1 = (bf16[8,40,128]{2,1,0:T(8,128)(2,1)S(1)}, bf16[8,40,128]{2,1,0:T(8,128)(2,1)S(1)}, u32[]{:S(2)}, u32[]{:S(2)}) collective-permute-start(bf16[8,40,128]{2,1,0:T(8,128)(2,1)S(1)} %fusion.26), channel_id=1, source_target_pairs={{16,0},{32,16},{48,32},{64,48},{80,64},{96,80},{112,96},{128,112},... | collective-permute-start | bytes 245768 | tf_op jit(solution)/shard_map/ppermute | solution.py:21
  94.4 2.4 %collective-permute-start = (bf16[8,40,128]{2,1,0:T(8,128)(2,1)S(1)}, bf16[8,40,128]{2,1,0:T(8,128)(2,1)S(1)}, u32[]{:S(2)}, u32[]{:S(2)}) collective-permute-start(bf16[8,40,128]{2,1,0:T(8,128)(2,1)S(1)} %fusion.27), channel_id=1, source_target_pairs={{0,16},{16,32},{32,48},{48,64},{64,80},{80,96},{96,112},{112,128},... | collective-permute-start | bytes 245768 | tf_op jit(solution)/shard_map/ppermute | solution.py:21
  97.1 3.1 %collective-permute-done = bf16[8,40,128]{2,1,0:T(8,128)(2,1)S(1)} collective-permute-done((bf16[8,40,128]{2,1,0:T(8,128)(2,1)S(1)}, bf16[8,40,128]{2,1,0:T(8,128)(2,1)S(1)}, u32[]{:S(2)}, u32[]{:S(2)}) %collective-permute-start) | collective-permute-done | bytes 81952 | tf_op jit(solution)/shard_map/ppermute | solution.py:21
  101.2 20.4 %all_to_all.46 = bf16[8,160,384]{2,0,1:T(8,128)(2,1)S(1)} all-to-all(bf16[8,160,384]{2,0,1:T(8,128)(2,1)S(1)} %copy.107), channel_id=1, replica_groups=mesh['section'=32,'blk'=16] {'blk'}, dimensions={1} | all-to-all | bytes 1966080 | tf_op jit(solution)/shard_map/all_to_all | solution.py:25
  122.7 5.3 %shard_map.137 = (bf16[10,128,384]{2,1,0:T(8,128)(2,1)}, bf16[2,10,128,128]{3,2,1,0:T(8,128)(2,1)}) custom-call(bf16[10,128,384]{2,1,0:T(8,128)(2,1)} %bitcast.130, bf16[2,10,128,128]{3,2,1,0:T(8,128)(2,1)} %copy.98.refs_1_, bf16[2,10,128,128]{3,2,1,0:T(8,128)(2,1)} %bitcast.129, bf16[10,128,128]{2,1,0:T(8,128)(2,1)} %copy-done.1, ...), custom_call_target="tpu_custom_call" | custom-call | flops 251658240 | bytes 5898240 | tf_op jit(solution)/shard_map/pallas_call | solution.py:109
  128.0 2.4 %copy_bitcast_fusion.2 = bf16[16,10,8,384]{3,2,1,0:T(8,128)(2,1)} fusion(bf16[10,128,384]{2,1,0:T(8,128)(2,1)} %get-tuple-element.14), kind=kLoop, calls=%fused_computation.37 | loop fusion | bytes 1966080 | tf_op jit(solution)/shard_map/transpose | solution.py:32
  130.4 4.5 %all-to-all-start.3 = ((bf16[16,10,8,384]{3,2,1,0:T(8,128)(2,1)}), bf16[16,10,8,384]{3,2,1,0:T(8,128)(2,1)}, u32[]{:S(2)}, u32[]{:S(2)}) async-start(bf16[16,10,8,384]{3,2,1,0:T(8,128)(2,1)} %copy_bitcast_fusion.2), calls=%async_computation.3 | async-start | bytes 1966080 | tf_op jit(solution)/shard_map/all_to_all | solution.py:33
  135.7 1.2 slice_bitcast_fusion.1
  140.3 1.7 %slice.58 = bf16[10,128,128]{2,1,0:T(8,128)(2,1)} slice(bf16[10,128,384]{2,1,0:T(8,128)(2,1)} %bitcast.131), slice={[0:10], [0:128], [256:384]} | slice | bytes 655360 | tf_op jit(solution)/shard_map/slice | solution.py:197
  142.0 1.8 %fusion = bf16[2,10,128,128]{3,2,1,0:T(8,128)(2,1)S(1)} fusion(bf16[1,10,128,256]{3,2,1,0:T(8,128)(2,1)S(1)} %copy-done.8, bf16[1,10,128,256]{3,2,1,0:T(8,128)(2,1)S(1)} %copy-done.7, bf16[2,10,128,128]{3,2,1,0:T(8,128)(2,1)} %get-tuple-element.16, bf16[2,10,128,128]{3,2,1,0:T(8,128)(2,1)} %get-tuple-element.15), kind=kOutput, calls=%fused_computation.5 | convolution fusion | flops 171704320 | bytes 3276800 | tf_op jit(solution)/shard_map/grpt,grot->grpo/dot_general | solution.py:203
  144.9 1.4 fusion.15
  147.3 4.2 %all-to-all-done.3 = bf16[16,10,8,384]{3,2,1,0:T(8,128)(2,1)} async-done(((bf16[16,10,8,384]{3,2,1,0:T(8,128)(2,1)}), bf16[16,10,8,384]{3,2,1,0:T(8,128)(2,1)}, u32[]{:S(2)}, u32[]{:S(2)}) %all-to-all-start.3) | async-done | bytes 983072 | tf_op jit(solution)/shard_map/all_to_all | solution.py:33
  (67 shorter events, 22.4 us)
Async XLA Ops:
  2.9 3.4 %copy-start.2 = (bf16[2,8,40,160]{3,2,1,0:T(8,128)(2,1)}, bf16[2,8,40,160]{3,2,1,0:T(8,128)(2,1)S(1)}, u32[]{:S(2)}) copy-start(bf16[2,8,40,160]{3,2,1,0:T(8,128)(2,1)S(1)} %reshape_squeeze.27) | copy-start | bytes 614404
  6.1 0.9 copy-start.14
  9.6 41.6 %all-to-all-start = ((bf16[8,160,896]{2,0,1:T(8,128)(2,1)}), bf16[8,160,896]{2,0,1:T(8,128)(2,1)S(1)}, u32[]{:S(2)}, u32[]{:S(2)}) async-start(bf16[8,160,896]{2,0,1:T(8,128)(2,1)} %copy.94), calls=%async_computation | async-start | bytes 4587520 | tf_op jit(solution)/shard_map/all_to_all | solution.py:25
  22.1 30.8 %copy-start.1 = (bf16[10,128,128]{2,1,0:T(8,128)(2,1)}, bf16[10,128,128]{2,1,0:T(8,128)(2,1)S(1)}, u32[]{:S(2)}) copy-start(bf16[10,128,128]{2,1,0:T(8,128)(2,1)S(1)} %slice.60.refs_3_) | copy-start | bytes 983044
  63.5 27.3 %all-to-all-start.1 = ((bf16[16,10,8,640]{3,2,1,0:T(8,128)(2,1)}), bf16[16,10,8,640]{3,2,1,0:T(8,128)(2,1)S(1)}, u32[]{:S(2)}, u32[]{:S(2)}) async-start(bf16[16,10,8,640]{3,2,1,0:T(8,128)(2,1)} %copy_bitcast_fusion.1), calls=%async_computation.1 | async-start | bytes 3276800 | tf_op jit(solution)/shard_map/all_to_all | solution.py:33
  90.8 1.1 copy-start.3
  90.8 3.3 %copy-start.9 = (bf16[1,320,128]{2,1,0:T(8,128)(2,1)S(1)}, bf16[1,320,128]{2,1,0:T(8,128)(2,1)}, u32[]{:S(2)}) copy-start(bf16[1,320,128]{2,1,0:T(8,128)(2,1)} %param.9) | copy-start | bytes 245764
  91.8 8.8 %copy-start.4 = (bf16[160,8,2,128]{3,1,2,0:T(8,128)(2,1)}, bf16[160,8,2,128]{3,1,2,0:T(8,128)(2,1)S(1)}, u32[]{:S(2)}) copy-start(bf16[160,8,2,128]{3,1,2,0:T(8,128)(2,1)S(1)} %get-tuple-element.45) | copy-start | bytes 1966084
  91.8 5.0 %copy-start.13 = (bf16[320,128]{1,0:T(8,128)(2,1)S(1)}, bf16[320,128]{1,0:T(8,128)(2,1)}, u32[]{:S(2)}) copy-start(bf16[320,128]{1,0:T(8,128)(2,1)} %param.13) | copy-start | bytes 245764
  91.8 8.3 %copy-start.10 = (bf16[320,128]{1,0:T(8,128)(2,1)S(1)}, bf16[320,128]{1,0:T(8,128)(2,1)}, u32[]{:S(2)}) copy-start(bf16[320,128]{1,0:T(8,128)(2,1)} %param.10) | copy-start | bytes 245764
  92.2 4.6 %collective-permute-start.1 = (bf16[8,40,128]{2,1,0:T(8,128)(2,1)S(1)}, bf16[8,40,128]{2,1,0:T(8,128)(2,1)S(1)}, u32[]{:S(2)}, u32[]{:S(2)}) collective-permute-start(bf16[8,40,128]{2,1,0:T(8,128)(2,1)S(1)} %fusion.26), channel_id=1, source_target_pairs={{16,0},{32,16},{48,32},{64,48},{80,64},{96,80},{112,96},{128,112},... | collective-permute-start | bytes 245768 | tf_op jit(solution)/shard_map/ppermute | solution.py:21
  94.4 5.8 %collective-permute-start = (bf16[8,40,128]{2,1,0:T(8,128)(2,1)S(1)}, bf16[8,40,128]{2,1,0:T(8,128)(2,1)S(1)}, u32[]{:S(2)}, u32[]{:S(2)}) collective-permute-start(bf16[8,40,128]{2,1,0:T(8,128)(2,1)S(1)} %fusion.27), channel_id=1, source_target_pairs={{0,16},{16,32},{32,48},{48,64},{64,80},{80,96},{96,112},{112,128},... | collective-permute-start | bytes 245768 | tf_op jit(solution)/shard_map/ppermute | solution.py:21
  128.0 6.9 %copy-start = (bf16[16,8,10,896]{3,1,0,2:T(8,128)(2,1)S(1)}, bf16[16,8,10,896]{3,1,0,2:T(8,128)(2,1)}, u32[]{:S(2)}) copy-start(bf16[16,8,10,896]{3,1,0,2:T(8,128)(2,1)} %copy.165) | copy-start | bytes 6881284
  130.4 21.1 %all-to-all-start.3 = ((bf16[16,10,8,384]{3,2,1,0:T(8,128)(2,1)}), bf16[16,10,8,384]{3,2,1,0:T(8,128)(2,1)}, u32[]{:S(2)}, u32[]{:S(2)}) async-start(bf16[16,10,8,384]{3,2,1,0:T(8,128)(2,1)} %copy_bitcast_fusion.2), calls=%async_computation.3 | async-start | bytes 1966080 | tf_op jit(solution)/shard_map/all_to_all | solution.py:33
  134.9 2.0 %copy-start.5 = (bf16[160,8,2,128]{3,1,2,0:T(8,128)(2,1)S(1)}, bf16[160,8,2,128]{3,1,2,0:T(8,128)(2,1)}, u32[]{:S(2)}) copy-start(bf16[160,8,2,128]{3,1,2,0:T(8,128)(2,1)} %copy-done.4) | copy-start | bytes 1966084
  135.7 1.4 copy-start.6
  137.1 4.9 %copy-start.7 = (bf16[1,10,128,256]{3,2,1,0:T(8,128)(2,1)S(1)}, bf16[1,10,128,256]{3,2,1,0:T(8,128)(2,1)}, u32[]{:S(2)}) copy-start(bf16[1,10,128,256]{3,2,1,0:T(8,128)(2,1)} %get-tuple-element.42) | copy-start | bytes 1966084
  137.1 4.9 %copy-start.8 = (bf16[1,10,128,256]{3,2,1,0:T(8,128)(2,1)S(1)}, bf16[1,10,128,256]{3,2,1,0:T(8,128)(2,1)}, u32[]{:S(2)}) copy-start(bf16[1,10,128,256]{3,2,1,0:T(8,128)(2,1)} %get-tuple-element.43) | copy-start | bytes 1966084
  143.8 1.1 copy-start.11
  143.8 1.1 copy-start.12

commit v6 on v5

--- a/solution.py
+++ b/solution.py
@@ -46,71 +46,85 @@
     ).astype(jnp.bfloat16)
 
 
-def _middle_kernel(fwd, bwd, bwd_at, keep_at, has_mixed_in, *refs):
+def _middle_kernel(fwd, bwd, bwd_at, keep_hidden, recompute, *refs):
     refs = list(refs)
     arrived, up, up_t, down, down_t = refs[:5]
     refs = refs[5:]
-    mixed_in = refs.pop(0) if has_mixed_in else None
+    if recompute:
+        gate_src, up_src = refs[0], refs[1]
+        refs = refs[2:]
     payload, grad_mixed = refs[0], refs[1]
-    rest = refs[2:]
-    hidden_out = rest.pop(0) if not has_mixed_in else None
-    keep_out = rest.pop(0) if keep_at is not None else None
-    for r in range(arrived.shape[0]):
-        gate = jnp.dot(up_t[0, r], arrived[r, :, :fwd], preferred_element_type=jnp.float32)
-        upper = jnp.dot(
-            up_t[1, r], arrived[r, :, fwd : 2 * fwd], preferred_element_type=jnp.float32
-        )
-        hidden = (gate / (1.0 + jnp.exp(-gate)) * upper).astype(jnp.bfloat16)
-        payload[r, :, :fwd] = jnp.dot(
-            down_t[r], hidden, preferred_element_type=jnp.float32
-        ).astype(jnp.bfloat16)
-        if hidden_out is not None:
-            hidden_out[r] = hidden
-        if keep_out is not None:
-            keep_out[0, r] = gate[:, keep_at : keep_at + bwd]
-            keep_out[1, r] = upper[:, keep_at : keep_at + bwd]
-        if has_mixed_in:
-            m0, m1 = mixed_in[0, r], mixed_in[1, r]
-        else:
-            m0, m1 = gate[:, bwd_at : bwd_at + bwd], upper[:, bwd_at : bwd_at + bwd]
-        grad_hidden = jnp.dot(
-            down[r], arrived[r, :, 2 * fwd :], preferred_element_type=jnp.float32
-        )
-        sg = 1.0 / (1.0 + jnp.exp(-m0))
-        gm0 = (grad_hidden * m1 * (sg * (1.0 + m0 * (1.0 - sg)))).astype(jnp.bfloat16)
-        gm1 = (grad_hidden * m0 * sg).astype(jnp.bfloat16)
-        grad_mixed[0, r] = gm0
-        grad_mixed[1, r] = gm1
-        payload[r, :, fwd : fwd + bwd] = jnp.dot(
-            up[0, r], gm0, preferred_element_type=jnp.float32
-        ).astype(jnp.bfloat16)
-        payload[r, :, fwd + bwd :] = jnp.dot(
-            up[1, r], gm1, preferred_element_type=jnp.float32
-        ).astype(jnp.bfloat16)
-
-
-def middle(arrived, up, up_t, down, down_t, fwd, bwd, bwd_at=0, keep_at=None, mixed_in=None):
+    hidden_out = refs[2] if keep_hidden else None
+    gate = jnp.dot(up_t[0, 0], arrived[0, :, :fwd], preferred_element_type=jnp.float32)
+    upper = jnp.dot(
+        up_t[1, 0], arrived[0, :, fwd : 2 * fwd], preferred_element_type=jnp.float32
+    )
+    hidden = (gate / (1.0 + jnp.exp(-gate)) * upper).astype(jnp.bfloat16)
+    payload[0, :, :fwd] = jnp.dot(
+        down_t[0], hidden, preferred_element_type=jnp.float32
+    ).astype(jnp.bfloat16)
+    if hidden_out is not None:
+        hidden_out[0] = hidden[:, bwd_at:]
+    if recompute:
+        m0 = jnp.dot(up_t[0, 0], gate_src[0], preferred_element_type=jnp.float32)
+        m1 = jnp.dot(up_t[1, 0], up_src[0], preferred_element_type=jnp.float32)
+    else:
+        m0, m1 = gate[:, bwd_at : bwd_at + bwd], upper[:, bwd_at : bwd_at + bwd]
+    grad_hidden = jnp.dot(down[0], arrived[0, :, 2 * fwd :], preferred_element_type=jnp.float32)
+    sg = 1.0 / (1.0 + jnp.exp(-m0))
+    gm0 = (grad_hidden * m1 * (sg * (1.0 + m0 * (1.0 - sg)))).astype(jnp.bfloat16)
+    gm1 = (grad_hidden * m0 * sg).astype(jnp.bfloat16)
+    grad_mixed[0, 0] = gm0
+    grad_mixed[1, 0] = gm1
+    payload[0, :, fwd : fwd + bwd] = jnp.dot(
+        up[0, 0], gm0, preferred_element_type=jnp.float32
+    ).astype(jnp.bfloat16)
+    payload[0, :, fwd + bwd :] = jnp.dot(
+        up[1, 0], gm1, preferred_element_type=jnp.float32
+    ).astype(jnp.bfloat16)
+
+
+def middle(arrived, up, up_t, down, down_t, fwd, bwd, bwd_at=0, keep_hidden=False, source=None):
     rb, pa, _ = arrived.shape
     o = up.shape[3]
     outs = [
         jax.ShapeDtypeStruct((rb, pa, fwd + 2 * bwd), jnp.bfloat16),
         jax.ShapeDtypeStruct((2, rb, o, bwd), jnp.bfloat16),
     ]
-    if mixed_in is None:
-        outs.append(jax.ShapeDtypeStruct((rb, o, fwd), jnp.bfloat16))
-    if keep_at is not None:
-        outs.append(jax.ShapeDtypeStruct((2, rb, o, bwd), jnp.float32))
-    ins = [arrived, up, up_t, down, down_t] + ([mixed_in] if mixed_in is not None else [])
-    flops = 2 * rb * o * pa * (3 * fwd + 3 * bwd)
-    bytes_accessed = sum(x.size * x.dtype.itemsize for x in ins) + sum(
+    out_specs = [
+        pl.BlockSpec((1, pa, fwd + 2 * bwd), lambda r: (r, 0, 0)),
+        pl.BlockSpec((2, 1, o, bwd), lambda r: (0, r, 0, 0)),
+    ]
+    if keep_hidden:
+        outs.append(jax.ShapeDtypeStruct((rb, o, fwd - bwd_at), jnp.bfloat16))
+        out_specs.append(pl.BlockSpec((1, o, fwd - bwd_at), lambda r: (r, 0, 0)))
+    ins = [arrived, up, up_t, down, down_t]
+    in_specs = [
+        pl.BlockSpec((1, pa, arrived.shape[2]), lambda r: (r, 0, 0)),
+        pl.BlockSpec((2, 1) + up.shape[2:], lambda r: (0, r, 0, 0)),
+        pl.BlockSpec((2, 1) + up_t.shape[2:], lambda r: (0, r, 0, 0)),
+        pl.BlockSpec((1,) + down.shape[1:], lambda r: (r, 0, 0)),
+        pl.BlockSpec((1,) + down_t.shape[1:], lambda r: (r, 0, 0)),
+    ]
+    if source is not None:
+        held, gate_block, up_block = source
+        ins += [held, held]
+        in_specs += [
+            pl.BlockSpec((1, pa, bwd), lambda r, b=gate_block: (r, 0, b)),
+            pl.BlockSpec((1, pa, bwd), lambda r, b=up_block: (r, 0, b)),
+        ]
+    flops = 2 * rb * o * pa * (3 * fwd + (5 if source is not None else 3) * bwd)
+    bytes_accessed = sum(x.size * x.dtype.itemsize for x in ins[:5]) + sum(
         math.prod(s.shape) * s.dtype.itemsize for s in outs
     )
-    vmem = pltpu.MemorySpace.VMEM
     return pl.pallas_call(
-        functools.partial(_middle_kernel, fwd, bwd, bwd_at, keep_at, mixed_in is not None),
+        functools.partial(
+            _middle_kernel, fwd, bwd, bwd_at, keep_hidden, source is not None
+        ),
         out_shape=tuple(outs),
-        in_specs=[pl.BlockSpec(memory_space=vmem)] * len(ins),
-        out_specs=tuple(pl.BlockSpec(memory_space=vmem) for _ in outs),
+        grid=(rb,),
+        in_specs=in_specs,
+        out_specs=tuple(out_specs),
         cost_estimate=pl.CostEstimate(
             flops=flops, transcendentals=rb * o * (fwd + bwd), bytes_accessed=bytes_accessed
         ),
@@ -161,8 +175,8 @@
     glow_1 = lowered_grad_of(first_grads, down_second)
     payload = jnp.concatenate([spread_a.reshape(pb, SECOND_BLOCKS, 6 * t), glow_1], axis=2)
     arrived_a = jnp.swapaxes(to_blocks(payload), 0, 1)
-    payload_a, gmix_1, hidden_a, mixed_s1 = middle(
-        arrived_a, *weights, fwd=3 * t, bwd=t, bwd_at=t, keep_at=2 * t
+    payload_a, gmix_1, hidden_both = middle(
+        arrived_a, *weights, fwd=3 * t, bwd=t, bwd_at=t, keep_hidden=True
     )
     back = to_features(payload_a)
     lowered_ap = back[:, :, : 3 * t]
@@ -181,7 +195,7 @@
     glow_2 = lowered_grad_of(grads, down_second)
     payload = jnp.concatenate([spread_b.reshape(pb, SECOND_BLOCKS, 2 * t), glow_2], axis=2)
     arrived_b = jnp.swapaxes(to_blocks(payload), 0, 1)
-    payload_b, gmix_2 = middle(arrived_b, *weights, fwd=t, bwd=t, mixed_in=mixed_s1)
+    payload_b, gmix_2 = middle(arrived_b, *weights, fwd=t, bwd=t, source=(arrived_a, 2, 5))
     back = to_features(payload_b)
     outputs = output_of(inputs, back[:, :, :t], down_second)
     gspread_2p = back[:, :, t:].reshape(SECOND_BLOCKS, pb, 2, t)
@@ -193,7 +207,6 @@
         [arrived_a[:, :, t : 3 * t], arrived_a[:, :, 4 * t : 6 * t]]
     )
     gmix_both = jnp.concatenate([gmix_1, gmix_2], axis=3)
-    hidden_both = hidden_a[:, :, t:]
     glow_both = jnp.concatenate([arrived_a[:, :, 6 * t :], arrived_b[:, :, 2 * t :]], axis=2)
     lowered_both = lowered_ap[:, :, t:]
     grads_both = jnp.concatenate([first_grads, grads], axis=2)

time: 158 us -> 163 us (1.032)
  Pallas kernels: 13.1 us -> 18.1 us
  local copies, waits for them, and re-layouts: 34.4 us -> 32.5 us
    pallas_call x2, Pallas kernels: 13.1 us -> 18.1 us  [middle(): pl.pallas_call(functools.partial(_middle_kernel, fwd, bwd, bwd_at, keep_h...]
  transfers between devices with their start and end apart: 5 -> 5, of which waited for: 4 -> 4; matrix products, arithmetic and copies ran while one was open for 12% -> 11% of each run, Pallas kernels for 0% -> 0%
where the time goes in v6:
time: 163 us; the launch traced here: 162 us
  waiting for transfers between devices  60.3 us (37%)
  local copies, waits for them, and re-layouts  32.5 us (20%)
  blocking collectives  20.5 us (13%)
  starting transfers between devices  19.6 us (12%)
  Pallas kernels  18.1 us (11%)
  matrix products  9.73 us (6%)
    all_to_all x1, waiting for transfers between devices, to_blocks(): lax.all_to_all(pieces, 'blk', split_axis=1, concat_axis=0, tiled=True)  28.8 us
    all_to_all x2, waiting for transfers between devices, to_features(): lax.all_to_all(grouped, 'blk', split_axis=0, concat_axis=0, tiled=True)  28.5 us
    all_to_all x1, blocking collectives, to_blocks(): lax.all_to_all(pieces, 'blk', split_axis=1, concat_axis=0, tiled=True)  20.5 us
    pallas_call x2, Pallas kernels, middle(): pl.pallas_call(functools.partial(_middle_kernel, fwd, bwd, bwd_at, keep_h...  18.1 us
    all_to_all x2, starting transfers between devices, to_features(): lax.all_to_all(grouped, 'blk', split_axis=0, concat_axis=0, tiled=True)  8.24 us
    all_to_all x1, starting transfers between devices, to_blocks(): lax.all_to_all(pieces, 'blk', split_axis=1, concat_axis=0, tiled=True)  7.03 us
    transpose x2, local copies, waits for them, and re-layouts, to_features(): grouped = pieces.reshape(r_local, groups, p_local, n).transpose(1, 0, 2, 3)  5.28 us
    ppermute x2, starting transfers between devices, from_behind(): return lax.ppermute(value, axis, pairs)  4.33 us
  transfers between devices with their start and end apart: 5, of which 4 were waited for; matrix products, arithmetic and copies ran while one was open for 11% of the time, Pallas kernels for 0%

profile of v6, /device:TPU:224, one launch (start us, length us, event | category | flops | bytes accessed | tf_op | source)
XLA Modules:
  0.0 162.0 jit_solution(12591119464103534658)
XLA Ops:
  0.6 1.4 reshape_squeeze.27
  3.1 1.6 convert_bitcast_fusion
  6.6 2.2 %copy.94 = bf16[8,160,896]{2,0,1:T(8,128)(2,1)} copy(bf16[8,160,896]{2,1,0:T(8,128)(2,1)S(1)} %pad_maximum_fusion) | data formatting | bytes 4587520 | tf_op jit(solution)/shard_map/concatenate | solution.py:176
  8.7 7.0 %all-to-all-start = ((bf16[8,160,896]{2,0,1:T(8,128)(2,1)}), bf16[8,160,896]{2,0,1:T(8,128)(2,1)S(1)}, u32[]{:S(2)}, u32[]{:S(2)}) async-start(bf16[8,160,896]{2,0,1:T(8,128)(2,1)} %copy.94), calls=%async_computation | async-start | bytes 4587520 | tf_op jit(solution)/shard_map/all_to_all | solution.py:25
  15.8 2.3 %reshape_squeeze.30 = bf16[2,10,128,128]{3,2,0,1:T(8,128)(2,1)S(1)} reshape(bf16[1,2,10,16384]{3,1,2,0:T(2,128)(2,1)} %param.15) | data formatting | bytes 1310720 | tf_op jit(solution)/shard_map/reshape;squeeze | solution.py:161
  21.5 28.8 %all-to-all-done = bf16[8,160,896]{2,0,1:T(8,128)(2,1)S(1)} async-done(((bf16[8,160,896]{2,0,1:T(8,128)(2,1)}), bf16[8,160,896]{2,0,1:T(8,128)(2,1)S(1)}, u32[]{:S(2)}, u32[]{:S(2)}) %all-to-all-start) | async-done | bytes 2293792 | tf_op jit(solution)/shard_map/all_to_all | solution.py:25
  50.3 1.7 %copy.165 = bf16[16,8,10,896]{3,1,0,2:T(8,128)(2,1)} copy(bf16[16,8,10,896]{3,1,2,0:T(8,128)(2,1)S(1)} %bitcast.127) | data formatting | bytes 4587520 | tf_op jit(solution)/shard_map/all_to_all | solution.py:25
  52.0 9.4 %shard_map.136 = (bf16[10,128,640]{2,1,0:T(8,128)(2,1)}, bf16[2,10,128,128]{3,2,1,0:T(8,128)(2,1)}, bf16[10,128,256]{2,1,0:T(8,128)(2,1)}) custom-call(bf16[10,128,896]{2,1,0:T(8,128)(2,1)} %bitcast.122, bf16[2,10,128,128]{3,2,1,0:T(8,128)(2,1)} %copy.98.refs_1_, bf16[2,10,128,128]{3,2,1,0:T(8,128)(2,1)} %bitcast.131, bf16[10,128,128]{2,1,0:T(8,128)(2,1)} %copy-done.1, ...), custom_call_target="tpu_custom_call" | custom-call | flops 503316480 | bytes 7208960 | tf_op jit(solution)/shard_map/pallas_call | solution.py:120
  61.5 2.8 %copy_bitcast_fusion.1 = bf16[16,10,8,640]{3,2,1,0:T(8,128)(2,1)} fusion(bf16[10,128,640]{2,1,0:T(8,128)(2,1)} %get-tuple-element.11), kind=kLoop, calls=%fused_computation.3 | loop fusion | bytes 3276800 | tf_op jit(solution)/shard_map/transpose | solution.py:32
  64.3 3.7 %all-to-all-start.1 = ((bf16[16,10,8,640]{3,2,1,0:T(8,128)(2,1)}), bf16[16,10,8,640]{3,2,1,0:T(8,128)(2,1)S(1)}, u32[]{:S(2)}, u32[]{:S(2)}) async-start(bf16[16,10,8,640]{3,2,1,0:T(8,128)(2,1)} %copy_bitcast_fusion.1), calls=%async_computation.1 | async-start | bytes 3276800 | tf_op jit(solution)/shard_map/all_to_all | solution.py:33
  68.0 23.6 %all-to-all-done.1 = bf16[16,10,8,640]{3,2,1,0:T(8,128)(2,1)S(1)} async-done(((bf16[16,10,8,640]{3,2,1,0:T(8,128)(2,1)}), bf16[16,10,8,640]{3,2,1,0:T(8,128)(2,1)S(1)}, u32[]{:S(2)}, u32[]{:S(2)}) %all-to-all-start.1) | async-done | bytes 1638432 | tf_op jit(solution)/shard_map/all_to_all | solution.py:33
  93.0 1.9 %collective-permute-start.1 = (bf16[8,40,128]{2,1,0:T(8,128)(2,1)S(1)}, bf16[8,40,128]{2,1,0:T(8,128)(2,1)S(1)}, u32[]{:S(2)}, u32[]{:S(2)}) collective-permute-start(bf16[8,40,128]{2,1,0:T(8,128)(2,1)S(1)} %fusion.26), channel_id=1, source_target_pairs={{16,0},{32,16},{48,32},{64,48},{80,64},{96,80},{112,96},{128,112},... | collective-permute-start | bytes 245768 | tf_op jit(solution)/shard_map/ppermute | solution.py:21
  95.2 2.4 %collective-permute-start = (bf16[8,40,128]{2,1,0:T(8,128)(2,1)S(1)}, bf16[8,40,128]{2,1,0:T(8,128)(2,1)S(1)}, u32[]{:S(2)}, u32[]{:S(2)}) collective-permute-start(bf16[8,40,128]{2,1,0:T(8,128)(2,1)S(1)} %fusion.27), channel_id=1, source_target_pairs={{0,16},{16,32},{32,48},{48,64},{64,80},{80,96},{96,112},{112,128},... | collective-permute-start | bytes 245768 | tf_op jit(solution)/shard_map/ppermute | solution.py:21
  97.9 3.1 %collective-permute-done = bf16[8,40,128]{2,1,0:T(8,128)(2,1)S(1)} collective-permute-done((bf16[8,40,128]{2,1,0:T(8,128)(2,1)S(1)}, bf16[8,40,128]{2,1,0:T(8,128)(2,1)S(1)}, u32[]{:S(2)}, u32[]{:S(2)}) %collective-permute-start) | collective-permute-done | bytes 81952 | tf_op jit(solution)/shard_map/ppermute | solution.py:21
  101.9 20.5 %all_to_all.46 = bf16[8,160,384]{2,0,1:T(8,128)(2,1)S(1)} all-to-all(bf16[8,160,384]{2,0,1:T(8,128)(2,1)S(1)} %copy.107), channel_id=1, replica_groups=mesh['section'=32,'blk'=16] {'blk'}, dimensions={1} | all-to-all | bytes 1966080 | tf_op jit(solution)/shard_map/all_to_all | solution.py:25
  123.6 8.6 %shard_map.137 = (bf16[10,128,384]{2,1,0:T(8,128)(2,1)}, bf16[2,10,128,128]{3,2,1,0:T(8,128)(2,1)}) custom-call(bf16[10,128,384]{2,1,0:T(8,128)(2,1)} %bitcast.133, bf16[2,10,128,128]{3,2,1,0:T(8,128)(2,1)} %copy.98.refs_1_, bf16[2,10,128,128]{3,2,1,0:T(8,128)(2,1)} %bitcast.132, bf16[10,128,128]{2,1,0:T(8,128)(2,1)} %copy-done.1, ...), custom_call_target="tpu_custom_call" | custom-call | flops 335544320 | bytes 4587520 | tf_op jit(solution)/shard_map/pallas_call | solution.py:120
  132.3 2.4 %copy_bitcast_fusion.2 = bf16[16,10,8,384]{3,2,1,0:T(8,128)(2,1)} fusion(bf16[10,128,384]{2,1,0:T(8,128)(2,1)} %get-tuple-element.12), kind=kLoop, calls=%fused_computation.37 | loop fusion | bytes 1966080 | tf_op jit(solution)/shard_map/transpose | solution.py:32
  134.7 4.5 %all-to-all-start.3 = ((bf16[16,10,8,384]{3,2,1,0:T(8,128)(2,1)}), bf16[16,10,8,384]{3,2,1,0:T(8,128)(2,1)}, u32[]{:S(2)}, u32[]{:S(2)}) async-start(bf16[16,10,8,384]{3,2,1,0:T(8,128)(2,1)} %copy_bitcast_fusion.2), calls=%async_computation.3 | async-start | bytes 1966080 | tf_op jit(solution)/shard_map/all_to_all | solution.py:33
  140.0 1.2 slice_bitcast_fusion.1
  144.2 2.2 %fusion.15 = bf16[10,128,128]{2,1,0:T(8,128)(2,1)} fusion(bf16[10,128,256]{2,1,0:T(8,128)(2,1)} %get-tuple-element.15, bf16[10,128,128]{2,1,0:T(8,128)(2,1)S(1)} %slice.54, bf16[10,128,128]{2,1,0:T(8,128)(2,1)S(1)} %copy-done.12), kind=kOutput, calls=%fused_computation.20 | convolution fusion | flops 85524480 | bytes 1638400 | tf_op jit(solution)/shard_map/rot,rpt->rop/dot_general | solution.py:219
  146.3 2.0 %reshape.74 = bf16[1,10,16384]{2,1,0:T(8,128)(2,1)} reshape(bf16[10,128,128]{2,1,0:T(8,128)(2,1)} %fusion.15) | data formatting | bytes 655360 | tf_op jit(solution)/shard_map/reshape | solution.py:231
  148.3 1.8 %fusion = bf16[2,10,128,128]{3,2,1,0:T(8,128)(2,1)S(1)} fusion(bf16[1,10,128,256]{3,2,1,0:T(8,128)(2,1)S(1)} %copy-done.8, bf16[1,10,128,256]{3,2,1,0:T(8,128)(2,1)S(1)} %copy-done.7, bf16[2,10,128,128]{3,2,1,0:T(8,128)(2,1)} %get-tuple-element.14, bf16[2,10,128,128]{3,2,1,0:T(8,128)(2,1)} %get-tuple-element.13), kind=kOutput, calls=%fused_computation.5 | convolution fusion | flops 171704320 | bytes 3276800 | tf_op jit(solution)/shard_map/grpt,grot->grpo/dot_general | solution.py:216
  151.1 4.9 %all-to-all-done.3 = bf16[16,10,8,384]{3,2,1,0:T(8,128)(2,1)} async-done(((bf16[16,10,8,384]{3,2,1,0:T(8,128)(2,1)}), bf16[16,10,8,384]{3,2,1,0:T(8,128)(2,1)}, u32[]{:S(2)}, u32[]{:S(2)}) %all-to-all-start.3) | async-done | bytes 983072 | tf_op jit(solution)/shard_map/all_to_all | solution.py:33
  156.1 1.2 slice_bitcast_fusion.2
  (69 shorter events, 19.8 us)
Async XLA Ops:
  2.0 2.7 %copy-start.2 = (bf16[2,8,40,160]{3,2,1,0:T(8,128)(2,1)}, bf16[2,8,40,160]{3,2,1,0:T(8,128)(2,1)S(1)}, u32[]{:S(2)}) copy-start(bf16[2,8,40,160]{3,2,1,0:T(8,128)(2,1)S(1)} %reshape_squeeze.27) | copy-start | bytes 614404
  4.7 0.9 copy-start.13
  4.7 1.4 copy-start.15
  8.7 41.6 %all-to-all-start = ((bf16[8,160,896]{2,0,1:T(8,128)(2,1)}), bf16[8,160,896]{2,0,1:T(8,128)(2,1)S(1)}, u32[]{:S(2)}, u32[]{:S(2)}) async-start(bf16[8,160,896]{2,0,1:T(8,128)(2,1)} %copy.94), calls=%async_computation | async-start | bytes 4587520 | tf_op jit(solution)/shard_map/all_to_all | solution.py:25
  19.2 1.3 copy-start.9
  20.6 31.4 %copy-start.1 = (bf16[10,128,128]{2,1,0:T(8,128)(2,1)}, bf16[10,128,128]{2,1,0:T(8,128)(2,1)S(1)}, u32[]{:S(2)}) copy-start(bf16[10,128,128]{2,1,0:T(8,128)(2,1)S(1)} %slice.56.refs_3_) | copy-start | bytes 983044
  64.3 27.3 %all-to-all-start.1 = ((bf16[16,10,8,640]{3,2,1,0:T(8,128)(2,1)}), bf16[16,10,8,640]{3,2,1,0:T(8,128)(2,1)S(1)}, u32[]{:S(2)}, u32[]{:S(2)}) async-start(bf16[16,10,8,640]{3,2,1,0:T(8,128)(2,1)} %copy_bitcast_fusion.1), calls=%async_computation.1 | async-start | bytes 3276800 | tf_op jit(solution)/shard_map/all_to_all | solution.py:33
  91.6 1.0 copy-start.3
  92.6 5.3 %copy-start.4 = (bf16[160,8,2,128]{3,1,2,0:T(8,128)(2,1)}, bf16[160,8,2,128]{3,1,2,0:T(8,128)(2,1)S(1)}, u32[]{:S(2)}) copy-start(bf16[160,8,2,128]{3,1,2,0:T(8,128)(2,1)S(1)} %get-tuple-element.43) | copy-start | bytes 1966084
  92.6 2.3 %copy-start.10 = (bf16[1,320,128]{2,1,0:T(8,128)(2,1)S(1)}, bf16[1,320,128]{2,1,0:T(8,128)(2,1)}, u32[]{:S(2)}) copy-start(bf16[1,320,128]{2,1,0:T(8,128)(2,1)} %param.9) | copy-start | bytes 245764
  92.6 5.0 %copy-start.14 = (bf16[320,128]{1,0:T(8,128)(2,1)S(1)}, bf16[320,128]{1,0:T(8,128)(2,1)}, u32[]{:S(2)}) copy-start(bf16[320,128]{1,0:T(8,128)(2,1)} %param.13) | copy-start | bytes 245764
  92.6 8.3 %copy-start.11 = (bf16[320,128]{1,0:T(8,128)(2,1)S(1)}, bf16[320,128]{1,0:T(8,128)(2,1)}, u32[]{:S(2)}) copy-start(bf16[320,128]{1,0:T(8,128)(2,1)} %param.10) | copy-start | bytes 245764
  93.0 4.6 %collective-permute-start.1 = (bf16[8,40,128]{2,1,0:T(8,128)(2,1)S(1)}, bf16[8,40,128]{2,1,0:T(8,128)(2,1)S(1)}, u32[]{:S(2)}, u32[]{:S(2)}) collective-permute-start(bf16[8,40,128]{2,1,0:T(8,128)(2,1)S(1)} %fusion.26), channel_id=1, source_target_pairs={{16,0},{32,16},{48,32},{64,48},{80,64},{96,80},{112,96},{128,112},... | collective-permute-start | bytes 245768 | tf_op jit(solution)/shard_map/ppermute | solution.py:21
  95.2 5.8 %collective-permute-start = (bf16[8,40,128]{2,1,0:T(8,128)(2,1)S(1)}, bf16[8,40,128]{2,1,0:T(8,128)(2,1)S(1)}, u32[]{:S(2)}, u32[]{:S(2)}) collective-permute-start(bf16[8,40,128]{2,1,0:T(8,128)(2,1)S(1)} %fusion.27), channel_id=1, source_target_pairs={{0,16},{16,32},{32,48},{48,64},{64,80},{80,96},{96,112},{112,128},... | collective-permute-start | bytes 245768 | tf_op jit(solution)/shard_map/ppermute | solution.py:21
  132.3 7.0 %copy-start = (bf16[16,8,10,896]{3,1,0,2:T(8,128)(2,1)S(1)}, bf16[16,8,10,896]{3,1,0,2:T(8,128)(2,1)}, u32[]{:S(2)}) copy-start(bf16[16,8,10,896]{3,1,0,2:T(8,128)(2,1)} %copy.165) | copy-start | bytes 6881284
  134.7 21.4 %all-to-all-start.3 = ((bf16[16,10,8,384]{3,2,1,0:T(8,128)(2,1)}), bf16[16,10,8,384]{3,2,1,0:T(8,128)(2,1)}, u32[]{:S(2)}, u32[]{:S(2)}) async-start(bf16[16,10,8,384]{3,2,1,0:T(8,128)(2,1)} %copy_bitcast_fusion.2), calls=%async_computation.3 | async-start | bytes 1966080 | tf_op jit(solution)/shard_map/all_to_all | solution.py:33
  139.2 2.0 %copy-start.5 = (bf16[160,8,2,128]{3,1,2,0:T(8,128)(2,1)S(1)}, bf16[160,8,2,128]{3,1,2,0:T(8,128)(2,1)}, u32[]{:S(2)}) copy-start(bf16[160,8,2,128]{3,1,2,0:T(8,128)(2,1)} %copy-done.4) | copy-start | bytes 1966084
  140.0 1.4 copy-start.6
  141.4 2.7 %copy-start.12 = (bf16[10,128,128]{2,1,0:T(8,128)(2,1)S(1)}, bf16[10,128,128]{2,1,0:T(8,128)(2,1)}, u32[]{:S(2)}) copy-start(bf16[10,128,128]{2,1,0:T(8,128)(2,1)} %slice.53) | copy-start | bytes 983044
  143.1 5.2 %copy-start.7 = (bf16[1,10,128,256]{3,2,1,0:T(8,128)(2,1)S(1)}, bf16[1,10,128,256]{3,2,1,0:T(8,128)(2,1)}, u32[]{:S(2)}) copy-start(bf16[1,10,128,256]{3,2,1,0:T(8,128)(2,1)} %get-tuple-element.40) | copy-start | bytes 1966084
  143.1 5.2 %copy-start.8 = (bf16[1,10,128,256]{3,2,1,0:T(8,128)(2,1)S(1)}, bf16[1,10,128,256]{3,2,1,0:T(8,128)(2,1)}, u32[]{:S(2)}) copy-start(bf16[1,10,128,256]{3,2,1,0:T(8,128)(2,1)} %get-tuple-element.41) | copy-start | bytes 1966084

commit v7 on v5

--- a/solution.py
+++ b/solution.py
@@ -25,11 +25,8 @@
     return lax.all_to_all(pieces, "blk", split_axis=1, concat_axis=0, tiled=True)
 
 
-def to_features(pieces):
-    groups = lax.axis_size("blk")
-    r_local, p_all, n = pieces.shape
-    p_local = p_all // groups
-    grouped = pieces.reshape(r_local, groups, p_local, n).transpose(1, 0, 2, 3)
+def to_features(grouped):
+    groups, r_local, p_local, n = grouped.shape
     arrived = lax.all_to_all(grouped, "blk", split_axis=0, concat_axis=0, tiled=True)
     return arrived.reshape(groups * r_local, p_local, n)
 
@@ -44,6 +41,15 @@
     return jnp.einsum(
         "pqt,prq->prt", grads, down_second, preferred_element_type=jnp.float32
     ).astype(jnp.bfloat16)
+
+
+def put(payload, r, at, value):
+    rows = payload.shape[2]
+    width = value.shape[1]
+    for group in range(payload.shape[0]):
+        payload[group, r, :, at : at + width] = value[group * rows : (group + 1) * rows].astype(
+            payload.dtype
+        )
 
 
 def _middle_kernel(fwd, bwd, bwd_at, keep_at, has_mixed_in, *refs):
@@ -61,9 +67,7 @@
             up_t[1, r], arrived[r, :, fwd : 2 * fwd], preferred_element_type=jnp.float32
         )
         hidden = (gate / (1.0 + jnp.exp(-gate)) * upper).astype(jnp.bfloat16)
-        payload[r, :, :fwd] = jnp.dot(
-            down_t[r], hidden, preferred_element_type=jnp.float32
-        ).astype(jnp.bfloat16)
+        put(payload, r, 0, jnp.dot(down_t[r], hidden, preferred_element_type=jnp.float32))
         if hidden_out is not None:
             hidden_out[r] = hidden
         if keep_out is not None:
@@ -81,19 +85,16 @@
         gm1 = (grad_hidden * m0 * sg).astype(jnp.bfloat16)
         grad_mixed[0, r] = gm0
         grad_mixed[1, r] = gm1
-        payload[r, :, fwd : fwd + bwd] = jnp.dot(
-            up[0, r], gm0, preferred_element_type=jnp.float32
-        ).astype(jnp.bfloat16)
-        payload[r, :, fwd + bwd :] = jnp.dot(
-            up[1, r], gm1, preferred_element_type=jnp.float32
-        ).astype(jnp.bfloat16)
+        put(payload, r, fwd, jnp.dot(up[0, r], gm0, preferred_element_type=jnp.float32))
+        put(payload, r, fwd + bwd, jnp.dot(up[1, r], gm1, preferred_element_type=jnp.float32))
 
 
 def middle(arrived, up, up_t, down, down_t, fwd, bwd, bwd_at=0, keep_at=None, mixed_in=None):
     rb, pa, _ = arrived.shape
     o = up.shape[3]
+    groups = lax.axis_size("blk")
     outs = [
-        jax.ShapeDtypeStruct((rb, pa, fwd + 2 * bwd), jnp.bfloat16),
+        jax.ShapeDtypeStruct((groups, rb, pa // groups, fwd + 2 * bwd), jnp.bfloat16),
         jax.ShapeDtypeStruct((2, rb, o, bwd), jnp.bfloat16),
     ]
     if mixed_in is None:

time: 158 us -> 153 us (0.968)
  local copies, waits for them, and re-layouts: 34.4 us -> 29.3 us
    transpose x2 -> x0, local copies, waits for them, and re-layouts: 5.13 us -> none  [to_features(): grouped = pieces.reshape(r_local, groups, p_local, n).transpose(1, 0, 2, 3)]
  transfers between devices with their start and end apart: 5 -> 5, of which waited for: 4 -> 4; matrix products, arithmetic and copies ran while one was open for 12% -> 13% of each run, Pallas kernels for 0% -> 0%
where the time goes in v7:
time: 153 us; the launch traced here: 152 us
  waiting for transfers between devices  59 us (39%)
  local copies, waits for them, and re-layouts  29.3 us (19%)
  blocking collectives  20.5 us (13%)
  starting transfers between devices  19.6 us (13%)
  Pallas kernels  13.2 us (9%)
  matrix products  9.64 us (6%)
    all_to_all x1, waiting for transfers between devices, to_blocks(): lax.all_to_all(pieces, 'blk', split_axis=1, concat_axis=0, tiled=True)  28.1 us
    all_to_all x2, waiting for transfers between devices, to_features(): lax.all_to_all(grouped, 'blk', split_axis=0, concat_axis=0, tiled=True)  27.8 us
    all_to_all x1, blocking collectives, to_blocks(): lax.all_to_all(pieces, 'blk', split_axis=1, concat_axis=0, tiled=True)  20.5 us
    pallas_call x2, Pallas kernels, middle(): pl.pallas_call(functools.partial(_middle_kernel, fwd, bwd, bwd_at, keep_a...  13.2 us
    all_to_all x2, starting transfers between devices, to_features(): lax.all_to_all(grouped, 'blk', split_axis=0, concat_axis=0, tiled=True)  8.21 us
    all_to_all x1, starting transfers between devices, to_blocks(): lax.all_to_all(pieces, 'blk', split_axis=1, concat_axis=0, tiled=True)  7.04 us
    ppermute x2, starting transfers between devices, from_behind(): return lax.ppermute(value, axis, pairs)  4.33 us
    another operation x3, local copies, waits for them, and re-layouts, shards(): up_second = second_up[0].reshape(2, rb, FIRST_BLOCKS, BLOCK)  4.3 us
  transfers between devices with their start and end apart: 5, of which 4 were waited for; matrix products, arithmetic and copies ran while one was open for 13% of the time, Pallas kernels for 0%

profile of v7, /device:TPU:224, one launch (start us, length us, event | category | flops | bytes accessed | tf_op | source)
XLA Modules:
  0.0 152.4 jit_solution(7436281154641752786)
XLA Ops:
  1.6 1.4 reshape_squeeze.27
  3.0 1.6 %reshape_squeeze.28 = bf16[8,160,40]{2,1,0:T(8,128)(2,1)S(1)} reshape(bf16[1,8,6400]{2,1,0:T(8,128)(2,1)} %param.17) | data formatting | bytes 204800 | tf_op jit(solution)/shard_map/reshape;squeeze | solution.py:150
  4.5 1.6 %convert_bitcast_fusion = bf16[8,2,20,8,384]{4,3,2,1,0:T(8,128)(2,1)S(1)} fusion(bf16[8,40,128]{2,1,0:T(8,128)(2,1)S(1)} %bitcast.134, bf16[8,40,128]{2,1,0:T(8,128)(2,1)S(1)} %bitcast.132, bf16[8,40,128]{2,1,0:T(8,128)(2,1)} %bitcast.128, bf16[2,8,40,160]{3,2,1,0:T(8,128)(2,1)S(1)} %reshape_squeeze.27), kind=kOutput, calls=%fused_computation.2 | convolution fusion | flops 80363520 | bytes 2416640 | tf_op jit(solution)/shard_map/pqt,gpqr->prgt/dot_general | solution.py:35
  7.4 2.2 %copy.63 = bf16[8,160,896]{2,0,1:T(8,128)(2,1)} copy(bf16[8,160,896]{2,1,0:T(8,128)(2,1)S(1)} %pad_maximum_fusion) | data formatting | bytes 4587520 | tf_op jit(solution)/shard_map/concatenate | solution.py:163
  9.6 7.0 %all-to-all-start = ((bf16[8,160,896]{2,0,1:T(8,128)(2,1)}), bf16[8,160,896]{2,0,1:T(8,128)(2,1)S(1)}, u32[]{:S(2)}, u32[]{:S(2)}) async-start(bf16[8,160,896]{2,0,1:T(8,128)(2,1)} %copy.63), calls=%async_computation | async-start | bytes 4587520 | tf_op jit(solution)/shard_map/all_to_all | solution.py:25
  16.6 2.3 %reshape_squeeze.30 = bf16[2,10,128,128]{3,2,0,1:T(8,128)(2,1)S(1)} reshape(bf16[1,2,10,16384]{3,1,2,0:T(2,128)(2,1)} %param.15) | data formatting | bytes 1310720 | tf_op jit(solution)/shard_map/reshape;squeeze | solution.py:148
  21.0 1.1 copy.102
  23.0 28.1 %all-to-all-done = bf16[8,160,896]{2,0,1:T(8,128)(2,1)S(1)} async-done(((bf16[8,160,896]{2,0,1:T(8,128)(2,1)}), bf16[8,160,896]{2,0,1:T(8,128)(2,1)S(1)}, u32[]{:S(2)}, u32[]{:S(2)}) %all-to-all-start) | async-done | bytes 2293792 | tf_op jit(solution)/shard_map/all_to_all | solution.py:25
  51.2 1.7 %copy.130 = bf16[16,8,10,896]{3,1,0,2:T(8,128)(2,1)} copy(bf16[16,8,10,896]{3,1,2,0:T(8,128)(2,1)S(1)} %bitcast.114) | data formatting | bytes 4587520 | tf_op jit(solution)/shard_map/all_to_all | solution.py:25
  52.9 7.8 %shard_map.136 = (bf16[16,10,8,640]{3,2,1,0:T(8,128)(2,1)}, bf16[2,10,128,128]{3,2,1,0:T(8,128)(2,1)}, bf16[10,128,384]{2,1,0:T(8,128)(2,1)}, f32[2,10,128,128]{3,2,1,0:T(8,128)}) custom-call(bf16[10,128,896]{2,1,0:T(8,128)(2,1)} %bitcast.111, bf16[2,10,128,128]{3,2,1,0:T(8,128)(2,1)} %copy.67.refs_1_, bf16[2,10,128,128]{3,2,1,0:T(8,128)(2,1)} %bitcast.118, ...), custom_call_target="tpu_custom_call" | custom-call | flops 503316480 | bytes 8847360 | tf_op jit(solution)/shard_map/pallas_call | solution.py:110
  60.7 3.7 %all-to-all-start.1 = ((bf16[16,10,8,640]{3,2,1,0:T(8,128)(2,1)}), bf16[16,10,8,640]{3,2,1,0:T(8,128)(2,1)S(1)}, u32[]{:S(2)}, u32[]{:S(2)}) async-start(bf16[16,10,8,640]{3,2,1,0:T(8,128)(2,1)} %get-tuple-element.12), calls=%async_computation.1 | async-start | bytes 3276800 | tf_op jit(solution)/shard_map/all_to_all | solution.py:30
  64.4 23.6 %all-to-all-done.1 = bf16[16,10,8,640]{3,2,1,0:T(8,128)(2,1)S(1)} async-done(((bf16[16,10,8,640]{3,2,1,0:T(8,128)(2,1)}), bf16[16,10,8,640]{3,2,1,0:T(8,128)(2,1)S(1)}, u32[]{:S(2)}, u32[]{:S(2)}) %all-to-all-start.1) | async-done | bytes 1638432 | tf_op jit(solution)/shard_map/all_to_all | solution.py:30
  89.4 1.9 %collective-permute-start.1 = (bf16[8,40,128]{2,1,0:T(8,128)(2,1)S(1)}, bf16[8,40,128]{2,1,0:T(8,128)(2,1)S(1)}, u32[]{:S(2)}, u32[]{:S(2)}) collective-permute-start(bf16[8,40,128]{2,1,0:T(8,128)(2,1)S(1)} %fusion.26), channel_id=1, source_target_pairs={{16,0},{32,16},{48,32},{64,48},{80,64},{96,80},{112,96},{128,112},... | collective-permute-start | bytes 245768 | tf_op jit(solution)/shard_map/ppermute | solution.py:21
  91.6 2.4 %collective-permute-start = (bf16[8,40,128]{2,1,0:T(8,128)(2,1)S(1)}, bf16[8,40,128]{2,1,0:T(8,128)(2,1)S(1)}, u32[]{:S(2)}, u32[]{:S(2)}) collective-permute-start(bf16[8,40,128]{2,1,0:T(8,128)(2,1)S(1)} %fusion.27), channel_id=1, source_target_pairs={{0,16},{16,32},{32,48},{48,64},{64,80},{80,96},{96,112},{112,128},... | collective-permute-start | bytes 245768 | tf_op jit(solution)/shard_map/ppermute | solution.py:21
  94.3 3.1 %collective-permute-done = bf16[8,40,128]{2,1,0:T(8,128)(2,1)S(1)} collective-permute-done((bf16[8,40,128]{2,1,0:T(8,128)(2,1)S(1)}, bf16[8,40,128]{2,1,0:T(8,128)(2,1)S(1)}, u32[]{:S(2)}, u32[]{:S(2)}) %collective-permute-start) | collective-permute-done | bytes 81952 | tf_op jit(solution)/shard_map/ppermute | solution.py:21
  98.4 20.5 %all_to_all.46 = bf16[8,160,384]{2,0,1:T(8,128)(2,1)S(1)} all-to-all(bf16[8,160,384]{2,0,1:T(8,128)(2,1)S(1)} %copy.75), channel_id=1, replica_groups=mesh['section'=32,'blk'=16] {'blk'}, dimensions={1} | all-to-all | bytes 1966080 | tf_op jit(solution)/shard_map/all_to_all | solution.py:25
  120.0 5.4 %shard_map.137 = (bf16[16,10,8,384]{3,2,1,0:T(8,128)(2,1)}, bf16[2,10,128,128]{3,2,1,0:T(8,128)(2,1)}) custom-call(bf16[10,128,384]{2,1,0:T(8,128)(2,1)} %bitcast.120, bf16[2,10,128,128]{3,2,1,0:T(8,128)(2,1)} %copy.67.refs_1_, bf16[2,10,128,128]{3,2,1,0:T(8,128)(2,1)} %bitcast.119, bf16[10,128,128]{2,1,0:T(8,128)(2,1)} %copy-done.1, ...), custom_call_target="tpu_custom_call" | custom-call | flops 251658240 | bytes 5898240 | tf_op jit(solution)/shard_map/pallas_call | solution.py:110
  125.4 4.5 %all-to-all-start.3 = ((bf16[16,10,8,384]{3,2,1,0:T(8,128)(2,1)}), bf16[16,10,8,384]{3,2,1,0:T(8,128)(2,1)}, u32[]{:S(2)}, u32[]{:S(2)}) async-start(bf16[16,10,8,384]{3,2,1,0:T(8,128)(2,1)} %get-tuple-element.14), calls=%async_computation.3 | async-start | bytes 1966080 | tf_op jit(solution)/shard_map/all_to_all | solution.py:30
  130.7 1.3 slice_bitcast_fusion.1
  135.3 1.7 %slice.58 = bf16[10,128,128]{2,1,0:T(8,128)(2,1)} slice(bf16[10,128,384]{2,1,0:T(8,128)(2,1)} %bitcast.121), slice={[0:10], [0:128], [256:384]} | slice | bytes 655360 | tf_op jit(solution)/shard_map/slice | solution.py:198
  137.0 1.8 %fusion = bf16[2,10,128,128]{3,2,1,0:T(8,128)(2,1)S(1)} fusion(bf16[1,10,128,256]{3,2,1,0:T(8,128)(2,1)S(1)} %copy-done.8, bf16[1,10,128,256]{3,2,1,0:T(8,128)(2,1)S(1)} %copy-done.7, bf16[2,10,128,128]{3,2,1,0:T(8,128)(2,1)} %get-tuple-element.16, bf16[2,10,128,128]{3,2,1,0:T(8,128)(2,1)} %get-tuple-element.15), kind=kOutput, calls=%fused_computation.4 | convolution fusion | flops 171704320 | bytes 3276800 | tf_op jit(solution)/shard_map/grpt,grot->grpo/dot_general | solution.py:204
  139.9 1.4 fusion.15
  142.3 4.2 %all-to-all-done.3 = bf16[16,10,8,384]{3,2,1,0:T(8,128)(2,1)} async-done(((bf16[16,10,8,384]{3,2,1,0:T(8,128)(2,1)}), bf16[16,10,8,384]{3,2,1,0:T(8,128)(2,1)}, u32[]{:S(2)}, u32[]{:S(2)}) %all-to-all-start.3) | async-done | bytes 983072 | tf_op jit(solution)/shard_map/all_to_all | solution.py:30
  147.5 1.2 slice_bitcast_fusion.2
  (65 shorter events, 20.0 us)
Async XLA Ops:
  2.9 3.4 %copy-start.2 = (bf16[2,8,40,160]{3,2,1,0:T(8,128)(2,1)}, bf16[2,8,40,160]{3,2,1,0:T(8,128)(2,1)S(1)}, u32[]{:S(2)}) copy-start(bf16[2,8,40,160]{3,2,1,0:T(8,128)(2,1)S(1)} %reshape_squeeze.27) | copy-start | bytes 614404
  6.1 0.9 copy-start.14
  9.6 41.6 %all-to-all-start = ((bf16[8,160,896]{2,0,1:T(8,128)(2,1)}), bf16[8,160,896]{2,0,1:T(8,128)(2,1)S(1)}, u32[]{:S(2)}, u32[]{:S(2)}) async-start(bf16[8,160,896]{2,0,1:T(8,128)(2,1)} %copy.63), calls=%async_computation | async-start | bytes 4587520 | tf_op jit(solution)/shard_map/all_to_all | solution.py:25
  22.1 30.8 %copy-start.1 = (bf16[10,128,128]{2,1,0:T(8,128)(2,1)}, bf16[10,128,128]{2,1,0:T(8,128)(2,1)S(1)}, u32[]{:S(2)}) copy-start(bf16[10,128,128]{2,1,0:T(8,128)(2,1)S(1)} %slice.60.refs_3_) | copy-start | bytes 983044
  60.7 27.3 %all-to-all-start.1 = ((bf16[16,10,8,640]{3,2,1,0:T(8,128)(2,1)}), bf16[16,10,8,640]{3,2,1,0:T(8,128)(2,1)S(1)}, u32[]{:S(2)}, u32[]{:S(2)}) async-start(bf16[16,10,8,640]{3,2,1,0:T(8,128)(2,1)} %get-tuple-element.12), calls=%async_computation.1 | async-start | bytes 3276800 | tf_op jit(solution)/shard_map/all_to_all | solution.py:30
  64.4 24.7 %copy-start.3 = (bf16[2,8,40,160]{3,2,1,0:T(8,128)(2,1)S(1)}, bf16[2,8,40,160]{3,2,1,0:T(8,128)(2,1)}, u32[]{:S(2)}) copy-start(bf16[2,8,40,160]{3,2,1,0:T(8,128)(2,1)} %copy-done.2) | copy-start | bytes 614404
  88.0 3.3 %copy-start.9 = (bf16[1,320,128]{2,1,0:T(8,128)(2,1)S(1)}, bf16[1,320,128]{2,1,0:T(8,128)(2,1)}, u32[]{:S(2)}) copy-start(bf16[1,320,128]{2,1,0:T(8,128)(2,1)} %param.9) | copy-start | bytes 245764
  88.1 6.0 %copy-start.13 = (bf16[320,128]{1,0:T(8,128)(2,1)S(1)}, bf16[320,128]{1,0:T(8,128)(2,1)}, u32[]{:S(2)}) copy-start(bf16[320,128]{1,0:T(8,128)(2,1)} %param.13) | copy-start | bytes 245764
  89.1 8.7 %copy-start.4 = (bf16[160,8,2,128]{3,1,2,0:T(8,128)(2,1)}, bf16[160,8,2,128]{3,1,2,0:T(8,128)(2,1)S(1)}, u32[]{:S(2)}) copy-start(bf16[160,8,2,128]{3,1,2,0:T(8,128)(2,1)S(1)} %get-tuple-element.39) | copy-start | bytes 1966084
  89.1 8.3 %copy-start.10 = (bf16[320,128]{1,0:T(8,128)(2,1)S(1)}, bf16[320,128]{1,0:T(8,128)(2,1)}, u32[]{:S(2)}) copy-start(bf16[320,128]{1,0:T(8,128)(2,1)} %param.10) | copy-start | bytes 245764
  89.4 4.6 %collective-permute-start.1 = (bf16[8,40,128]{2,1,0:T(8,128)(2,1)S(1)}, bf16[8,40,128]{2,1,0:T(8,128)(2,1)S(1)}, u32[]{:S(2)}, u32[]{:S(2)}) collective-permute-start(bf16[8,40,128]{2,1,0:T(8,128)(2,1)S(1)} %fusion.26), channel_id=1, source_target_pairs={{16,0},{32,16},{48,32},{64,48},{80,64},{96,80},{112,96},{128,112},... | collective-permute-start | bytes 245768 | tf_op jit(solution)/shard_map/ppermute | solution.py:21
  91.6 5.8 %collective-permute-start = (bf16[8,40,128]{2,1,0:T(8,128)(2,1)S(1)}, bf16[8,40,128]{2,1,0:T(8,128)(2,1)S(1)}, u32[]{:S(2)}, u32[]{:S(2)}) collective-permute-start(bf16[8,40,128]{2,1,0:T(8,128)(2,1)S(1)} %fusion.27), channel_id=1, source_target_pairs={{0,16},{16,32},{32,48},{48,64},{64,80},{80,96},{96,112},{112,128},... | collective-permute-start | bytes 245768 | tf_op jit(solution)/shard_map/ppermute | solution.py:21
  120.0 9.9 %copy-start = (bf16[16,8,10,896]{3,1,0,2:T(8,128)(2,1)S(1)}, bf16[16,8,10,896]{3,1,0,2:T(8,128)(2,1)}, u32[]{:S(2)}) copy-start(bf16[16,8,10,896]{3,1,0,2:T(8,128)(2,1)} %copy.130) | copy-start | bytes 6881284
  125.4 21.1 %all-to-all-start.3 = ((bf16[16,10,8,384]{3,2,1,0:T(8,128)(2,1)}), bf16[16,10,8,384]{3,2,1,0:T(8,128)(2,1)}, u32[]{:S(2)}, u32[]{:S(2)}) async-start(bf16[16,10,8,384]{3,2,1,0:T(8,128)(2,1)} %get-tuple-element.14), calls=%async_computation.3 | async-start | bytes 1966080 | tf_op jit(solution)/shard_map/all_to_all | solution.py:30
  129.9 2.1 %copy-start.5 = (bf16[160,8,2,128]{3,1,2,0:T(8,128)(2,1)S(1)}, bf16[160,8,2,128]{3,1,2,0:T(8,128)(2,1)}, u32[]{:S(2)}) copy-start(bf16[160,8,2,128]{3,1,2,0:T(8,128)(2,1)} %copy-done.4) | copy-start | bytes 1966084
  130.7 1.4 copy-start.6
  131.9 5.1 %copy-start.7 = (bf16[1,10,128,256]{3,2,1,0:T(8,128)(2,1)S(1)}, bf16[1,10,128,256]{3,2,1,0:T(8,128)(2,1)}, u32[]{:S(2)}) copy-start(bf16[1,10,128,256]{3,2,1,0:T(8,128)(2,1)} %get-tuple-element.36) | copy-start | bytes 1966084
  131.9 5.1 %copy-start.8 = (bf16[1,10,128,256]{3,2,1,0:T(8,128)(2,1)S(1)}, bf16[1,10,128,256]{3,2,1,0:T(8,128)(2,1)}, u32[]{:S(2)}) copy-start(bf16[1,10,128,256]{3,2,1,0:T(8,128)(2,1)} %get-tuple-element.37) | copy-start | bytes 1966084
  138.8 1.1 copy-start.11
  138.8 1.1 copy-start.12

commit v8 on v7

--- a/solution.py
+++ b/solution.py
@@ -22,7 +22,10 @@
 
 
 def to_blocks(pieces):
-    return lax.all_to_all(pieces, "blk", split_axis=1, concat_axis=0, tiled=True)
+    groups = lax.axis_size("blk")
+    p_local, r_all, n = pieces.shape
+    grouped = pieces.reshape(p_local, groups, r_all // groups, n).transpose(1, 2, 0, 3)
+    return lax.all_to_all(grouped, "blk", split_axis=0, concat_axis=0, tiled=True)
 
 
 def to_features(grouped):
@@ -50,6 +53,11 @@
         payload[group, r, :, at : at + width] = value[group * rows : (group + 1) * rows].astype(
             payload.dtype
         )
+
+
+def take(arrived, r, lo, hi):
+    pieces = [arrived[g, r, :, lo:hi].astype(jnp.float32) for g in range(arrived.shape[0])]
+    return jnp.concatenate(pieces, axis=0).astype(jnp.bfloat16)
 
 
 def _middle_kernel(fwd, bwd, bwd_at, keep_at, has_mixed_in, *refs):
@@ -61,10 +69,10 @@
     rest = refs[2:]
     hidden_out = rest.pop(0) if not has_mixed_in else None
     keep_out = rest.pop(0) if keep_at is not None else None
-    for r in range(arrived.shape[0]):
-        gate = jnp.dot(up_t[0, r], arrived[r, :, :fwd], preferred_element_type=jnp.float32)
+    for r in range(arrived.shape[1]):
+        gate = jnp.dot(up_t[0, r], take(arrived, r, 0, fwd), preferred_element_type=jnp.float32)
         upper = jnp.dot(
-            up_t[1, r], arrived[r, :, fwd : 2 * fwd], preferred_element_type=jnp.float32
+            up_t[1, r], take(arrived, r, fwd, 2 * fwd), preferred_element_type=jnp.float32
         )
         hidden = (gate / (1.0 + jnp.exp(-gate)) * upper).astype(jnp.bfloat16)
         put(payload, r, 0, jnp.dot(down_t[r], hidden, preferred_element_type=jnp.float32))
@@ -78,7 +86,7 @@
         else:
             m0, m1 = gate[:, bwd_at : bwd_at + bwd], upper[:, bwd_at : bwd_at + bwd]
         grad_hidden = jnp.dot(
-            down[r], arrived[r, :, 2 * fwd :], preferred_element_type=jnp.float32
+            down[r], take(arrived, r, 2 * fwd, arrived.shape[3]), preferred_element_type=jnp.float32
         )
         sg = 1.0 / (1.0 + jnp.exp(-m0))
         gm0 = (grad_hidden * m1 * (sg * (1.0 + m0 * (1.0 - sg)))).astype(jnp.bfloat16)
@@ -90,8 +98,8 @@
 
 
 def middle(arrived, up, up_t, down, down_t, fwd, bwd, bwd_at=0, keep_at=None, mixed_in=None):
-    rb, pa, _ = arrived.shape
-    o = up.shape[3]
+    _, rb, _, _ = arrived.shape
+    pa, o = up.shape[2], up.shape[3]
     groups = lax.axis_size("blk")
     outs = [
         jax.ShapeDtypeStruct((groups, rb, pa // groups, fwd + 2 * bwd), jnp.bfloat16),
@@ -161,7 +169,7 @@
     spread_a = spread_of(jnp.concatenate([first_inputs, stash_0, stash_1], axis=2), up_first)
     glow_1 = lowered_grad_of(first_grads, down_second)
     payload = jnp.concatenate([spread_a.reshape(pb, SECOND_BLOCKS, 6 * t), glow_1], axis=2)
-    arrived_a = jnp.swapaxes(to_blocks(payload), 0, 1)
+    arrived_a = to_blocks(payload)
     payload_a, gmix_1, hidden_a, mixed_s1 = middle(
         arrived_a, *weights, fwd=3 * t, bwd=t, bwd_at=t, keep_at=2 * t
     )
@@ -181,7 +189,7 @@
     spread_b = spread_of(inputs, up_first)
     glow_2 = lowered_grad_of(grads, down_second)
     payload = jnp.concatenate([spread_b.reshape(pb, SECOND_BLOCKS, 2 * t), glow_2], axis=2)
-    arrived_b = jnp.swapaxes(to_blocks(payload), 0, 1)
+    arrived_b = to_blocks(payload)
     payload_b, gmix_2 = middle(arrived_b, *weights, fwd=t, bwd=t, mixed_in=mixed_s1)
     back = to_features(payload_b)
     outputs = output_of(inputs, back[:, :, :t], down_second)
@@ -191,22 +199,22 @@
     stash_both = jnp.concatenate([stash_0, stash_1], axis=2)
     gspread_both = jnp.concatenate([gspread_1p, gspread_2p], axis=3)
     spread_both = jnp.stack(
-        [arrived_a[:, :, t : 3 * t], arrived_a[:, :, 4 * t : 6 * t]]
+        [arrived_a[..., t : 3 * t], arrived_a[..., 4 * t : 6 * t]]
     )
     gmix_both = jnp.concatenate([gmix_1, gmix_2], axis=3)
     hidden_both = hidden_a[:, :, t:]
-    glow_both = jnp.concatenate([arrived_a[:, :, 6 * t :], arrived_b[:, :, 2 * t :]], axis=2)
+    glow_both = jnp.concatenate([arrived_a[..., 6 * t :], arrived_b[..., 2 * t :]], axis=3)
     lowered_both = lowered_ap[:, :, t:]
     grads_both = jnp.concatenate([first_grads, grads], axis=2)
     total_first_up = jnp.einsum(
         "pqt,rpgt->gpqr", stash_both, gspread_both, preferred_element_type=jnp.float32
     )
     total_second_up = jnp.einsum(
-        "grpt,grot->grpo", spread_both, gmix_both, preferred_element_type=jnp.float32
-    )
+        "gsrlt,grot->grslo", spread_both, gmix_both, preferred_element_type=jnp.float32
+    ).reshape(2, rb, FIRST_BLOCKS, BLOCK)
     total_first_down = jnp.einsum(
-        "rot,rpt->rop", hidden_both, glow_both, preferred_element_type=jnp.float32
-    )
+        "rot,srlt->rosl", hidden_both, glow_both, preferred_element_type=jnp.float32
+    ).reshape(rb, BLOCK, FIRST_BLOCKS)
     total_second_down = jnp.einsum(
         "rpt,pqt->prq", lowered_both, grads_both, preferred_element_type=jnp.float32
     )

time: 153 us -> 171 us (1.12)
  the two profiles are of different devices: /device:TPU:224 before, /device:TPU:97 now
where the time goes in v8:
time: 171 us; the launch traced here: 170 us
  waiting for transfers between devices  68.8 us (40%)
  local copies, waits for them, and re-layouts  46.7 us (27%)
  starting transfers between devices  29.2 us (17%)
  Pallas kernels  13.3 us (8%)
  matrix products  7.93 us (5%)
  other arithmetic  2.74 us (2%)
    all_to_all x2, waiting for transfers between devices, to_blocks(): lax.all_to_all(grouped, 'blk', split_axis=0, concat_axis=0, tiled=True)  46.3 us
    convert_element_type x2, local copies, waits for them, and re-layouts, shards(): (total_first_down * factor).astype(jnp.bfloat16).reshape(first_down.shape)  22.4 us
    all_to_all x2, waiting for transfers between devices, to_features(): lax.all_to_all(grouped, 'blk', split_axis=0, concat_axis=0, tiled=True)  21.4 us
    pallas_call x2, Pallas kernels, middle(): pl.pallas_call(functools.partial(_middle_kernel, fwd, bwd, bwd_at, keep_a...  13.3 us
    ppermute x2, starting transfers between devices, from_behind(): return lax.ppermute(value, axis, pairs)  10.6 us
    all_to_all x2, starting transfers between devices, to_blocks(): lax.all_to_all(grouped, 'blk', split_axis=0, concat_axis=0, tiled=True)  10.4 us
    all_to_all x2, starting transfers between devices, to_features(): lax.all_to_all(grouped, 'blk', split_axis=0, concat_axis=0, tiled=True)  8.21 us
    unnamed x36, local copies, waits for them, and re-layouts  5.76 us
  transfers between devices with their start and end apart: 6, of which 4 were waited for; matrix products, arithmetic and copies ran while one was open for 21% of the time, Pallas kernels for 0%

profile of v8, /device:TPU:97, one launch (start us, length us, event | category | flops | bytes accessed | tf_op | source)
XLA Modules:
  0.0 169.6 jit_solution(8398236167325449313)
XLA Ops:
  1.6 1.4 reshape_squeeze.27
  3.0 1.6 reshape_squeeze.28
  6.6 1.2 copy.39
  7.7 1.6 maximum_bitcast_fusion
  9.3 6.8 %all-to-all-start = ((bf16[16,10,8,896]{3,2,1,0:T(8,128)(2,1)}), bf16[16,10,8,896]{3,2,1,0:T(8,128)(2,1)S(1)}, u32[]{:S(2)}, u32[]{:S(2)}) async-start(bf16[16,10,8,896]{3,2,1,0:T(8,128)(2,1)} %maximum_bitcast_fusion), calls=%async_computation | async-start | bytes 4587520 | tf_op jit(solution)/shard_map/all_to_all | solution.py:28
  16.1 2.3 %reshape_squeeze.30 = bf16[2,10,128,128]{3,2,0,1:T(8,128)(2,1)S(1)} reshape(bf16[1,2,10,16384]{3,1,2,0:T(2,128)(2,1)} %param.15) | data formatting | bytes 1310720 | tf_op jit(solution)/shard_map/reshape;squeeze | solution.py:156
  19.3 1.1 copy.42
  20.4 1.1 copy.81
  22.5 27.2 %all-to-all-done.refs_0_ = bf16[16,10,8,896]{3,2,1,0:T(8,128)(2,1)S(1)} async-done(((bf16[16,10,8,896]{3,2,1,0:T(8,128)(2,1)}), bf16[16,10,8,896]{3,2,1,0:T(8,128)(2,1)S(1)}, u32[]{:S(2)}, u32[]{:S(2)}) %all-to-all-start) | async-done | bytes 2293792 | tf_op jit(solution)/shard_map/all_to_all | solution.py:28
  49.7 1.4 copy-done
  51.1 7.9 %shard_map.136 = (bf16[16,10,8,640]{3,2,1,0:T(8,128)(2,1)}, bf16[2,10,128,128]{3,2,1,0:T(8,128)(2,1)}, bf16[10,128,384]{2,1,0:T(8,128)(2,1)}, f32[2,10,128,128]{3,2,1,0:T(8,128)}) custom-call(bf16[16,10,8,896]{3,2,1,0:T(8,128)(2,1)} %copy-done, bf16[2,10,128,128]{3,2,1,0:T(8,128)(2,1)} %copy.44.refs_1_, bf16[2,10,128,128]{3,2,1,0:T(8,128)(2,1)} %bitcast.112, ...), custom_call_target="tpu_custom_call" | custom-call | flops 503316480 | bytes 8847360 | tf_op jit(solution)/shard_map/pallas_call | solution.py:118
  59.0 3.7 %all-to-all-start.1 = ((bf16[16,10,8,640]{3,2,1,0:T(8,128)(2,1)}), bf16[16,10,8,640]{3,2,1,0:T(8,128)(2,1)S(1)}, u32[]{:S(2)}, u32[]{:S(2)}) async-start(bf16[16,10,8,640]{3,2,1,0:T(8,128)(2,1)} %get-tuple-element.12), calls=%async_computation.1 | async-start | bytes 3276800 | tf_op jit(solution)/shard_map/all_to_all | solution.py:33
  62.8 21.4 %all-to-all-done.1 = bf16[16,10,8,640]{3,2,1,0:T(8,128)(2,1)S(1)} async-done(((bf16[16,10,8,640]{3,2,1,0:T(8,128)(2,1)}), bf16[16,10,8,640]{3,2,1,0:T(8,128)(2,1)S(1)}, u32[]{:S(2)}, u32[]{:S(2)}) %all-to-all-start.1) | async-done | bytes 1638432 | tf_op jit(solution)/shard_map/all_to_all | solution.py:33
  85.5 5.9 %collective-permute-start.1 = (bf16[8,40,128]{2,1,0:T(8,128)(2,1)S(1)}, bf16[8,40,128]{2,1,0:T(8,128)(2,1)S(1)}, u32[]{:S(2)}, u32[]{:S(2)}) collective-permute-start(bf16[8,40,128]{2,1,0:T(8,128)(2,1)S(1)} %fusion.23), channel_id=1, source_target_pairs={{16,0},{32,16},{48,32},{64,48},{80,64},{96,80},{112,96},{128,112},... | collective-permute-start | bytes 245768 | tf_op jit(solution)/shard_map/ppermute | solution.py:21
  91.8 4.6 %collective-permute-start = (bf16[8,40,128]{2,1,0:T(8,128)(2,1)S(1)}, bf16[8,40,128]{2,1,0:T(8,128)(2,1)S(1)}, u32[]{:S(2)}, u32[]{:S(2)}) collective-permute-start(bf16[8,40,128]{2,1,0:T(8,128)(2,1)S(1)} %fusion.24), channel_id=1, source_target_pairs={{0,16},{16,32},{32,48},{48,64},{64,80},{80,96},{96,112},{112,128},... | collective-permute-start | bytes 245768 | tf_op jit(solution)/shard_map/ppermute | solution.py:21
  99.8 3.6 %all-to-all-start.2 = ((bf16[16,10,8,384]{3,2,1,0:T(8,128)(2,1)}), bf16[16,10,8,384]{3,2,1,0:T(8,128)(2,1)S(1)}, u32[]{:S(2)}, u32[]{:S(2)}) async-start(bf16[16,10,8,384]{3,2,1,0:T(8,128)(2,1)} %maximum_bitcast_fusion.3), calls=%async_computation.2 | async-start | bytes 1966080 | tf_op jit(solution)/shard_map/all_to_all | solution.py:28
  103.4 19.1 %all-to-all-done.2.refs_0_ = bf16[16,10,8,384]{3,2,1,0:T(8,128)(2,1)S(1)} async-done(((bf16[16,10,8,384]{3,2,1,0:T(8,128)(2,1)}), bf16[16,10,8,384]{3,2,1,0:T(8,128)(2,1)S(1)}, u32[]{:S(2)}, u32[]{:S(2)}) %all-to-all-start.2) | async-done | bytes 983072 | tf_op jit(solution)/shard_map/all_to_all | solution.py:28
  123.5 5.4 %shard_map.137 = (bf16[16,10,8,384]{3,2,1,0:T(8,128)(2,1)}, bf16[2,10,128,128]{3,2,1,0:T(8,128)(2,1)}) custom-call(bf16[16,10,8,384]{3,2,1,0:T(8,128)(2,1)} %copy-done.2, bf16[2,10,128,128]{3,2,1,0:T(8,128)(2,1)} %copy.44.refs_1_, bf16[2,10,128,128]{3,2,1,0:T(8,128)(2,1)} %bitcast.113, bf16[10,128,128]{2,1,0:T(8,128)(2,1)} %copy-done.3, ...), custom_call_target="tpu_custom_call" | custom-call | flops 251658240 | bytes 5898240 | tf_op jit(solution)/shard_map/pallas_call | solution.py:118
  128.9 4.5 %all-to-all-start.3 = ((bf16[16,10,8,384]{3,2,1,0:T(8,128)(2,1)}), bf16[16,10,8,384]{3,2,1,0:T(8,128)(2,1)}, u32[]{:S(2)}, u32[]{:S(2)}) async-start(bf16[16,10,8,384]{3,2,1,0:T(8,128)(2,1)} %get-tuple-element.14), calls=%async_computation.3 | async-start | bytes 1966080 | tf_op jit(solution)/shard_map/all_to_all | solution.py:33
  133.5 1.1 slice_bitcast_fusion.1
  136.8 1.8 %fusion = bf16[2,10,16,8,128]{4,3,2,1,0:T(8,128)(2,1)S(1)} fusion(bf16[2,10,128,128]{3,2,1,0:T(8,128)(2,1)} %get-tuple-element.16, bf16[2,10,128,128]{3,2,1,0:T(8,128)(2,1)} %get-tuple-element.15, bf16[1,16,10,8,256]{4,3,2,1,0:T(8,128)(2,1)S(1)} %copy-done.10, bf16[1,16,10,8,256]{4,3,2,1,0:T(8,128)(2,1)S(1)} %copy-done.9), kind=kOutput, calls=%fused_computation.3 | convolution fusion | flops 171704320 | bytes 3276800 | tf_op jit(solution)/shard_map/gsrlt,grot->grslo/dot_general | solution.py:212
  141.3 4.1 %copy.63 = bf16[10,128,16,8]{3,2,1,0:T(8,128)(2,1)} copy(bf16[10,128,16,8]{1,2,3,0:T(8,128)(2,1)S(1)} %fusion.12) | data formatting | bytes 655360 | tf_op jit(solution)/shard_map/convert_element_type | solution.py:227
  145.4 18.3 %convert_element_type.100 = bf16[1,10,16384]{2,1,0:T(8,128)(2,1)} reshape(bf16[10,128,16,8]{3,2,1,0:T(8,128)(2,1)} %copy.63) | data formatting | bytes 655360 | tf_op jit(solution)/shard_map/convert_element_type | solution.py:227
  164.7 1.2 slice_bitcast_fusion.2
  (72 shorter events, 20.2 us)
Async XLA Ops:
  0.6 5.2 %copy-start.11 = (bf16[1,320,128]{2,1,0:T(8,128)(2,1)S(1)}, bf16[1,320,128]{2,1,0:T(8,128)(2,1)}, u32[]{:S(2)}) copy-start(bf16[1,320,128]{2,1,0:T(8,128)(2,1)} %param.9) | copy-start | bytes 245764
  3.0 3.6 %copy-start.4 = (bf16[2,8,40,160]{3,2,1,0:T(8,128)(2,1)}, bf16[2,8,40,160]{3,2,1,0:T(8,128)(2,1)S(1)}, u32[]{:S(2)}) copy-start(bf16[2,8,40,160]{3,2,1,0:T(8,128)(2,1)S(1)} %reshape_squeeze.27) | copy-start | bytes 614404
  9.3 40.4 %all-to-all-start = ((bf16[16,10,8,896]{3,2,1,0:T(8,128)(2,1)}), bf16[16,10,8,896]{3,2,1,0:T(8,128)(2,1)S(1)}, u32[]{:S(2)}, u32[]{:S(2)}) async-start(bf16[16,10,8,896]{3,2,1,0:T(8,128)(2,1)} %maximum_bitcast_fusion), calls=%async_computation | async-start | bytes 4587520 | tf_op jit(solution)/shard_map/all_to_all | solution.py:28
  21.6 28.2 %copy-start.3 = (bf16[10,128,128]{2,1,0:T(8,128)(2,1)}, bf16[10,128,128]{2,1,0:T(8,128)(2,1)S(1)}, u32[]{:S(2)}) copy-start(bf16[10,128,128]{2,1,0:T(8,128)(2,1)S(1)} %slice.60.refs_3_) | copy-start | bytes 983044
  49.7 1.4 copy-start
  59.0 25.1 %all-to-all-start.1 = ((bf16[16,10,8,640]{3,2,1,0:T(8,128)(2,1)}), bf16[16,10,8,640]{3,2,1,0:T(8,128)(2,1)S(1)}, u32[]{:S(2)}, u32[]{:S(2)}) async-start(bf16[16,10,8,640]{3,2,1,0:T(8,128)(2,1)} %get-tuple-element.12), calls=%async_computation.1 | async-start | bytes 3276800 | tf_op jit(solution)/shard_map/all_to_all | solution.py:33
  84.2 1.0 copy-start.5
  84.2 1.0 copy-start.14
  85.2 11.6 %copy-start.6 = (bf16[160,8,2,128]{3,1,2,0:T(8,128)(2,1)}, bf16[160,8,2,128]{3,1,2,0:T(8,128)(2,1)S(1)}, u32[]{:S(2)}) copy-start(bf16[160,8,2,128]{3,1,2,0:T(8,128)(2,1)S(1)} %get-tuple-element.33) | copy-start | bytes 1966084
  85.2 11.2 %copy-start.13 = (bf16[320,128]{1,0:T(8,128)(2,1)S(1)}, bf16[320,128]{1,0:T(8,128)(2,1)}, u32[]{:S(2)}) copy-start(bf16[320,128]{1,0:T(8,128)(2,1)} %param.13) | copy-start | bytes 245764
  85.2 12.7 %copy-start.12 = (bf16[320,128]{1,0:T(8,128)(2,1)S(1)}, bf16[320,128]{1,0:T(8,128)(2,1)}, u32[]{:S(2)}) copy-start(bf16[320,128]{1,0:T(8,128)(2,1)} %param.10) | copy-start | bytes 245764
  85.5 10.9 %collective-permute-start.1 = (bf16[8,40,128]{2,1,0:T(8,128)(2,1)S(1)}, bf16[8,40,128]{2,1,0:T(8,128)(2,1)S(1)}, u32[]{:S(2)}, u32[]{:S(2)}) collective-permute-start(bf16[8,40,128]{2,1,0:T(8,128)(2,1)S(1)} %fusion.23), channel_id=1, source_target_pairs={{16,0},{32,16},{48,32},{64,48},{80,64},{96,80},{112,96},{128,112},... | collective-permute-start | bytes 245768 | tf_op jit(solution)/shard_map/ppermute | solution.py:21
  91.8 6.1 %collective-permute-start = (bf16[8,40,128]{2,1,0:T(8,128)(2,1)S(1)}, bf16[8,40,128]{2,1,0:T(8,128)(2,1)S(1)}, u32[]{:S(2)}, u32[]{:S(2)}) collective-permute-start(bf16[8,40,128]{2,1,0:T(8,128)(2,1)S(1)} %fusion.24), channel_id=1, source_target_pairs={{0,16},{16,32},{32,48},{48,64},{64,80},{80,96},{96,112},{112,128},... | collective-permute-start | bytes 245768 | tf_op jit(solution)/shard_map/ppermute | solution.py:21
  99.8 22.8 %all-to-all-start.2 = ((bf16[16,10,8,384]{3,2,1,0:T(8,128)(2,1)}), bf16[16,10,8,384]{3,2,1,0:T(8,128)(2,1)S(1)}, u32[]{:S(2)}, u32[]{:S(2)}) async-start(bf16[16,10,8,384]{3,2,1,0:T(8,128)(2,1)} %maximum_bitcast_fusion.3), calls=%async_computation.2 | async-start | bytes 1966080 | tf_op jit(solution)/shard_map/all_to_all | solution.py:28
  123.5 9.9 %copy-start.1 = (bf16[16,10,8,896]{3,2,1,0:T(8,128)(2,1)S(1)}, bf16[16,10,8,896]{3,2,1,0:T(8,128)(2,1)}, u32[]{:S(2)}) copy-start(bf16[16,10,8,896]{3,2,1,0:T(8,128)(2,1)} %copy-done) | copy-start | bytes 6881284
  128.9 34.8 %all-to-all-start.3 = ((bf16[16,10,8,384]{3,2,1,0:T(8,128)(2,1)}), bf16[16,10,8,384]{3,2,1,0:T(8,128)(2,1)}, u32[]{:S(2)}, u32[]{:S(2)}) async-start(bf16[16,10,8,384]{3,2,1,0:T(8,128)(2,1)} %get-tuple-element.14), calls=%async_computation.3 | async-start | bytes 1966080 | tf_op jit(solution)/shard_map/all_to_all | solution.py:33
  133.4 1.2 copy-start.7
  133.4 1.8 %copy-start.8 = (bf16[160,8,256]{2,1,0:T(8,128)(2,1)S(1)}, bf16[160,8,256]{2,1,0:T(8,128)(2,1)}, u32[]{:S(2)}) copy-start(bf16[160,8,256]{2,1,0:T(8,128)(2,1)} %get-tuple-element.32) | copy-start | bytes 1966084
  133.5 1.7 %copy-start.15 = (bf16[1,320,128]{2,1,0:T(8,128)(2,1)S(1)}, bf16[1,320,128]{2,1,0:T(8,128)(2,1)}, u32[]{:S(2)}) copy-start(bf16[1,320,128]{2,1,0:T(8,128)(2,1)} %param.12) | copy-start | bytes 245764
  134.7 2.1 %copy-start.9 = (bf16[1,16,10,8,256]{4,3,2,1,0:T(8,128)(2,1)S(1)}, bf16[1,16,10,8,256]{4,3,2,1,0:T(8,128)(2,1)}, u32[]{:S(2)}) copy-start(bf16[1,16,10,8,256]{4,3,2,1,0:T(8,128)(2,1)} %get-tuple-element.30) | copy-start | bytes 1966084
  134.7 2.1 %copy-start.10 = (bf16[1,16,10,8,256]{4,3,2,1,0:T(8,128)(2,1)S(1)}, bf16[1,16,10,8,256]{4,3,2,1,0:T(8,128)(2,1)}, u32[]{:S(2)}) copy-start(bf16[1,16,10,8,256]{4,3,2,1,0:T(8,128)(2,1)} %get-tuple-element.31) | copy-start | bytes 1966084
  138.6 1.1 slice-start
  138.6 1.1 slice-start.1
  139.7 1.2 copy-start.16
  (1 other events, 1.0 us)

commit v9 on v7

--- a/solution.py
+++ b/solution.py
@@ -52,19 +52,62 @@
         )
 
 
-def _middle_kernel(fwd, bwd, bwd_at, keep_at, has_mixed_in, *refs):
+def _forward_kernel(width, gate_at, up_at, *refs):
+    arrived, up_t, down_t, lowered, hidden_out, keep_out = refs
+    for r in range(arrived.shape[0]):
+        gate = jnp.dot(
+            up_t[0, r], arrived[r, :, gate_at : gate_at + width], preferred_element_type=jnp.float32
+        )
+        upper = jnp.dot(
+            up_t[1, r], arrived[r, :, up_at : up_at + width], preferred_element_type=jnp.float32
+        )
+        hidden = (gate / (1.0 + jnp.exp(-gate)) * upper).astype(jnp.bfloat16)
+        put(lowered, r, 0, jnp.dot(down_t[r], hidden, preferred_element_type=jnp.float32))
+        hidden_out[r] = hidden
+        keep_out[0, r] = gate
+        keep_out[1, r] = upper
+
+
+def forward_only(arrived, up_t, down_t, width, gate_at, up_at):
+    rb, pa, _ = arrived.shape
+    o = up_t.shape[2]
+    groups = lax.axis_size("blk")
+    outs = (
+        jax.ShapeDtypeStruct((groups, rb, pa // groups, width), jnp.bfloat16),
+        jax.ShapeDtypeStruct((rb, o, width), jnp.bfloat16),
+        jax.ShapeDtypeStruct((2, rb, o, width), jnp.float32),
+    )
+    vmem = pltpu.MemorySpace.VMEM
+    return pl.pallas_call(
+        functools.partial(_forward_kernel, width, gate_at, up_at),
+        out_shape=outs,
+        in_specs=[pl.BlockSpec(memory_space=vmem)] * 3,
+        out_specs=tuple(pl.BlockSpec(memory_space=vmem) for _ in outs),
+        cost_estimate=pl.CostEstimate(
+            flops=2 * rb * o * pa * 3 * width,
+            transcendentals=rb * o * width,
+            bytes_accessed=arrived.size * 2 + up_t.size * 2 + down_t.size * 2 + rb * o * width * 14,
+        ),
+    )(arrived, up_t, down_t)
+
+
+def _middle_kernel(fwd, bwd, bwd_at, keep_at, has_mixed_in, cols, has_extra, *refs):
     refs = list(refs)
     arrived, up, up_t, down, down_t = refs[:5]
     refs = refs[5:]
     mixed_in = refs.pop(0) if has_mixed_in else None
+    extra = refs.pop(0) if has_extra else None
     payload, grad_mixed = refs[0], refs[1]
     rest = refs[2:]
     hidden_out = rest.pop(0) if not has_mixed_in else None
     keep_out = rest.pop(0) if keep_at is not None else None
+    gate_at, up_at, grad_at = cols
     for r in range(arrived.shape[0]):
-        gate = jnp.dot(up_t[0, r], arrived[r, :, :fwd], preferred_element_type=jnp.float32)
+        gate = jnp.dot(
+            up_t[0, r], arrived[r, :, gate_at : gate_at + fwd], preferred_element_type=jnp.float32
+        )
         upper = jnp.dot(
-            up_t[1, r], arrived[r, :, fwd : 2 * fwd], preferred_element_type=jnp.float32
+            up_t[1, r], arrived[r, :, up_at : up_at + fwd], preferred_element_type=jnp.float32
         )
         hidden = (gate / (1.0 + jnp.exp(-gate)) * upper).astype(jnp.bfloat16)
         put(payload, r, 0, jnp.dot(down_t[r], hidden, preferred_element_type=jnp.float32))
@@ -78,7 +121,7 @@
         else:
             m0, m1 = gate[:, bwd_at : bwd_at + bwd], upper[:, bwd_at : bwd_at + bwd]
         grad_hidden = jnp.dot(
-            down[r], arrived[r, :, 2 * fwd :], preferred_element_type=jnp.float32
+            down[r], arrived[r, :, grad_at : grad_at + bwd], preferred_element_type=jnp.float32
         )
         sg = 1.0 / (1.0 + jnp.exp(-m0))
         gm0 = (grad_hidden * m1 * (sg * (1.0 + m0 * (1.0 - sg)))).astype(jnp.bfloat16)
@@ -87,14 +130,21 @@
         grad_mixed[1, r] = gm1
         put(payload, r, fwd, jnp.dot(up[0, r], gm0, preferred_element_type=jnp.float32))
         put(payload, r, fwd + bwd, jnp.dot(up[1, r], gm1, preferred_element_type=jnp.float32))
-
-
-def middle(arrived, up, up_t, down, down_t, fwd, bwd, bwd_at=0, keep_at=None, mixed_in=None):
+        if extra is not None:
+            payload[:, r, :, fwd + 2 * bwd :] = extra[:, r]
+
+
+def middle(
+    arrived, up, up_t, down, down_t, fwd, bwd, cols, bwd_at=0, keep_at=None, mixed_in=None, extra=None
+):
     rb, pa, _ = arrived.shape
     o = up.shape[3]
     groups = lax.axis_size("blk")
     outs = [
-        jax.ShapeDtypeStruct((groups, rb, pa // groups, fwd + 2 * bwd), jnp.bfloat16),
+        jax.ShapeDtypeStruct(
+            (groups, rb, pa // groups, fwd + 2 * bwd + (0 if extra is None else extra.shape[3])),
+            jnp.bfloat16,
+        ),
         jax.ShapeDtypeStruct((2, rb, o, bwd), jnp.bfloat16),
     ]
     if mixed_in is None:
@@ -102,13 +152,16 @@
     if keep_at is not None:
         outs.append(jax.ShapeDtypeStruct((2, rb, o, bwd), jnp.float32))
     ins = [arrived, up, up_t, down, down_t] + ([mixed_in] if mixed_in is not None else [])
+    ins += [extra] if extra is not None else []
     flops = 2 * rb * o * pa * (3 * fwd + 3 * bwd)
     bytes_accessed = sum(x.size * x.dtype.itemsize for x in ins) + sum(
         math.prod(s.shape) * s.dtype.itemsize for s in outs
     )
     vmem = pltpu.MemorySpace.VMEM
     return pl.pallas_call(
-        functools.partial(_middle_kernel, fwd, bwd, bwd_at, keep_at, mixed_in is not None),
+        functools.partial(
+            _middle_kernel, fwd, bwd, bwd_at, keep_at, mixed_in is not None, cols, extra is not None
+        ),
         out_shape=tuple(outs),
         in_specs=[pl.BlockSpec(memory_space=vmem)] * len(ins),
         out_specs=tuple(pl.BlockSpec(memory_space=vmem) for _ in outs),
@@ -162,12 +215,15 @@
     glow_1 = lowered_grad_of(first_grads, down_second)
     payload = jnp.concatenate([spread_a.reshape(pb, SECOND_BLOCKS, 6 * t), glow_1], axis=2)
     arrived_a = jnp.swapaxes(to_blocks(payload), 0, 1)
-    payload_a, gmix_1, hidden_a, mixed_s1 = middle(
-        arrived_a, *weights, fwd=3 * t, bwd=t, bwd_at=t, keep_at=2 * t
+    payload_a, gmix_1, hidden_a = middle(
+        arrived_a, *weights, fwd=2 * t, bwd=t, cols=(0, 3 * t, 6 * t), bwd_at=t
     )
     back = to_features(payload_a)
-    lowered_ap = back[:, :, : 3 * t]
-    gspread_1p = back[:, :, 3 * t :].reshape(SECOND_BLOCKS, pb, 2, t)
+    lowered_ap = back[:, :, : 2 * t]
+    gspread_1p = back[:, :, 2 * t :].reshape(SECOND_BLOCKS, pb, 2, t)
+    lowered_s1, hidden_s1, mixed_s1 = forward_only(
+        arrived_a, up_second_t, down_first_t, t, 2 * t, 5 * t
+    )
     outputs = output_of(first_inputs, lowered_ap[:, :, :t], down_second)
     backward = input_grad_of(first_grads, gspread_1p, up_first)
 
@@ -182,10 +238,13 @@
     glow_2 = lowered_grad_of(grads, down_second)
     payload = jnp.concatenate([spread_b.reshape(pb, SECOND_BLOCKS, 2 * t), glow_2], axis=2)
     arrived_b = jnp.swapaxes(to_blocks(payload), 0, 1)
-    payload_b, gmix_2 = middle(arrived_b, *weights, fwd=t, bwd=t, mixed_in=mixed_s1)
+    payload_b, gmix_2 = middle(
+        arrived_b, *weights, fwd=t, bwd=t, cols=(0, t, 2 * t), mixed_in=mixed_s1, extra=lowered_s1
+    )
     back = to_features(payload_b)
     outputs = output_of(inputs, back[:, :, :t], down_second)
-    gspread_2p = back[:, :, t:].reshape(SECOND_BLOCKS, pb, 2, t)
+    gspread_2p = back[:, :, t : 3 * t].reshape(SECOND_BLOCKS, pb, 2, t)
+    lowered_s1p = back[:, :, 3 * t :]
     backward = input_grad_of(grads, gspread_2p, up_first)
 
     stash_both = jnp.concatenate([stash_0, stash_1], axis=2)
@@ -194,9 +253,9 @@
         [arrived_a[:, :, t : 3 * t], arrived_a[:, :, 4 * t : 6 * t]]
     )
     gmix_both = jnp.concatenate([gmix_1, gmix_2], axis=3)
-    hidden_both = hidden_a[:, :, t:]
+    hidden_both = jnp.concatenate([hidden_a[:, :, t:], hidden_s1], axis=2)
     glow_both = jnp.concatenate([arrived_a[:, :, 6 * t :], arrived_b[:, :, 2 * t :]], axis=2)
-    lowered_both = lowered_ap[:, :, t:]
+    lowered_both = jnp.concatenate([lowered_ap[:, :, t:], lowered_s1p], axis=2)
     grads_both = jnp.concatenate([first_grads, grads], axis=2)
     total_first_up = jnp.einsum(
         "pqt,rpgt->gpqr", stash_both, gspread_both, preferred_element_type=jnp.float32

time: 153 us -> 158 us (1.033)
  blocking collectives: 20.5 us -> 0 us
  waiting for transfers between devices: 59 us -> 78.1 us
  starting transfers between devices: 19.6 us -> 23.4 us
  matrix products: 9.64 us -> 6.8 us
  Pallas kernels: 13.2 us -> 16 us
  local copies, waits for them, and re-layouts: 29.3 us -> 31.3 us
    all_to_all x1 -> x0, blocking collectives: 20.5 us -> none  [to_blocks(): lax.all_to_all(pieces, 'blk', split_axis=1, concat_axis=0, tiled=True)]
    all_to_all x1 -> x2, waiting for transfers between devices: 28.1 us -> 43.4 us  [to_blocks(): lax.all_to_all(pieces, 'blk', split_axis=1, concat_axis=0, tiled=True)]
    pallas_call x0 -> x1, Pallas kernels: none -> 4.71 us  [forward_only(): pl.pallas_call(functools.partial(_forward_kernel, width, gate_at, up_at),...]
    all_to_all x2, waiting for transfers between devices: 27.8 us -> 31.6 us  [to_features(): lax.all_to_all(grouped, 'blk', split_axis=0, concat_axis=0, tiled=True)]
    all_to_all x1 -> x2, starting transfers between devices: 7.04 us -> 10.7 us  [to_blocks(): lax.all_to_all(pieces, 'blk', split_axis=1, concat_axis=0, tiled=True)]
    pallas_call x2, Pallas kernels: 13.2 us -> 11.2 us  [middle(): pl.pallas_call(functools.partial(_middle_kernel, fwd, bwd, bwd_at, keep_a...]
    unnamed x32 -> x44, local copies, waits for them, and re-layouts: 2.57 us -> 4.43 us
  transfers between devices with their start and end apart: 5 -> 6, of which waited for: 4 -> 5; matrix products, arithmetic and copies ran while one was open for 13% -> 10% of each run, Pallas kernels for 0% -> 3%
where the time goes in v9:
time: 158 us; the launch traced here: 157 us
  waiting for transfers between devices  78.1 us (49%)
  local copies, waits for them, and re-layouts  31.3 us (20%)
  starting transfers between devices  23.4 us (15%)
  Pallas kernels  16 us (10%)
  matrix products  6.8 us (4%)
    all_to_all x2, waiting for transfers between devices, to_blocks(): lax.all_to_all(pieces, 'blk', split_axis=1, concat_axis=0, tiled=True)  43.4 us
    all_to_all x2, waiting for transfers between devices, to_features(): lax.all_to_all(grouped, 'blk', split_axis=0, concat_axis=0, tiled=True)  31.6 us
    pallas_call x2, Pallas kernels, middle(): pl.pallas_call(functools.partial(_middle_kernel, fwd, bwd, bwd_at, keep_a...  11.2 us
    all_to_all x2, starting transfers between devices, to_blocks(): lax.all_to_all(pieces, 'blk', split_axis=1, concat_axis=0, tiled=True)  10.7 us
    all_to_all x2, starting transfers between devices, to_features(): lax.all_to_all(grouped, 'blk', split_axis=0, concat_axis=0, tiled=True)  8.44 us
    pallas_call x1, Pallas kernels, forward_only(): pl.pallas_call(functools.partial(_forward_kernel, width, gate_at, up_at),...  4.71 us
    unnamed x44, local copies, waits for them, and re-layouts  4.43 us
    ppermute x2, starting transfers between devices, from_behind(): return lax.ppermute(value, axis, pairs)  4.32 us
  transfers between devices with their start and end apart: 6, of which 5 were waited for; matrix products, arithmetic and copies ran while one was open for 10% of the time, Pallas kernels for 3%

profile of v9, /device:TPU:224, one launch (start us, length us, event | category | flops | bytes accessed | tf_op | source)
XLA Modules:
  0.0 157.0 jit_solution(4129502886274846415)
XLA Ops:
  1.6 1.4 reshape_squeeze.27
  3.0 1.6 reshape_squeeze.28
  6.7 2.1 %copy.65 = bf16[8,160,896]{2,0,1:T(8,128)(2,1)} copy(bf16[8,160,896]{2,1,0:T(8,128)(2,1)S(1)} %pad_maximum_fusion) | data formatting | bytes 4587520 | tf_op jit(solution)/shard_map/concatenate | solution.py:216
  8.8 7.0 %all-to-all-start = ((bf16[8,160,896]{2,0,1:T(8,128)(2,1)}), bf16[8,160,896]{2,0,1:T(8,128)(2,1)S(1)}, u32[]{:S(2)}, u32[]{:S(2)}) async-start(bf16[8,160,896]{2,0,1:T(8,128)(2,1)} %copy.65), calls=%async_computation | async-start | bytes 4587520 | tf_op jit(solution)/shard_map/all_to_all | solution.py:25
  15.9 2.3 %reshape_squeeze.30 = bf16[2,10,128,128]{3,2,0,1:T(8,128)(2,1)S(1)} reshape(bf16[1,2,10,16384]{3,1,2,0:T(2,128)(2,1)} %param.15) | data formatting | bytes 1310720 | tf_op jit(solution)/shard_map/reshape;squeeze | solution.py:201
  22.3 28.1 %all-to-all-done = bf16[8,160,896]{2,0,1:T(8,128)(2,1)S(1)} async-done(((bf16[8,160,896]{2,0,1:T(8,128)(2,1)}), bf16[8,160,896]{2,0,1:T(8,128)(2,1)S(1)}, u32[]{:S(2)}, u32[]{:S(2)}) %all-to-all-start) | async-done | bytes 2293792 | tf_op jit(solution)/shard_map/all_to_all | solution.py:25
  50.4 1.7 %copy.132 = bf16[16,8,10,896]{3,1,0,2:T(8,128)(2,1)} copy(bf16[16,8,10,896]{3,1,2,0:T(8,128)(2,1)S(1)} %bitcast.118) | data formatting | bytes 4587520 | tf_op jit(solution)/shard_map/all_to_all | solution.py:25
  52.1 5.8 %shard_map.136 = (bf16[16,10,8,512]{3,2,1,0:T(8,128)(2,1)}, bf16[2,10,128,128]{3,2,1,0:T(8,128)(2,1)}, bf16[10,128,256]{2,1,0:T(8,128)(2,1)}) custom-call(bf16[10,128,896]{2,1,0:T(8,128)(2,1)} %bitcast.111, bf16[2,10,128,128]{3,2,1,0:T(8,128)(2,1)} %copy.69.refs_1_, bf16[2,10,128,128]{3,2,1,0:T(8,128)(2,1)} %bitcast.115, bf16[10,128,128]{2,1,0:T(8,128)(2,1)} %copy-done.1, ...), custom_call_target="tpu_custom_call" | custom-call | flops 377487360 | bytes 6881280 | tf_op jit(solution)/shard_map/pallas_call | solution.py:161
  57.9 3.7 %all-to-all-start.1 = ((bf16[16,10,8,512]{3,2,1,0:T(8,128)(2,1)}), bf16[16,10,8,512]{3,2,1,0:T(8,128)(2,1)S(1)}, u32[]{:S(2)}, u32[]{:S(2)}) async-start(bf16[16,10,8,512]{3,2,1,0:T(8,128)(2,1)} %get-tuple-element.14), calls=%async_computation.1 | async-start | bytes 2621440 | tf_op jit(solution)/shard_map/all_to_all | solution.py:30
  61.6 19.6 %all-to-all-done.1 = bf16[16,10,8,512]{3,2,1,0:T(8,128)(2,1)S(1)} async-done(((bf16[16,10,8,512]{3,2,1,0:T(8,128)(2,1)}), bf16[16,10,8,512]{3,2,1,0:T(8,128)(2,1)S(1)}, u32[]{:S(2)}, u32[]{:S(2)}) %all-to-all-start.1) | async-done | bytes 1310752 | tf_op jit(solution)/shard_map/all_to_all | solution.py:30
  82.6 1.9 %collective-permute-start.1 = (bf16[8,40,128]{2,1,0:T(8,128)(2,1)S(1)}, bf16[8,40,128]{2,1,0:T(8,128)(2,1)S(1)}, u32[]{:S(2)}, u32[]{:S(2)}) collective-permute-start(bf16[8,40,128]{2,1,0:T(8,128)(2,1)S(1)} %fusion.26), channel_id=1, source_target_pairs={{16,0},{32,16},{48,32},{64,48},{80,64},{96,80},{112,96},{128,112},... | collective-permute-start | bytes 245768 | tf_op jit(solution)/shard_map/ppermute | solution.py:21
  84.8 2.4 %collective-permute-start = (bf16[8,40,128]{2,1,0:T(8,128)(2,1)S(1)}, bf16[8,40,128]{2,1,0:T(8,128)(2,1)S(1)}, u32[]{:S(2)}, u32[]{:S(2)}) collective-permute-start(bf16[8,40,128]{2,1,0:T(8,128)(2,1)S(1)} %fusion.27), channel_id=1, source_target_pairs={{0,16},{16,32},{32,48},{48,64},{64,80},{80,96},{96,112},{112,128},... | collective-permute-start | bytes 245768 | tf_op jit(solution)/shard_map/ppermute | solution.py:21
  87.5 3.1 %collective-permute-done = bf16[8,40,128]{2,1,0:T(8,128)(2,1)S(1)} collective-permute-done((bf16[8,40,128]{2,1,0:T(8,128)(2,1)S(1)}, bf16[8,40,128]{2,1,0:T(8,128)(2,1)S(1)}, u32[]{:S(2)}, u32[]{:S(2)}) %collective-permute-start) | collective-permute-done | bytes 81952 | tf_op jit(solution)/shard_map/ppermute | solution.py:21
  91.2 1.3 copy.77
  92.5 3.6 %all-to-all-start.2 = ((bf16[8,160,384]{2,0,1:T(8,128)(2,1)}), bf16[8,160,384]{2,0,1:T(8,128)(2,1)S(1)}, u32[]{:S(2)}, u32[]{:S(2)}) async-start(bf16[8,160,384]{2,0,1:T(8,128)(2,1)} %copy.77), calls=%async_computation.2 | async-start | bytes 1966080 | tf_op jit(solution)/shard_map/all_to_all | solution.py:25
  96.1 4.7 %shard_map.137 = (bf16[16,10,8,128]{3,2,1,0:T(8,128)(2,1)}, bf16[10,128,128]{2,1,0:T(8,128)(2,1)}, f32[2,10,128,128]{3,2,1,0:T(8,128)}) custom-call(bf16[10,128,896]{2,1,0:T(8,128)(2,1)} %bitcast.112, bf16[2,10,128,128]{3,2,1,0:T(8,128)(2,1)} %bitcast.116, bf16[10,128,128]{2,1,0:T(8,128)(2,1)} %bitcast.123), custom_call_target="tpu_custom_call" | custom-call | flops 125829120 | bytes 5570560 | tf_op jit(solution)/shard_map/pallas_call | solution.py:81
  100.9 15.3 %all-to-all-done.2 = bf16[8,160,384]{2,0,1:T(8,128)(2,1)S(1)} async-done(((bf16[8,160,384]{2,0,1:T(8,128)(2,1)}), bf16[8,160,384]{2,0,1:T(8,128)(2,1)S(1)}, u32[]{:S(2)}, u32[]{:S(2)}) %all-to-all-start.2) | async-done | bytes 983072 | tf_op jit(solution)/shard_map/all_to_all | solution.py:25
  117.2 5.5 %shard_map.138 = (bf16[16,10,8,512]{3,2,1,0:T(8,128)(2,1)}, bf16[2,10,128,128]{3,2,1,0:T(8,128)(2,1)}) custom-call(bf16[10,128,384]{2,1,0:T(8,128)(2,1)} %bitcast.120, bf16[2,10,128,128]{3,2,1,0:T(8,128)(2,1)} %copy.69.refs_1_, bf16[2,10,128,128]{3,2,1,0:T(8,128)(2,1)} %bitcast.117, bf16[10,128,128]{2,1,0:T(8,128)(2,1)} %copy-done.1, ...), custom_call_target="tpu_custom_call" | custom-call | flops 251658240 | bytes 6553600 | tf_op jit(solution)/shard_map/pallas_call | solution.py:161
  122.7 4.7 %all-to-all-start.3 = ((bf16[16,10,8,512]{3,2,1,0:T(8,128)(2,1)}), bf16[16,10,8,512]{3,2,1,0:T(8,128)(2,1)}, u32[]{:S(2)}, u32[]{:S(2)}) async-start(bf16[16,10,8,512]{3,2,1,0:T(8,128)(2,1)} %get-tuple-element.17), calls=%async_computation.3 | async-start | bytes 2621440 | tf_op jit(solution)/shard_map/all_to_all | solution.py:30
  128.2 1.7 %slice.50 = bf16[10,128,128]{2,1,0:T(8,128)(2,1)} slice(bf16[10,128,256]{2,1,0:T(8,128)(2,1)} %get-tuple-element.20), slice={[0:10], [0:128], [128:256]} | slice | bytes 655360 | tf_op jit(solution)/shard_map/slice | solution.py:256
  131.3 1.9 %slice.62 = bf16[10,128,128]{2,1,0:T(8,128)(2,1)} slice(bf16[10,128,384]{2,1,0:T(8,128)(2,1)} %bitcast.121), slice={[0:10], [0:128], [256:384]} | slice | bytes 655360 | tf_op jit(solution)/shard_map/slice | solution.py:257
  134.7 1.4 fusion.15
  137.1 12.0 %all-to-all-done.3 = bf16[16,10,8,512]{3,2,1,0:T(8,128)(2,1)} async-done(((bf16[16,10,8,512]{3,2,1,0:T(8,128)(2,1)}), bf16[16,10,8,512]{3,2,1,0:T(8,128)(2,1)}, u32[]{:S(2)}, u32[]{:S(2)}) %all-to-all-start.3) | async-done | bytes 1310752 | tf_op jit(solution)/shard_map/all_to_all | solution.py:30
  149.2 1.2 slice_bitcast_fusion.2
  (80 shorter events, 21.8 us)
Async XLA Ops:
  0.6 4.0 %copy-start.6 = (bf16[1,320,128]{2,1,0:T(8,128)(2,1)S(1)}, bf16[1,320,128]{2,1,0:T(8,128)(2,1)}, u32[]{:S(2)}) copy-start(bf16[1,320,128]{2,1,0:T(8,128)(2,1)} %param.9) | copy-start | bytes 245764
  1.6 3.7 %copy-start.8 = (bf16[1,1,320,128]{3,2,1,0:T(8,128)(2,1)}, bf16[1,1,320,128]{3,2,1,0:T(8,128)(2,1)S(1)}, u32[]{:S(2)}) copy-start(bf16[1,1,320,128]{3,2,1,0:T(8,128)(2,1)S(1)} %get-tuple-element.47) | copy-start | bytes 245764
  3.0 2.3 %copy-start.2 = (bf16[2,8,40,160]{3,2,1,0:T(8,128)(2,1)}, bf16[2,8,40,160]{3,2,1,0:T(8,128)(2,1)S(1)}, u32[]{:S(2)}) copy-start(bf16[2,8,40,160]{3,2,1,0:T(8,128)(2,1)S(1)} %reshape_squeeze.27) | copy-start | bytes 614404
  8.8 41.6 %all-to-all-start = ((bf16[8,160,896]{2,0,1:T(8,128)(2,1)}), bf16[8,160,896]{2,0,1:T(8,128)(2,1)S(1)}, u32[]{:S(2)}, u32[]{:S(2)}) async-start(bf16[8,160,896]{2,0,1:T(8,128)(2,1)} %copy.65), calls=%async_computation | async-start | bytes 4587520 | tf_op jit(solution)/shard_map/all_to_all | solution.py:25
  21.3 30.8 %copy-start.1 = (bf16[10,128,128]{2,1,0:T(8,128)(2,1)}, bf16[10,128,128]{2,1,0:T(8,128)(2,1)S(1)}, u32[]{:S(2)}) copy-start(bf16[10,128,128]{2,1,0:T(8,128)(2,1)S(1)} %slice.65.refs_3_) | copy-start | bytes 983044
  57.9 23.3 %all-to-all-start.1 = ((bf16[16,10,8,512]{3,2,1,0:T(8,128)(2,1)}), bf16[16,10,8,512]{3,2,1,0:T(8,128)(2,1)S(1)}, u32[]{:S(2)}, u32[]{:S(2)}) async-start(bf16[16,10,8,512]{3,2,1,0:T(8,128)(2,1)} %get-tuple-element.14), calls=%async_computation.1 | async-start | bytes 2621440 | tf_op jit(solution)/shard_map/all_to_all | solution.py:30
  81.2 1.0 copy-start.16
  81.4 1.2 copy-start.4
  82.2 5.0 %copy-start.14 = (bf16[320,128]{1,0:T(8,128)(2,1)S(1)}, bf16[320,128]{1,0:T(8,128)(2,1)}, u32[]{:S(2)}) copy-start(bf16[320,128]{1,0:T(8,128)(2,1)} %param.13) | copy-start | bytes 245764
  82.2 8.3 %copy-start.7 = (bf16[320,128]{1,0:T(8,128)(2,1)S(1)}, bf16[320,128]{1,0:T(8,128)(2,1)}, u32[]{:S(2)}) copy-start(bf16[320,128]{1,0:T(8,128)(2,1)} %param.10) | copy-start | bytes 245764
  82.6 4.6 %collective-permute-start.1 = (bf16[8,40,128]{2,1,0:T(8,128)(2,1)S(1)}, bf16[8,40,128]{2,1,0:T(8,128)(2,1)S(1)}, u32[]{:S(2)}, u32[]{:S(2)}) collective-permute-start(bf16[8,40,128]{2,1,0:T(8,128)(2,1)S(1)} %fusion.26), channel_id=1, source_target_pairs={{16,0},{32,16},{48,32},{64,48},{80,64},{96,80},{112,96},{128,112},... | collective-permute-start | bytes 245768 | tf_op jit(solution)/shard_map/ppermute | solution.py:21
  84.8 5.8 %collective-permute-start = (bf16[8,40,128]{2,1,0:T(8,128)(2,1)S(1)}, bf16[8,40,128]{2,1,0:T(8,128)(2,1)S(1)}, u32[]{:S(2)}, u32[]{:S(2)}) collective-permute-start(bf16[8,40,128]{2,1,0:T(8,128)(2,1)S(1)} %fusion.27), channel_id=1, source_target_pairs={{0,16},{16,32},{32,48},{48,64},{64,80},{80,96},{96,112},{112,128},... | collective-permute-start | bytes 245768 | tf_op jit(solution)/shard_map/ppermute | solution.py:21
  87.2 3.8 %copy-start.12 = (bf16[8,40,128]{2,1,0:T(8,128)(2,1)}, bf16[8,40,128]{2,1,0:T(8,128)(2,1)S(1)}, u32[]{:S(2)}) copy-start(bf16[8,40,128]{2,1,0:T(8,128)(2,1)S(1)} %broadcast_select_fusion) | copy-start | bytes 245764
  92.5 23.7 %all-to-all-start.2 = ((bf16[8,160,384]{2,0,1:T(8,128)(2,1)}), bf16[8,160,384]{2,0,1:T(8,128)(2,1)S(1)}, u32[]{:S(2)}, u32[]{:S(2)}) async-start(bf16[8,160,384]{2,0,1:T(8,128)(2,1)} %copy.77), calls=%async_computation.2 | async-start | bytes 1966080 | tf_op jit(solution)/shard_map/all_to_all | solution.py:25
  122.7 4.7 %copy-start = (bf16[16,8,10,896]{3,1,0,2:T(8,128)(2,1)S(1)}, bf16[16,8,10,896]{3,1,0,2:T(8,128)(2,1)}, u32[]{:S(2)}) copy-start(bf16[16,8,10,896]{3,1,0,2:T(8,128)(2,1)} %copy.132) | copy-start | bytes 6881284
  122.7 26.5 %all-to-all-start.3 = ((bf16[16,10,8,512]{3,2,1,0:T(8,128)(2,1)}), bf16[16,10,8,512]{3,2,1,0:T(8,128)(2,1)}, u32[]{:S(2)}, u32[]{:S(2)}) async-start(bf16[16,10,8,512]{3,2,1,0:T(8,128)(2,1)} %get-tuple-element.17), calls=%async_computation.3 | async-start | bytes 2621440 | tf_op jit(solution)/shard_map/all_to_all | solution.py:30
  130.0 1.1 copy-start.5
  131.0 2.1 %copy-start.18 = (bf16[2,10,128,128]{3,2,1,0:T(8,128)(2,1)S(1)}, bf16[2,10,128,128]{3,2,1,0:T(8,128)(2,1)}, u32[]{:S(2)}) copy-start(bf16[2,10,128,128]{3,2,1,0:T(8,128)(2,1)} %get-tuple-element.18) | copy-start | bytes 1966084
  131.0 2.1 %copy-start.19 = (bf16[2,10,128,128]{3,2,1,0:T(8,128)(2,1)S(1)}, bf16[2,10,128,128]{3,2,1,0:T(8,128)(2,1)}, u32[]{:S(2)}) copy-start(bf16[2,10,128,128]{3,2,1,0:T(8,128)(2,1)} %get-tuple-element.19) | copy-start | bytes 1966084
  133.7 1.1 copy-start.10
  133.7 1.1 copy-start.11
  149.2 2.4 %copy-start.13 = (bf16[8,40,128]{2,1,0:T(8,128)(2,1)S(1)}, bf16[8,40,128]{2,1,0:T(8,128)(2,1)}, u32[]{:S(2)}) copy-start(bf16[8,40,128]{2,1,0:T(8,128)(2,1)} %copy-done.12) | copy-start | bytes 245764
  151.6 1.2 copy-start.9
  153.2 1.3 copy-start.17
  (2 other events, 1.9 us)

commit v10 on v7

--- a/solution.py
+++ b/solution.py
@@ -69,7 +69,7 @@
         hidden = (gate / (1.0 + jnp.exp(-gate)) * upper).astype(jnp.bfloat16)
         put(payload, r, 0, jnp.dot(down_t[r], hidden, preferred_element_type=jnp.float32))
         if hidden_out is not None:
-            hidden_out[r] = hidden
+            hidden_out[r] = hidden[:, bwd_at:]
         if keep_out is not None:
             keep_out[0, r] = gate[:, keep_at : keep_at + bwd]
             keep_out[1, r] = upper[:, keep_at : keep_at + bwd]
@@ -98,7 +98,7 @@
         jax.ShapeDtypeStruct((2, rb, o, bwd), jnp.bfloat16),
     ]
     if mixed_in is None:
-        outs.append(jax.ShapeDtypeStruct((rb, o, fwd), jnp.bfloat16))
+        outs.append(jax.ShapeDtypeStruct((rb, o, fwd - bwd_at), jnp.bfloat16))
     if keep_at is not None:
         outs.append(jax.ShapeDtypeStruct((2, rb, o, bwd), jnp.float32))
     ins = [arrived, up, up_t, down, down_t] + ([mixed_in] if mixed_in is not None else [])
@@ -194,7 +194,7 @@
         [arrived_a[:, :, t : 3 * t], arrived_a[:, :, 4 * t : 6 * t]]
     )
     gmix_both = jnp.concatenate([gmix_1, gmix_2], axis=3)
-    hidden_both = hidden_a[:, :, t:]
+    hidden_both = hidden_a
     glow_both = jnp.concatenate([arrived_a[:, :, 6 * t :], arrived_b[:, :, 2 * t :]], axis=2)
     lowered_both = lowered_ap[:, :, t:]
     grads_both = jnp.concatenate([first_grads, grads], axis=2)

time: 153 us -> 153 us (level)
  no operation moved by 1% of the time
where the time goes in v10:
time: 153 us; the launch traced here: 152 us
  waiting for transfers between devices  59 us (39%)
  local copies, waits for them, and re-layouts  29.3 us (19%)
  blocking collectives  20.5 us (13%)
  starting transfers between devices  19.6 us (13%)
  Pallas kernels  13.1 us (9%)
  matrix products  9.65 us (6%)
    all_to_all x1, waiting for transfers between devices, to_blocks(): lax.all_to_all(pieces, 'blk', split_axis=1, concat_axis=0, tiled=True)  28.2 us
    all_to_all x2, waiting for transfers between devices, to_features(): lax.all_to_all(grouped, 'blk', split_axis=0, concat_axis=0, tiled=True)  27.8 us
    all_to_all x1, blocking collectives, to_blocks(): lax.all_to_all(pieces, 'blk', split_axis=1, concat_axis=0, tiled=True)  20.5 us
    pallas_call x2, Pallas kernels, middle(): pl.pallas_call(functools.partial(_middle_kernel, fwd, bwd, bwd_at, keep_a...  13.1 us
    all_to_all x2, starting transfers between devices, to_features(): lax.all_to_all(grouped, 'blk', split_axis=0, concat_axis=0, tiled=True)  8.22 us
    all_to_all x1, starting transfers between devices, to_blocks(): lax.all_to_all(pieces, 'blk', split_axis=1, concat_axis=0, tiled=True)  7.04 us
    ppermute x2, starting transfers between devices, from_behind(): return lax.ppermute(value, axis, pairs)  4.33 us
    another operation x3, local copies, waits for them, and re-layouts, shards(): up_second = second_up[0].reshape(2, rb, FIRST_BLOCKS, BLOCK)  4.28 us
  transfers between devices with their start and end apart: 5, of which 4 were waited for; matrix products, arithmetic and copies ran while one was open for 13% of the time, Pallas kernels for 0%

profile of v10, /device:TPU:224, one launch (start us, length us, event | category | flops | bytes accessed | tf_op | source)
XLA Modules:
  0.0 152.4 jit_solution(3884411342169049976)
XLA Ops:
  1.6 1.4 reshape_squeeze.27
  3.0 1.6 %reshape_squeeze.28 = bf16[8,160,40]{2,1,0:T(8,128)(2,1)S(1)} reshape(bf16[1,8,6400]{2,1,0:T(8,128)(2,1)} %param.17) | data formatting | bytes 204800 | tf_op jit(solution)/shard_map/reshape;squeeze | solution.py:150
  4.5 1.6 %convert_bitcast_fusion = bf16[8,2,20,8,384]{4,3,2,1,0:T(8,128)(2,1)S(1)} fusion(bf16[8,40,128]{2,1,0:T(8,128)(2,1)S(1)} %bitcast.135, bf16[8,40,128]{2,1,0:T(8,128)(2,1)S(1)} %bitcast.133, bf16[8,40,128]{2,1,0:T(8,128)(2,1)} %bitcast.129, bf16[2,8,40,160]{3,2,1,0:T(8,128)(2,1)S(1)} %reshape_squeeze.27), kind=kOutput, calls=%fused_computation.2 | convolution fusion | flops 80363520 | bytes 2416640 | tf_op jit(solution)/shard_map/pqt,gpqr->prgt/dot_general | solution.py:35
  7.4 2.2 %copy.63 = bf16[8,160,896]{2,0,1:T(8,128)(2,1)} copy(bf16[8,160,896]{2,1,0:T(8,128)(2,1)S(1)} %pad_maximum_fusion) | data formatting | bytes 4587520 | tf_op jit(solution)/shard_map/concatenate | solution.py:163
  9.6 7.0 %all-to-all-start = ((bf16[8,160,896]{2,0,1:T(8,128)(2,1)}), bf16[8,160,896]{2,0,1:T(8,128)(2,1)S(1)}, u32[]{:S(2)}, u32[]{:S(2)}) async-start(bf16[8,160,896]{2,0,1:T(8,128)(2,1)} %copy.63), calls=%async_computation | async-start | bytes 4587520 | tf_op jit(solution)/shard_map/all_to_all | solution.py:25
  16.6 2.3 %reshape_squeeze.30 = bf16[2,10,128,128]{3,2,0,1:T(8,128)(2,1)S(1)} reshape(bf16[1,2,10,16384]{3,1,2,0:T(2,128)(2,1)} %param.15) | data formatting | bytes 1310720 | tf_op jit(solution)/shard_map/reshape;squeeze | solution.py:148
  23.0 28.2 %all-to-all-done = bf16[8,160,896]{2,0,1:T(8,128)(2,1)S(1)} async-done(((bf16[8,160,896]{2,0,1:T(8,128)(2,1)}), bf16[8,160,896]{2,0,1:T(8,128)(2,1)S(1)}, u32[]{:S(2)}, u32[]{:S(2)}) %all-to-all-start) | async-done | bytes 2293792 | tf_op jit(solution)/shard_map/all_to_all | solution.py:25
  51.2 1.7 %copy.130 = bf16[16,8,10,896]{3,1,0,2:T(8,128)(2,1)} copy(bf16[16,8,10,896]{3,1,2,0:T(8,128)(2,1)S(1)} %bitcast.115) | data formatting | bytes 4587520 | tf_op jit(solution)/shard_map/all_to_all | solution.py:25
  52.9 7.7 %shard_map.136 = (bf16[16,10,8,640]{3,2,1,0:T(8,128)(2,1)}, bf16[2,10,128,128]{3,2,1,0:T(8,128)(2,1)}, bf16[10,128,256]{2,1,0:T(8,128)(2,1)}, f32[2,10,128,128]{3,2,1,0:T(8,128)}) custom-call(bf16[10,128,896]{2,1,0:T(8,128)(2,1)} %bitcast.112, bf16[2,10,128,128]{3,2,1,0:T(8,128)(2,1)} %copy.67.refs_1_, bf16[2,10,128,128]{3,2,1,0:T(8,128)(2,1)} %bitcast.119, ...), custom_call_target="tpu_custom_call" | custom-call | flops 503316480 | bytes 8519680 | tf_op jit(solution)/shard_map/pallas_call | solution.py:110
  60.6 3.7 %all-to-all-start.1 = ((bf16[16,10,8,640]{3,2,1,0:T(8,128)(2,1)}), bf16[16,10,8,640]{3,2,1,0:T(8,128)(2,1)S(1)}, u32[]{:S(2)}, u32[]{:S(2)}) async-start(bf16[16,10,8,640]{3,2,1,0:T(8,128)(2,1)} %get-tuple-element.12), calls=%async_computation.1 | async-start | bytes 3276800 | tf_op jit(solution)/shard_map/all_to_all | solution.py:30
  64.3 23.6 %all-to-all-done.1 = bf16[16,10,8,640]{3,2,1,0:T(8,128)(2,1)S(1)} async-done(((bf16[16,10,8,640]{3,2,1,0:T(8,128)(2,1)}), bf16[16,10,8,640]{3,2,1,0:T(8,128)(2,1)S(1)}, u32[]{:S(2)}, u32[]{:S(2)}) %all-to-all-start.1) | async-done | bytes 1638432 | tf_op jit(solution)/shard_map/all_to_all | solution.py:30
  89.3 1.9 %collective-permute-start.1 = (bf16[8,40,128]{2,1,0:T(8,128)(2,1)S(1)}, bf16[8,40,128]{2,1,0:T(8,128)(2,1)S(1)}, u32[]{:S(2)}, u32[]{:S(2)}) collective-permute-start(bf16[8,40,128]{2,1,0:T(8,128)(2,1)S(1)} %fusion.26), channel_id=1, source_target_pairs={{16,0},{32,16},{48,32},{64,48},{80,64},{96,80},{112,96},{128,112},... | collective-permute-start | bytes 245768 | tf_op jit(solution)/shard_map/ppermute | solution.py:21
  91.5 2.4 %collective-permute-start = (bf16[8,40,128]{2,1,0:T(8,128)(2,1)S(1)}, bf16[8,40,128]{2,1,0:T(8,128)(2,1)S(1)}, u32[]{:S(2)}, u32[]{:S(2)}) collective-permute-start(bf16[8,40,128]{2,1,0:T(8,128)(2,1)S(1)} %fusion.27), channel_id=1, source_target_pairs={{0,16},{16,32},{32,48},{48,64},{64,80},{80,96},{96,112},{112,128},... | collective-permute-start | bytes 245768 | tf_op jit(solution)/shard_map/ppermute | solution.py:21
  94.2 3.1 %collective-permute-done = bf16[8,40,128]{2,1,0:T(8,128)(2,1)S(1)} collective-permute-done((bf16[8,40,128]{2,1,0:T(8,128)(2,1)S(1)}, bf16[8,40,128]{2,1,0:T(8,128)(2,1)S(1)}, u32[]{:S(2)}, u32[]{:S(2)}) %collective-permute-start) | collective-permute-done | bytes 81952 | tf_op jit(solution)/shard_map/ppermute | solution.py:21
  98.3 20.5 %all_to_all.46 = bf16[8,160,384]{2,0,1:T(8,128)(2,1)S(1)} all-to-all(bf16[8,160,384]{2,0,1:T(8,128)(2,1)S(1)} %copy.75), channel_id=1, replica_groups=mesh['section'=32,'blk'=16] {'blk'}, dimensions={1} | all-to-all | bytes 1966080 | tf_op jit(solution)/shard_map/all_to_all | solution.py:25
  118.7 1.2 copy.131
  119.9 5.4 %shard_map.137 = (bf16[16,10,8,384]{3,2,1,0:T(8,128)(2,1)}, bf16[2,10,128,128]{3,2,1,0:T(8,128)(2,1)}) custom-call(bf16[10,128,384]{2,1,0:T(8,128)(2,1)} %bitcast.121, bf16[2,10,128,128]{3,2,1,0:T(8,128)(2,1)} %copy.67.refs_1_, bf16[2,10,128,128]{3,2,1,0:T(8,128)(2,1)} %bitcast.120, bf16[10,128,128]{2,1,0:T(8,128)(2,1)} %copy-done.1, ...), custom_call_target="tpu_custom_call" | custom-call | flops 251658240 | bytes 5898240 | tf_op jit(solution)/shard_map/pallas_call | solution.py:110
  125.3 4.5 %all-to-all-start.3 = ((bf16[16,10,8,384]{3,2,1,0:T(8,128)(2,1)}), bf16[16,10,8,384]{3,2,1,0:T(8,128)(2,1)}, u32[]{:S(2)}, u32[]{:S(2)}) async-start(bf16[16,10,8,384]{3,2,1,0:T(8,128)(2,1)} %get-tuple-element.14), calls=%async_computation.3 | async-start | bytes 1966080 | tf_op jit(solution)/shard_map/all_to_all | solution.py:30
  130.6 1.2 slice_bitcast_fusion.1
  135.2 1.7 %slice.54 = bf16[10,128,128]{2,1,0:T(8,128)(2,1)} slice(bf16[10,128,384]{2,1,0:T(8,128)(2,1)} %bitcast.122), slice={[0:10], [0:128], [256:384]} | slice | bytes 655360 | tf_op jit(solution)/shard_map/slice | solution.py:198
  136.9 1.8 %fusion = bf16[2,10,128,128]{3,2,1,0:T(8,128)(2,1)S(1)} fusion(bf16[1,10,128,256]{3,2,1,0:T(8,128)(2,1)S(1)} %copy-done.8, bf16[1,10,128,256]{3,2,1,0:T(8,128)(2,1)S(1)} %copy-done.7, bf16[2,10,128,128]{3,2,1,0:T(8,128)(2,1)} %get-tuple-element.16, bf16[2,10,128,128]{3,2,1,0:T(8,128)(2,1)} %get-tuple-element.15), kind=kOutput, calls=%fused_computation.4 | convolution fusion | flops 171704320 | bytes 3276800 | tf_op jit(solution)/shard_map/grpt,grot->grpo/dot_general | solution.py:204
  139.8 1.4 fusion.15
  142.2 4.2 %all-to-all-done.3 = bf16[16,10,8,384]{3,2,1,0:T(8,128)(2,1)} async-done(((bf16[16,10,8,384]{3,2,1,0:T(8,128)(2,1)}), bf16[16,10,8,384]{3,2,1,0:T(8,128)(2,1)}, u32[]{:S(2)}, u32[]{:S(2)}) %all-to-all-start.3) | async-done | bytes 983072 | tf_op jit(solution)/shard_map/all_to_all | solution.py:30
  147.4 1.2 slice_bitcast_fusion.2
  (65 shorter events, 20.0 us)
Async XLA Ops:
  2.9 3.4 %copy-start.2 = (bf16[2,8,40,160]{3,2,1,0:T(8,128)(2,1)}, bf16[2,8,40,160]{3,2,1,0:T(8,128)(2,1)S(1)}, u32[]{:S(2)}) copy-start(bf16[2,8,40,160]{3,2,1,0:T(8,128)(2,1)S(1)} %reshape_squeeze.27) | copy-start | bytes 614404
  6.1 0.9 copy-start.14
  9.6 41.6 %all-to-all-start = ((bf16[8,160,896]{2,0,1:T(8,128)(2,1)}), bf16[8,160,896]{2,0,1:T(8,128)(2,1)S(1)}, u32[]{:S(2)}, u32[]{:S(2)}) async-start(bf16[8,160,896]{2,0,1:T(8,128)(2,1)} %copy.63), calls=%async_computation | async-start | bytes 4587520 | tf_op jit(solution)/shard_map/all_to_all | solution.py:25
  22.1 30.8 %copy-start.1 = (bf16[10,128,128]{2,1,0:T(8,128)(2,1)}, bf16[10,128,128]{2,1,0:T(8,128)(2,1)S(1)}, u32[]{:S(2)}) copy-start(bf16[10,128,128]{2,1,0:T(8,128)(2,1)S(1)} %slice.56.refs_3_) | copy-start | bytes 983044
  60.6 27.3 %all-to-all-start.1 = ((bf16[16,10,8,640]{3,2,1,0:T(8,128)(2,1)}), bf16[16,10,8,640]{3,2,1,0:T(8,128)(2,1)S(1)}, u32[]{:S(2)}, u32[]{:S(2)}) async-start(bf16[16,10,8,640]{3,2,1,0:T(8,128)(2,1)} %get-tuple-element.12), calls=%async_computation.1 | async-start | bytes 3276800 | tf_op jit(solution)/shard_map/all_to_all | solution.py:30
  64.3 24.7 %copy-start.3 = (bf16[2,8,40,160]{3,2,1,0:T(8,128)(2,1)S(1)}, bf16[2,8,40,160]{3,2,1,0:T(8,128)(2,1)}, u32[]{:S(2)}) copy-start(bf16[2,8,40,160]{3,2,1,0:T(8,128)(2,1)} %copy-done.2) | copy-start | bytes 614404
  87.9 3.3 %copy-start.9 = (bf16[1,320,128]{2,1,0:T(8,128)(2,1)S(1)}, bf16[1,320,128]{2,1,0:T(8,128)(2,1)}, u32[]{:S(2)}) copy-start(bf16[1,320,128]{2,1,0:T(8,128)(2,1)} %param.9) | copy-start | bytes 245764
  87.9 6.0 %copy-start.13 = (bf16[320,128]{1,0:T(8,128)(2,1)S(1)}, bf16[320,128]{1,0:T(8,128)(2,1)}, u32[]{:S(2)}) copy-start(bf16[320,128]{1,0:T(8,128)(2,1)} %param.13) | copy-start | bytes 245764
  88.9 8.7 %copy-start.4 = (bf16[160,8,2,128]{3,1,2,0:T(8,128)(2,1)}, bf16[160,8,2,128]{3,1,2,0:T(8,128)(2,1)S(1)}, u32[]{:S(2)}) copy-start(bf16[160,8,2,128]{3,1,2,0:T(8,128)(2,1)S(1)} %get-tuple-element.39) | copy-start | bytes 1966084
  88.9 8.3 %copy-start.10 = (bf16[320,128]{1,0:T(8,128)(2,1)S(1)}, bf16[320,128]{1,0:T(8,128)(2,1)}, u32[]{:S(2)}) copy-start(bf16[320,128]{1,0:T(8,128)(2,1)} %param.10) | copy-start | bytes 245764
  89.3 4.6 %collective-permute-start.1 = (bf16[8,40,128]{2,1,0:T(8,128)(2,1)S(1)}, bf16[8,40,128]{2,1,0:T(8,128)(2,1)S(1)}, u32[]{:S(2)}, u32[]{:S(2)}) collective-permute-start(bf16[8,40,128]{2,1,0:T(8,128)(2,1)S(1)} %fusion.26), channel_id=1, source_target_pairs={{16,0},{32,16},{48,32},{64,48},{80,64},{96,80},{112,96},{128,112},... | collective-permute-start | bytes 245768 | tf_op jit(solution)/shard_map/ppermute | solution.py:21
  91.5 5.8 %collective-permute-start = (bf16[8,40,128]{2,1,0:T(8,128)(2,1)S(1)}, bf16[8,40,128]{2,1,0:T(8,128)(2,1)S(1)}, u32[]{:S(2)}, u32[]{:S(2)}) collective-permute-start(bf16[8,40,128]{2,1,0:T(8,128)(2,1)S(1)} %fusion.27), channel_id=1, source_target_pairs={{0,16},{16,32},{32,48},{48,64},{64,80},{80,96},{96,112},{112,128},... | collective-permute-start | bytes 245768 | tf_op jit(solution)/shard_map/ppermute | solution.py:21
  119.9 9.9 %copy-start = (bf16[16,8,10,896]{3,1,0,2:T(8,128)(2,1)S(1)}, bf16[16,8,10,896]{3,1,0,2:T(8,128)(2,1)}, u32[]{:S(2)}) copy-start(bf16[16,8,10,896]{3,1,0,2:T(8,128)(2,1)} %copy.130) | copy-start | bytes 6881284
  125.3 21.1 %all-to-all-start.3 = ((bf16[16,10,8,384]{3,2,1,0:T(8,128)(2,1)}), bf16[16,10,8,384]{3,2,1,0:T(8,128)(2,1)}, u32[]{:S(2)}, u32[]{:S(2)}) async-start(bf16[16,10,8,384]{3,2,1,0:T(8,128)(2,1)} %get-tuple-element.14), calls=%async_computation.3 | async-start | bytes 1966080 | tf_op jit(solution)/shard_map/all_to_all | solution.py:30
  129.8 2.0 %copy-start.5 = (bf16[160,8,2,128]{3,1,2,0:T(8,128)(2,1)S(1)}, bf16[160,8,2,128]{3,1,2,0:T(8,128)(2,1)}, u32[]{:S(2)}) copy-start(bf16[160,8,2,128]{3,1,2,0:T(8,128)(2,1)} %copy-done.4) | copy-start | bytes 1966084
  130.6 1.4 copy-start.6
  131.8 5.1 %copy-start.7 = (bf16[1,10,128,256]{3,2,1,0:T(8,128)(2,1)S(1)}, bf16[1,10,128,256]{3,2,1,0:T(8,128)(2,1)}, u32[]{:S(2)}) copy-start(bf16[1,10,128,256]{3,2,1,0:T(8,128)(2,1)} %get-tuple-element.36) | copy-start | bytes 1966084
  131.8 5.1 %copy-start.8 = (bf16[1,10,128,256]{3,2,1,0:T(8,128)(2,1)S(1)}, bf16[1,10,128,256]{3,2,1,0:T(8,128)(2,1)}, u32[]{:S(2)}) copy-start(bf16[1,10,128,256]{3,2,1,0:T(8,128)(2,1)} %get-tuple-element.37) | copy-start | bytes 1966084
  138.7 1.1 copy-start.11
  138.7 1.1 copy-start.12
